TPU v7x, 512 devices: a whole 4x8x8 slice. The times are simulated.
512 devices in a mesh: req: 64 (over x, z, core), tp: 8 (over y).
Axes of the slice: x: 4, y: 8, z: 8, core: 2. Of those that a mesh axis runs over, the one named last changes fastest.
Arguments:
- dec_q: bfloat16 [8192, 3072], P('req', 'tp'), may hold values from -12 to 12
- dec_kv: bfloat16 [8192, 2048], P('req', 'tp'), may hold values from -12 to 12
- dec_owner: int32 [8192], P('req'), may hold values from 0 to 63, as said below
- dec_table: int32 [16384, 2], P('req'), may hold values from 0 to 512, as said below
- pre_q: bfloat16 [16384, 3072], P('req', 'tp'), may hold values from -12 to 12
- pre_kv: bfloat16 [16384, 2048], P('req', 'tp'), may hold values from -12 to 12
- pre_meta: int32 [64, 3], P('req'), may hold values from 0 to 512, as said below
- pool: bfloat16 [32768, 2048], P('req', 'tp'), may hold values from -12 to 12
- wo: bfloat16 [3072, 3072], P('tp'), may hold values from -0.4375 to 0.4375
Outputs:
- dec_out: bfloat16 [8192, 3072], P(('req', 'tp'))
- pre_out: bfloat16 [16384, 3072], P(('req', 'tp'))
Inputs may be any that keep to these rules, and one draw needn't show every extreme that they name: `dec_owner`: among the decode tokens of one group at most 4 name the same owner; in every draw some group is named by exactly 4 tokens of every group. `dec_table`: row o * 256 + s * 4 + c describes the c-th decode token of group s (in row order) that names owner o: start and length of its cache in o's pool, length at least 1, start + length <= 512; rows with no such token hold 0 0. Some window has length 512. `pre_meta`: start + context length <= 512; span length from 64 to 256; some group has context length 512, some span length 256.
All inputs are finite; a program needn't handle non-finite values.
Results may differ from a plain program's by a relative error of at most 0.014.
Values may be sent and summed in bfloat16 or wider, within the bound.
No kernel may reach another device: no remote copies, remote signals or barrier semaphores. Data moves between devices by JAX's collectives and lax.ppermute only.
A program may use at most 64 MiB of HBM per device.

v0:
```python
import math

import jax
import jax.numpy as jnp
from jax import lax
from jax.sharding import PartitionSpec as P

HD = 128
QPK = 3


MASKED_SCORE = -1e30


def decode_block(q_block, kv_block, windows, pool_keys, pool_vals):
    score_scale = 1.0 / math.sqrt(HD)
    slot_rows = q_block.shape[0]
    places = lax.iota(jnp.int32, pool_keys.shape[0])
    begins = windows[:, 0:1]
    visible = (places[None, :] >= begins) & (places[None, :] < begins + windows[:, 1:2])
    visible = visible[:, None, None, :]
    pool_scores = (
        jnp.einsum("sghd,pgd->sghp", q_block, pool_keys, preferred_element_type=jnp.float32)
        * score_scale
    )
    pool_scores = jnp.where(visible, pool_scores, MASKED_SCORE)
    self_scores = (
        jnp.einsum(
            "sghd,sgd->sgh", q_block, kv_block[:, :, 0, :], preferred_element_type=jnp.float32
        )
        * score_scale
    )
    row_peak = jnp.maximum(jnp.max(pool_scores, axis=-1), self_scores)
    pool_exp = jnp.where(visible, jnp.exp(pool_scores - row_peak[..., None]), 0.0)
    self_exp = jnp.exp(self_scores - row_peak)
    row_total = jnp.sum(pool_exp, axis=-1) + self_exp
    pool_weight = (pool_exp / row_total[..., None]).astype(jnp.bfloat16)
    self_weight = (self_exp / row_total).astype(jnp.bfloat16)
    mixed_rows = jnp.einsum(
        "sghp,pgd->sghd", pool_weight, pool_vals, preferred_element_type=jnp.float32
    )
    mixed_rows = mixed_rows + self_weight.astype(jnp.float32)[..., None] * kv_block[
        :, :, None, 1, :
    ].astype(jnp.float32)
    return mixed_rows.astype(jnp.bfloat16).reshape(slot_rows, -1)


def prefill_attend(q_rows, kv_rows, meta_row, pool_keys, pool_vals, kv_heads):
    score_scale = 1.0 / math.sqrt(HD)
    span_rows = q_rows.shape[0]
    queries = q_rows.reshape(span_rows, kv_heads, QPK, HD)
    span_kv = kv_rows.reshape(span_rows, kv_heads, 2, HD)
    places = lax.iota(jnp.int32, pool_keys.shape[0])
    visible = (places >= meta_row[0]) & (places < meta_row[0] + meta_row[1])
    visible = visible[None, None, None, :]
    row_iota = lax.iota(jnp.int32, span_rows)
    causal = (row_iota[None, :] <= row_iota[:, None])[:, None, None, :]
    pool_scores = (
        jnp.einsum("jghd,pgd->jghp", queries, pool_keys, preferred_element_type=jnp.float32)
        * score_scale
    )
    pool_scores = jnp.where(visible, pool_scores, MASKED_SCORE)
    span_scores = (
        jnp.einsum(
            "jghd,igd->jghi", queries, span_kv[:, :, 0, :], preferred_element_type=jnp.float32
        )
        * score_scale
    )
    span_scores = jnp.where(causal, span_scores, MASKED_SCORE)
    row_peak = jnp.maximum(jnp.max(pool_scores, axis=-1), jnp.max(span_scores, axis=-1))
    pool_exp = jnp.where(visible, jnp.exp(pool_scores - row_peak[..., None]), 0.0)
    span_exp = jnp.where(causal, jnp.exp(span_scores - row_peak[..., None]), 0.0)
    row_total = jnp.sum(pool_exp, axis=-1) + jnp.sum(span_exp, axis=-1)
    pool_weight = (pool_exp / row_total[..., None]).astype(jnp.bfloat16)
    span_weight = (span_exp / row_total[..., None]).astype(jnp.bfloat16)
    mixed_rows = jnp.einsum(
        "jghp,pgd->jghd", pool_weight, pool_vals, preferred_element_type=jnp.float32
    )
    mixed_rows = mixed_rows + jnp.einsum(
        "jghi,igd->jghd", span_weight, span_kv[:, :, 1, :], preferred_element_type=jnp.float32
    )
    live = (row_iota < meta_row[2])[:, None, None, None]
    return jnp.where(live, mixed_rows, 0.0).astype(jnp.bfloat16).reshape(span_rows, -1)


def term_maker(rows_source, wo):
    return jnp.dot(rows_source, wo, preferred_element_type=jnp.float32)


def per_device(dec_q, dec_kv, dec_owner, dec_table, pre_q, pre_kv, pre_meta, pool, wo):
    groups = lax.axis_size("req")
    tp_count = lax.axis_size("tp")
    tok_rows = dec_q.shape[0]
    capacity = max(2, (2 * tok_rows + groups - 1) // groups)
    slot_count = groups * capacity
    q_width = dec_q.shape[1]
    kv_width = dec_kv.shape[1]
    kv_heads = pool.shape[1] // (2 * HD)
    group_iota = lax.iota(jnp.int32, groups)
    hot_table = (dec_owner[:, None] == group_iota[None, :]).astype(jnp.int32)
    ranking = jnp.sum((jnp.cumsum(hot_table, axis=0) - hot_table) * hot_table, axis=1)
    slot_ids = dec_owner * capacity + ranking
    dispatch = (slot_ids[None, :] == lax.iota(jnp.int32, slot_count)[:, None]).astype(jnp.bfloat16)
    send_q = (
        jnp.dot(dispatch, dec_q, preferred_element_type=jnp.float32)
        .astype(jnp.bfloat16)
        .reshape(groups, capacity, q_width)
    )
    send_kv = (
        jnp.dot(dispatch, dec_kv, preferred_element_type=jnp.float32)
        .astype(jnp.bfloat16)
        .reshape(groups, capacity, kv_width)
    )
    recv_q, recv_kv = (
        lax.all_to_all(send_q, "req", split_axis=0, concat_axis=0, tiled=True),
        lax.all_to_all(send_kv, "req", split_axis=0, concat_axis=0, tiled=True),
    )
    pool_rows = pool.reshape(pool.shape[0], kv_heads, 2, HD)
    pool_keys = pool_rows[:, :, 0, :]
    pool_vals = pool_rows[:, :, 1, :]
    q_slots = recv_q.reshape(slot_count, kv_heads, QPK, HD)
    kv_slots = recv_kv.reshape(slot_count, kv_heads, 2, HD)
    slot_attn = decode_block(q_slots, kv_slots, dec_table, pool_keys, pool_vals)
    replies = lax.all_to_all(
        slot_attn.reshape(groups, capacity, q_width), "req", split_axis=0, concat_axis=0, tiled=True
    )
    dec_attn = lax.dot_general(
        dispatch,
        replies.reshape(slot_count, q_width),
        (((0,), (0,)), ((), ())),
        preferred_element_type=jnp.float32,
    ).astype(jnp.bfloat16)
    pre_attn = prefill_attend(pre_q, pre_kv, pre_meta[0], pool_keys, pool_vals, kv_heads)
    share_dec = tok_rows // tp_count
    share_pre = pre_q.shape[0] // tp_count
    joined = jnp.concatenate(
        [
            dec_attn.reshape(tp_count, share_dec, q_width),
            pre_attn.reshape(tp_count, share_pre, q_width),
        ],
        axis=1,
    ).reshape(-1, q_width)
    summed = lax.psum_scatter(
        term_maker(joined, wo).astype(jnp.bfloat16), "tp", scatter_dimension=0, tiled=True
    ).astype(jnp.float32)
    dec_out = summed[:share_dec].astype(jnp.bfloat16)
    pre_out = summed[share_dec:].astype(jnp.bfloat16)
    return (dec_out, pre_out)


def solution(mesh):
    placed = (
        P("req", "tp"),
        P("req", "tp"),
        P("req"),
        P("req", None),
        P("req", "tp"),
        P("req", "tp"),
        P("req", None),
        P("req", "tp"),
        P("tp", None),
    )
    return jax.shard_map(
        per_device,
        mesh=mesh,
        in_specs=placed,
        out_specs=(P(("req", "tp"), None), P(("req", "tp"), None)),
        check_vma=False,
    )
```

profile of v0, /device:TPU:6, one launch (start us, length us, event | category | flops | bytes accessed | tf_op | source)
XLA Modules:
  0.0 138.3 jit_solution(9729089429358671733)
XLA Ops:
  7.2 0.9 fusion.26
  8.3 0.8 select_reduce_fusion
  9.8 1.0 convolution_convert_fusion.2
  11.5 14.2 %all-to-all-start.1 = ((bf16[64,4,256]{2,1,0:T(4,128)(2,1)}), bf16[64,4,256]{2,1,0:T(4,128)(2,1)}, u32[]{:S(2)}, u32[]{:S(2)}) async-start(bf16[64,4,256]{2,1,0:T(4,128)(2,1)} %reshape.233), calls=%async_computation.1 | async-start | bytes 262144 | tf_op jit(solution)/shard_map/all_to_all | solution.py:116
  26.3 1.1 copy.35
  31.8 1.2 fusion.36
  35.1 10.3 %all-to-all-start = ((bf16[64,4,384]{2,1,0:T(4,128)(2,1)}), bf16[64,4,384]{2,1,0:T(4,128)(2,1)S(1)}, u32[]{:S(2)}, u32[]{:S(2)}) async-start(bf16[64,4,384]{2,1,0:T(4,128)(2,1)} %reshape.229), calls=%async_computation | async-start | bytes 393216 | tf_op jit(solution)/shard_map/all_to_all | solution.py:115
  45.4 0.8 fusion.18
  46.3 1.0 reshape.234
  47.2 0.8 slice_convert_fusion
  48.0 7.6 %all-to-all-done = bf16[64,4,384]{2,1,0:T(4,128)(2,1)S(1)} async-done(((bf16[64,4,384]{2,1,0:T(4,128)(2,1)}), bf16[64,4,384]{2,1,0:T(4,128)(2,1)S(1)}, u32[]{:S(2)}, u32[]{:S(2)}) %all-to-all-start) | async-done | bytes 196640 | tf_op jit(solution)/shard_map/all_to_all | solution.py:115
  55.6 0.8 reshape.230
  56.4 2.0 %fusion.22 = f32[256,1,3]{2,1,0:T(1,128)} fusion(bf16[256,3,128]{2,1,0:T(4,128)(2,1)} %reshape.230, bf16[256,1,2,128]{3,2,0,1:T(2,128)(2,1)S(1)} %reshape.234), kind=kOutput, calls=%fused_computation.47 | convolution fusion | flops 196608 | bytes 330752 | tf_op jit(solution)/shard_map/sghd,sgd->sgh/dot_general | solution.py:28
  58.4 2.7 %fusion.37 = (f32[256,3]{0,1:T(4,128)S(1)}, f32[256,1,3,512]{3,0,2,1:T(8,128)}) fusion(bf16[512,1,2,128]{0,3,2,1:T(8,128)(2,1)} %bitcast.139, bf16[256,3,128]{2,1,0:T(4,128)(2,1)} %reshape.230, pred[256,512]{1,0:T(8,128)(4,1)} %fusion.18), kind=kOutput, calls=%fused_computation.74 | convolution fusion | flops 101842176 | bytes 2100224 | tf_op jit(solution)/shard_map/sghd,pgd->sghp/dot_general | solution.py:23
  61.1 1.0 copy.45
  62.1 2.1 %fusion.3 = f32[256,3]{0,1:T(4,128)S(1)} fusion(f32[256,1,3,512]{3,0,2,1:T(8,128)} %get-tuple-element.14, f32[256,3]{0,1:T(4,128)S(1)} %fusion.27, pred[256,512]{1,0:T(8,128)(4,1)S(1)} %copy-done.7), kind=kLoop, calls=%fused_computation.12 | loop fusion | flops 1178880 | bytes 1710080 | tf_op jit(solution)/shard_map/reduce_sum | solution.py:36
  65.0 0.8 reshape_reshape.6
  65.9 6.4 %all-to-all-start.2 = ((bf16[64,4,384]{2,1,0:T(4,128)(2,1)}), bf16[64,4,384]{2,1,0:T(4,128)(2,1)S(1)}, u32[]{:S(2)}, u32[]{:S(2)}) async-start(bf16[64,4,384]{2,1,0:T(4,128)(2,1)} %reshape_reshape.6), calls=%async_computation.2 | async-start | bytes 393216 | tf_op jit(solution)/shard_map/all_to_all | solution.py:124
  72.4 1.9 %fusion.12 = f32[256,3,128]{2,0,1:T(8,128)S(1)} fusion(f32[1,512,256,3]{1,2,3,0:T(8,128)} %copy-done.1, f32[256,3]{0,1:T(4,128)S(1)} %copy-done.15, f32[256,3]{0,1:T(4,128)S(1)} %max.14, pred[512]{0:T(512)(128)(4,1)S(1)} %copy-done.17, bf16[512,1,2,128]{0,3,2,1:T(8,128)(2,1)} %bitcast.140), kind=kOutput, calls=%fused_computation.26 | convolution fusion | flops 102236160 | bytes 2103808 | tf_op jit(solution)/shard_map/jghp,pgd->jghd/dot_general | solution.py:76
  75.7 6.7 %all-to-all-done.2 = bf16[64,4,384]{2,1,0:T(4,128)(2,1)S(1)} async-done(((bf16[64,4,384]{2,1,0:T(4,128)(2,1)}), bf16[64,4,384]{2,1,0:T(4,128)(2,1)S(1)}, u32[]{:S(2)}, u32[]{:S(2)}) %all-to-all-start.2) | async-done | bytes 196640 | tf_op jit(solution)/shard_map/all_to_all | solution.py:124
  82.8 2.8 %convolution_convert_fusion = bf16[384,3072]{1,0:T(8,128)(2,1)} fusion(bf16[384,384]{1,0:T(8,128)(2,1)S(1)} %bitcast.137, bf16[384,3072]{1,0:T(8,128)(2,1)S(1)} %copy-done), kind=kOutput, calls=%fused_computation | convolution fusion | flops 907149312 | bytes 5013504 | tf_op jit(solution)/shard_map/dot_general | solution.py:87
  85.7 42.6 %reduce-scatter.2.cloned.1.call-done = bf16[48,3072]{1,0:T(8,128)(2,1)} async-done(((bf16[384,3072]{1,0:T(8,128)(2,1)}), bf16[48,3072]{1,0:T(8,128)(2,1)}) %reduce-scatter.2.cloned.1.call-update) | async-done | bytes 294928 | tf_op jit(solution)/shard_map/reduce_scatter | solution.py:143
  128.3 1.5 %slice.64 = bf16[16,3072]{1,0:T(8,128)(2,1)} slice(bf16[48,3072]{1,0:T(8,128)(2,1)} %reduce-scatter.2.cloned.1.call-done), slice={[0:16], [0:3072]} | slice | bytes 196608 | tf_op jit(solution)/shard_map/slice | solution.py:146
  129.9 1.6 %slice.65 = bf16[32,3072]{1,0:T(8,128)(2,1)} slice(bf16[48,3072]{1,0:T(8,128)(2,1)} %reduce-scatter.2.cloned.1.call-done), slice={[16:48], [0:3072]} | slice | bytes 393216 | tf_op jit(solution)/shard_map/slice | solution.py:147
  (68 shorter events, 9.8 us)
Async XLA Ops:
  7.2 75.7 %copy-start = (bf16[384,3072]{1,0:T(8,128)(2,1)S(1)}, bf16[384,3072]{1,0:T(8,128)(2,1)}, u32[]{:S(2)}) copy-start(bf16[384,3072]{1,0:T(8,128)(2,1)} %param.17) | copy-start | bytes 7077892
  7.2 20.2 %copy-start.10 = (bf16[512,256]{1,0:T(8,128)(2,1)S(1)}, bf16[512,256]{1,0:T(8,128)(2,1)}, u32[]{:S(2)}) copy-start(bf16[512,256]{1,0:T(8,128)(2,1)} %param.16) | copy-start | bytes 786436
  7.2 20.4 %copy-start.14 = (s32[1,3]{1,0:T(1,128)S(1)}, s32[1,3]{1,0:T(1,128)}, u32[]{:S(2)}) copy-start(s32[1,3]{1,0:T(1,128)} %param.15) | copy-start | bytes 40
  7.2 22.9 %copy-start.11 = (bf16[256,256]{1,0:T(8,128)(2,1)S(1)}, bf16[256,256]{1,0:T(8,128)(2,1)}, u32[]{:S(2)}) copy-start(bf16[256,256]{1,0:T(8,128)(2,1)} %param.14) | copy-start | bytes 393220
  7.2 23.7 %copy-start.13 = (bf16[128,384]{1,0:T(8,128)(2,1)S(1)}, bf16[128,384]{1,0:T(8,128)(2,1)}, u32[]{:S(2)}) copy-start(bf16[128,384]{1,0:T(8,128)(2,1)} %param.9) | copy-start | bytes 294916
  11.5 23.6 %all-to-all-start.1 = ((bf16[64,4,256]{2,1,0:T(4,128)(2,1)}), bf16[64,4,256]{2,1,0:T(4,128)(2,1)}, u32[]{:S(2)}, u32[]{:S(2)}) async-start(bf16[64,4,256]{2,1,0:T(4,128)(2,1)} %reshape.233), calls=%async_computation.1 | async-start | bytes 262144 | tf_op jit(solution)/shard_map/all_to_all | solution.py:116
  27.6 4.0 %copy-start.3 = (bf16[512,256]{0,1:T(8,128)(2,1)}, bf16[512,256]{0,1:T(8,128)(2,1)S(1)}, u32[]{:S(2)}) copy-start(bf16[512,256]{0,1:T(8,128)(2,1)S(1)} %copy.30) | copy-start | bytes 786436
  30.1 2.9 %copy-start.16 = (pred[512]{0:T(512)(128)(4,1)}, pred[512]{0:T(512)(128)(4,1)S(1)}, u32[]{:S(2)}) copy-start(pred[512]{0:T(512)(128)(4,1)S(1)} %fusion.28) | copy-start | bytes 1540
  30.9 0.9 copy-start.8
  31.6 1.5 %copy-start.1 = (f32[1,512,256,3]{1,2,3,0:T(8,128)}, f32[1,512,256,3]{1,2,3,0:T(8,128)S(1)}, u32[]{:S(2)}) copy-start(f32[1,512,256,3]{1,2,3,0:T(8,128)S(1)} %get-tuple-element.10) | copy-start | bytes 4718596
  31.6 1.9 %copy-start.5 = (pred[256,256]{0,1:T(8,128)(4,1)S(1)}, pred[256,256]{0,1:T(8,128)(4,1)}, u32[]{:S(2)}) copy-start(pred[256,256]{0,1:T(8,128)(4,1)} %iota_compare_fusion.2) | copy-start | bytes 196612
  33.0 2.0 %copy-start.18 = (s32[256,2]{0,1:T(2,128)S(1)}, s32[256,2]{0,1:T(2,128)}, u32[]{:S(2)}) copy-start(s32[256,2]{0,1:T(2,128)} %param.12) | copy-start | bytes 6148
  35.1 20.5 %all-to-all-start = ((bf16[64,4,384]{2,1,0:T(4,128)(2,1)}), bf16[64,4,384]{2,1,0:T(4,128)(2,1)S(1)}, u32[]{:S(2)}, u32[]{:S(2)}) async-start(bf16[64,4,384]{2,1,0:T(4,128)(2,1)} %reshape.229), calls=%async_computation | async-start | bytes 393216 | tf_op jit(solution)/shard_map/all_to_all | solution.py:115
  58.4 3.7 %copy-start.7 = (pred[256,512]{1,0:T(8,128)(4,1)S(1)}, pred[256,512]{1,0:T(8,128)(4,1)}, u32[]{:S(2)}) copy-start(pred[256,512]{1,0:T(8,128)(4,1)} %fusion.18) | copy-start | bytes 393220
  58.4 5.8 %copy-start.4 = (bf16[512,256]{0,1:T(8,128)(2,1)S(1)}, bf16[512,256]{0,1:T(8,128)(2,1)}, u32[]{:S(2)}) copy-start(bf16[512,256]{0,1:T(8,128)(2,1)} %copy-done.3) | copy-start | bytes 786436
  62.1 2.2 %copy-start.2 = (f32[256,1,3,512]{3,0,2,1:T(8,128)S(1)}, f32[256,1,3,512]{3,0,2,1:T(8,128)}, u32[]{:S(2)}) copy-start(f32[256,1,3,512]{3,0,2,1:T(8,128)} %get-tuple-element.14) | copy-start | bytes 4718596
  62.1 2.2 %copy-start.12 = (f32[256,1,1,128]{3,2,0,1:T(1,128)S(1)}, f32[256,1,1,128]{3,2,0,1:T(1,128)}, u32[]{:S(2)}) copy-start(f32[256,1,1,128]{3,2,0,1:T(1,128)} %slice_convert_fusion) | copy-start | bytes 393220
  64.2 8.1 %copy-start.15 = (f32[256,3]{0,1:T(4,128)S(1)}, f32[256,3]{0,1:T(4,128)}, u32[]{:S(2)}) copy-start(f32[256,3]{0,1:T(4,128)} %add.42) | copy-start | bytes 9220
  64.2 8.1 %copy-start.17 = (pred[512]{0:T(512)(128)(4,1)S(1)}, pred[512]{0:T(512)(128)(4,1)}, u32[]{:S(2)}) copy-start(pred[512]{0:T(512)(128)(4,1)} %copy-done.16) | copy-start | bytes 1540
  65.9 16.6 %all-to-all-start.2 = ((bf16[64,4,384]{2,1,0:T(4,128)(2,1)}), bf16[64,4,384]{2,1,0:T(4,128)(2,1)S(1)}, u32[]{:S(2)}, u32[]{:S(2)}) async-start(bf16[64,4,384]{2,1,0:T(4,128)(2,1)} %reshape_reshape.6), calls=%async_computation.2 | async-start | bytes 393216 | tf_op jit(solution)/shard_map/all_to_all | solution.py:124
  72.3 2.7 %copy-start.6 = (pred[256,256]{0,1:T(8,128)(4,1)S(1)}, pred[256,256]{0,1:T(8,128)(4,1)}, u32[]{:S(2)}) copy-start(pred[256,256]{0,1:T(8,128)(4,1)} %iota_compare_fusion.2) | copy-start | bytes 196612
  72.3 2.7 %copy-start.9 = (bf16[256,256]{0,1:T(8,128)(2,1)S(1)}, bf16[256,256]{0,1:T(8,128)(2,1)}, u32[]{:S(2)}) copy-start(bf16[256,256]{0,1:T(8,128)(2,1)} %copy.38) | copy-start | bytes 393220
  72.3 56.0 %reduce-scatter.2.cloned.1.call-start = ((), (), s32[]{:S(2)}) async-start(), calls=%async_computation.4 | async-start | bytes 2654208 | tf_op jit(solution)/shard_map/reduce_scatter | solution.py:143
Sparse Core Ops, SparseCore 0:
  85.8 42.4 reduce-scatter.1
where the time goes:
time: 139 us; the launch traced here: 138 us
  waiting for transfers between devices  57 us (41%)
  starting transfers between devices  31 us (22%)
  between operations  15.7 us (11%)
  matrix products  13.6 us (10%)
  local copies, waits for them, and re-layouts  11.5 us (8%)
  other arithmetic  9.47 us (7%)
    reduce_scatter x1, waiting for transfers between devices, per_device(): lax.psum_scatter(term_maker(joined, wo).astype(jnp.bfloat16), 'tp', scatt...  42.6 us
    all_to_all x1, starting transfers between devices, per_device(): lax.all_to_all(send_kv, 'req', split_axis=0, concat_axis=0, tiled=True)  14.2 us
    all_to_all x1, starting transfers between devices, per_device(): lax.all_to_all(send_q, 'req', split_axis=0, concat_axis=0, tiled=True)  10.3 us
    all_to_all x1, waiting for transfers between devices, per_device(): lax.all_to_all(send_q, 'req', split_axis=0, concat_axis=0, tiled=True)  7.61 us
    all_to_all x1, waiting for transfers between devices, per_device(): lax.all_to_all(slot_attn.reshape(groups, capacity, q_width), 'req', split...  6.74 us
    all_to_all x1, starting transfers between devices, per_device(): lax.all_to_all(slot_attn.reshape(groups, capacity, q_width), 'req', split...  6.41 us
    dot_general x1, matrix products, term_maker(): return jnp.dot(rows_source, wo, preferred_element_type=jnp.float32)  2.83 us
  transfers between devices with their start and end apart: 4, of which 3 were waited for; matrix products, arithmetic and copies ran while one was open for 10% of the time, Pallas kernels for 0%

commit v1 on v0

--- a/solution.py
+++ b/solution.py
@@ -89,62 +89,50 @@
 
 def per_device(dec_q, dec_kv, dec_owner, dec_table, pre_q, pre_kv, pre_meta, pool, wo):
     groups = lax.axis_size("req")
-    tp_count = lax.axis_size("tp")
     tok_rows = dec_q.shape[0]
     capacity = max(2, (2 * tok_rows + groups - 1) // groups)
     slot_count = groups * capacity
     q_width = dec_q.shape[1]
     kv_width = dec_kv.shape[1]
     kv_heads = pool.shape[1] // (2 * HD)
+    pool_rows = pool.reshape(pool.shape[0], kv_heads, 2, HD)
+    pool_keys = pool_rows[:, :, 0, :]
+    pool_vals = pool_rows[:, :, 1, :]
+
+    pre_attn = prefill_attend(pre_q, pre_kv, pre_meta[0], pool_keys, pool_vals, kv_heads)
+    pre_part = term_maker(pre_attn, wo).astype(jnp.bfloat16)
+
     group_iota = lax.iota(jnp.int32, groups)
     hot_table = (dec_owner[:, None] == group_iota[None, :]).astype(jnp.int32)
     ranking = jnp.sum((jnp.cumsum(hot_table, axis=0) - hot_table) * hot_table, axis=1)
     slot_ids = dec_owner * capacity + ranking
     dispatch = (slot_ids[None, :] == lax.iota(jnp.int32, slot_count)[:, None]).astype(jnp.bfloat16)
-    send_q = (
-        jnp.dot(dispatch, dec_q, preferred_element_type=jnp.float32)
+    send = (
+        jnp.dot(dispatch, jnp.concatenate([dec_q, dec_kv], axis=1), preferred_element_type=jnp.float32)
         .astype(jnp.bfloat16)
-        .reshape(groups, capacity, q_width)
+        .reshape(groups, capacity, q_width + kv_width)
     )
-    send_kv = (
-        jnp.dot(dispatch, dec_kv, preferred_element_type=jnp.float32)
-        .astype(jnp.bfloat16)
-        .reshape(groups, capacity, kv_width)
+    recv = lax.all_to_all(send, "req", split_axis=0, concat_axis=0, tiled=True).reshape(
+        slot_count, q_width + kv_width
     )
-    recv_q, recv_kv = (
-        lax.all_to_all(send_q, "req", split_axis=0, concat_axis=0, tiled=True),
-        lax.all_to_all(send_kv, "req", split_axis=0, concat_axis=0, tiled=True),
-    )
-    pool_rows = pool.reshape(pool.shape[0], kv_heads, 2, HD)
-    pool_keys = pool_rows[:, :, 0, :]
-    pool_vals = pool_rows[:, :, 1, :]
-    q_slots = recv_q.reshape(slot_count, kv_heads, QPK, HD)
-    kv_slots = recv_kv.reshape(slot_count, kv_heads, 2, HD)
+    pre_part, recv = lax.optimization_barrier((pre_part, recv))
+    pre_out = lax.psum_scatter(pre_part, "tp", scatter_dimension=0, tiled=True)
+    q_slots = recv[:, :q_width].reshape(slot_count, kv_heads, QPK, HD)
+    kv_slots = recv[:, q_width:].reshape(slot_count, kv_heads, 2, HD)
     slot_attn = decode_block(q_slots, kv_slots, dec_table, pool_keys, pool_vals)
     replies = lax.all_to_all(
         slot_attn.reshape(groups, capacity, q_width), "req", split_axis=0, concat_axis=0, tiled=True
     )
+    pre_out, replies = lax.optimization_barrier((pre_out, replies))
     dec_attn = lax.dot_general(
         dispatch,
         replies.reshape(slot_count, q_width),
         (((0,), (0,)), ((), ())),
         preferred_element_type=jnp.float32,
     ).astype(jnp.bfloat16)
-    pre_attn = prefill_attend(pre_q, pre_kv, pre_meta[0], pool_keys, pool_vals, kv_heads)
-    share_dec = tok_rows // tp_count
-    share_pre = pre_q.shape[0] // tp_count
-    joined = jnp.concatenate(
-        [
-            dec_attn.reshape(tp_count, share_dec, q_width),
-            pre_attn.reshape(tp_count, share_pre, q_width),
-        ],
-        axis=1,
-    ).reshape(-1, q_width)
-    summed = lax.psum_scatter(
-        term_maker(joined, wo).astype(jnp.bfloat16), "tp", scatter_dimension=0, tiled=True
-    ).astype(jnp.float32)
-    dec_out = summed[:share_dec].astype(jnp.bfloat16)
-    pre_out = summed[share_dec:].astype(jnp.bfloat16)
+    dec_out = lax.psum_scatter(
+        term_maker(dec_attn, wo).astype(jnp.bfloat16), "tp", scatter_dimension=0, tiled=True
+    )
     return (dec_out, pre_out)
 
 

time: 139 us -> 129 us (0.928)
  blocking collectives: 0 us -> 17 us
  starting transfers between devices: 31 us -> 14.1 us
  waiting for transfers between devices: 57 us -> 64.8 us
  local copies, waits for them, and re-layouts: 11.5 us -> 4.08 us
  matrix products: 13.6 us -> 7.62 us
  other arithmetic: 9.47 us -> 5.57 us
    reduce_scatter x1 -> x2, waiting for transfers between devices: 42.6 us -> 60.9 us  [the longest x1 41.3 us: per_device(): lax.psum_scatter(term_maker(dec_attn, wo).astype(jnp.bfloat16), 'tp', sca...]
    all_to_all x0 -> x1, blocking collectives: none -> 17 us  [per_device(): lax.all_to_all(slot_attn.reshape(groups, capacity, q_width), 'req', split...]
    all_to_all x3 -> x1, starting transfers between devices: 31 us -> 14 us  [per_device(): lax.all_to_all(send, 'req', split_axis=0, concat_axis=0, tiled=True)]
    all_to_all x3 -> x1, waiting for transfers between devices: 14.4 us -> 3.84 us  [per_device(): lax.all_to_all(send, 'req', split_axis=0, concat_axis=0, tiled=True)]
    slice x2 -> x4, local copies, waits for them, and re-layouts: 3.15 us -> 0.28 us  [the longest x2 0.17 us: per_device(): q_slots = recv[:, :q_width].reshape(slot_count, kv_heads, QPK, HD)]
    dot_general x4 -> x1, matrix products: 3.44 us -> 1.16 us  [per_device(): jnp.dot(dispatch, jnp.concatenate([dec_q, dec_kv], axis=1), preferred_ele...]
    dot_general x1, matrix products: 2.67 us -> 0.45 us  [decode_block(): jnp.einsum('sghd,pgd->sghp', q_block, pool_keys, preferred_element_type=j...]
    reduce_sum x1, other arithmetic: 2.08 us -> 0.31 us  [decode_block(): row_total = jnp.sum(pool_exp, axis=-1) + self_exp]
  transfers between devices with their start and end apart: 4 -> 3, of which waited for: 3 -> 3; matrix products, arithmetic and copies ran while one was open for 10% -> 8% of each run, Pallas kernels for 0% -> 0%
where the time goes in v1:
time: 129 us
  waiting for transfers between devices  64.8 us (50%)
  blocking collectives  17 us (13%)
  between operations  15.7 us (12%)
  starting transfers between devices  14.1 us (11%)
  matrix products  7.62 us (6%)
  other arithmetic  5.57 us (4%)
  local copies, waits for them, and re-layouts  4.08 us (3%)
    reduce_scatter x1, waiting for transfers between devices, per_device(): lax.psum_scatter(term_maker(dec_attn, wo).astype(jnp.bfloat16), 'tp', sca...  41.3 us
    reduce_scatter x1, waiting for transfers between devices, per_device(): pre_out = lax.psum_scatter(pre_part, 'tp', scatter_dimension=0, tiled=True)  19.6 us
    all_to_all x1, blocking collectives, per_device(): lax.all_to_all(slot_attn.reshape(groups, capacity, q_width), 'req', split...  17 us
    all_to_all x1, starting transfers between devices, per_device(): lax.all_to_all(send, 'req', split_axis=0, concat_axis=0, tiled=True)  14 us
    all_to_all x1, waiting for transfers between devices, per_device(): lax.all_to_all(send, 'req', split_axis=0, concat_axis=0, tiled=True)  3.84 us
    dot_general x2, matrix products, term_maker(): return jnp.dot(rows_source, wo, preferred_element_type=jnp.float32)  3.78 us
  transfers between devices with their start and end apart: 3, of which 3 were waited for; matrix products, arithmetic and copies ran while one was open for 8% of the time, Pallas kernels for 0%

profile of v1, /device:TPU:6, one launch (start us, length us, event | category | flops | bytes accessed | tf_op | source)
XLA Modules:
  0.0 128.8 jit_solution(13625736870289806648)
XLA Ops:
  7.2 0.9 fusion.27
  8.3 0.8 select_reduce_fusion
  9.1 0.7 multiply_add_fusion
  9.8 1.2 convolution_convert_fusion.2
  10.9 0.8 reshape.236
  11.8 14.0 %all-to-all-start = ((bf16[64,4,640]{2,1,0:T(4,128)(2,1)}), bf16[64,4,640]{2,1,0:T(4,128)(2,1)S(1)}, u32[]{:S(2)}, u32[]{:S(2)}) async-start(bf16[64,4,640]{2,1,0:T(4,128)(2,1)} %reshape.236), calls=%async_computation | async-start | bytes 655360 | tf_op jit(solution)/shard_map/all_to_all | solution.py:115
  26.2 0.7 fusion.36
  28.2 0.7 fusion.28
  28.9 1.0 copy.39
  29.9 0.4 bitcast_reduce_fusion
  31.1 0.5 fusion.12
  31.6 0.7 iota_compare_fusion.10
  32.3 0.3 fusion.9
  32.6 2.2 %convolution_convert_fusion = bf16[256,3072]{1,0:T(8,128)(2,1)} fusion(bf16[256,384]{0,1:T(8,128)(2,1)S(1)} %bitcast.132, bf16[384,3072]{1,0:T(8,128)(2,1)S(1)} %copy-done), kind=kOutput, calls=%fused_computation | convolution fusion | flops 604766208 | bytes 4128768 | tf_op jit(solution)/shard_map/dot_general | solution.py:87
  34.8 3.8 %all-to-all-done = bf16[64,4,640]{2,1,0:T(4,128)(2,1)S(1)} async-done(((bf16[64,4,640]{2,1,0:T(4,128)(2,1)}), bf16[64,4,640]{2,1,0:T(4,128)(2,1)S(1)}, u32[]{:S(2)}, u32[]{:S(2)}) %all-to-all-start) | async-done | bytes 327712 | tf_op jit(solution)/shard_map/all_to_all | solution.py:115
  38.8 0.8 fusion.16
  40.1 0.5 copy-done.1
  40.5 0.4 fusion.38
  41.0 0.3 fusion.3
  41.3 0.7 fusion.10
  42.4 17.0 %all_to_all.10 = bf16[64,4,384]{2,1,0:T(4,128)(2,1)S(1)} all-to-all(bf16[64,4,384]{2,1,0:T(4,128)(2,1)S(1)} %reshape_reshape.3), channel_id=1, replica_groups=mesh['req'=64,'tp'=8] {'req'}, dimensions={0} | all-to-all | bytes 393216 | tf_op jit(solution)/shard_map/all_to_all | solution.py:123
  59.4 19.6 %reduce-scatter.3.cloned.1.call-done = bf16[32,3072]{1,0:T(8,128)(2,1)} async-done(((bf16[256,3072]{1,0:T(8,128)(2,1)}), bf16[32,3072]{1,0:T(8,128)(2,1)}) %reduce-scatter.3.cloned.1.call-update) | async-done | bytes 196624 | tf_op jit(solution)/shard_map/reduce_scatter | solution.py:119
  79.0 1.6 %convolution_convert_fusion.1 = bf16[128,3072]{1,0:T(8,128)(2,1)} fusion(bf16[384,3072]{1,0:T(8,128)(2,1)S(1)} %copy-done, bf16[256,384]{1,0:T(8,128)(2,1)S(1)} %reshape.242, s32[128]{0:T(128)S(1)} %multiply_add_fusion), kind=kOutput, calls=%fused_computation.1 | convolution fusion | flops 327630848 | bytes 3342848 | tf_op jit(solution)/shard_map/dot_general | solution.py:87
  80.6 41.3 %reduce-scatter.5.cloned.1.call-done = bf16[16,3072]{1,0:T(8,128)(2,1)} async-done(((bf16[128,3072]{1,0:T(8,128)(2,1)}), bf16[16,3072]{1,0:T(8,128)(2,1)}) %reduce-scatter.5.cloned.1.call-update) | async-done | bytes 98320 | tf_op jit(solution)/shard_map/reduce_scatter | solution.py:133
  (38 shorter events, 2.3 us)
Async XLA Ops:
  7.2 25.5 %copy-start = (bf16[384,3072]{1,0:T(8,128)(2,1)S(1)}, bf16[384,3072]{1,0:T(8,128)(2,1)}, u32[]{:S(2)}) copy-start(bf16[384,3072]{1,0:T(8,128)(2,1)} %param.17) | copy-start | bytes 7077892
  7.2 18.7 %copy-start.3 = (bf16[256,384]{1,0:T(8,128)(2,1)S(1)}, bf16[256,384]{1,0:T(8,128)(2,1)}, u32[]{:S(2)}) copy-start(bf16[256,384]{1,0:T(8,128)(2,1)} %param.13) | copy-start | bytes 589828
  7.2 18.8 %copy-start.2 = (bf16[512,256]{1,0:T(8,128)(2,1)S(1)}, bf16[512,256]{1,0:T(8,128)(2,1)}, u32[]{:S(2)}) copy-start(bf16[512,256]{1,0:T(8,128)(2,1)} %param.16) | copy-start | bytes 786436
  7.2 19.0 %copy-start.4 = (s32[1,3]{1,0:T(1,128)S(1)}, s32[1,3]{1,0:T(1,128)}, u32[]{:S(2)}) copy-start(s32[1,3]{1,0:T(1,128)} %param.15) | copy-start | bytes 40
  11.8 26.9 %all-to-all-start = ((bf16[64,4,640]{2,1,0:T(4,128)(2,1)}), bf16[64,4,640]{2,1,0:T(4,128)(2,1)S(1)}, u32[]{:S(2)}, u32[]{:S(2)}) async-start(bf16[64,4,640]{2,1,0:T(4,128)(2,1)} %reshape.236), calls=%async_computation | async-start | bytes 655360 | tf_op jit(solution)/shard_map/all_to_all | solution.py:115
  25.8 53.2 %reduce-scatter.3.cloned.1.call-start = ((), (), s32[]{:S(2)}) async-start(), calls=%async_computation.4 | async-start | bytes 1769472 | tf_op jit(solution)/shard_map/reduce_scatter | solution.py:119
  34.8 4.0 %copy-start.5 = (s32[256,2]{0,1:T(2,128)S(1)}, s32[256,2]{0,1:T(2,128)}, u32[]{:S(2)}) copy-start(s32[256,2]{0,1:T(2,128)} %param.12) | copy-start | bytes 6148
  38.8 83.2 %reduce-scatter.5.cloned.1.call-start = ((), (), s32[]{:S(2)}) async-start(), calls=%async_computation.5 | async-start | bytes 884736 | tf_op jit(solution)/shard_map/reduce_scatter | solution.py:133
  39.6 0.9 copy-start.1
Sparse Core Ops, SparseCore 0:
  38.9 40.0 reduce-scatter.2
  82.3 39.5 reduce-scatter.4

commit v2 on v1

--- a/solution.py
+++ b/solution.py
@@ -87,6 +87,28 @@
     return jnp.dot(rows_source, wo, preferred_element_type=jnp.float32)
 
 
+def ring_sum_scatter(part, axis):
+    n = lax.axis_size(axis)
+    me = lax.axis_index(axis)
+    rows = part.shape[0] // n
+    half = rows // 2
+    chunks = part.reshape(n, rows, part.shape[1])
+    fwd_chunks = chunks[:, :half]
+    bwd_chunks = chunks[:, half:]
+    fwd_perm = [(i, (i + 1) % n) for i in range(n)]
+    bwd_perm = [(i, (i + n - 1) % n) for i in range(n)]
+
+    def pick(source, index):
+        return lax.dynamic_index_in_dim(source, index % n, 0, keepdims=False).astype(jnp.float32)
+
+    fwd = pick(fwd_chunks, me + n - 1)
+    bwd = pick(bwd_chunks, me + 1)
+    for step in range(n - 1):
+        fwd = lax.ppermute(fwd, axis, fwd_perm) + pick(fwd_chunks, me + 2 * n - step - 2)
+        bwd = lax.ppermute(bwd, axis, bwd_perm) + pick(bwd_chunks, me + step + 2)
+    return jnp.concatenate([fwd, bwd], axis=0).astype(jnp.bfloat16)
+
+
 def per_device(dec_q, dec_kv, dec_owner, dec_table, pre_q, pre_kv, pre_meta, pool, wo):
     groups = lax.axis_size("req")
     tok_rows = dec_q.shape[0]
@@ -123,16 +145,13 @@
     replies = lax.all_to_all(
         slot_attn.reshape(groups, capacity, q_width), "req", split_axis=0, concat_axis=0, tiled=True
     )
-    pre_out, replies = lax.optimization_barrier((pre_out, replies))
     dec_attn = lax.dot_general(
         dispatch,
         replies.reshape(slot_count, q_width),
         (((0,), (0,)), ((), ())),
         preferred_element_type=jnp.float32,
     ).astype(jnp.bfloat16)
-    dec_out = lax.psum_scatter(
-        term_maker(dec_attn, wo).astype(jnp.bfloat16), "tp", scatter_dimension=0, tiled=True
-    )
+    dec_out = ring_sum_scatter(term_maker(dec_attn, wo).astype(jnp.bfloat16), "tp")
     return (dec_out, pre_out)
 
 

time: 129 us -> 136 us (1.054)
  the two profiles are of different devices: /device:TPU:6 before, /device:TPU:28 now
where the time goes in v2:
time: 136 us; the launch traced here: 135 us
  starting transfers between devices  70.6 us (52%)
  waiting for transfers between devices  30 us (22%)
  between operations  16 us (12%)
  matrix products  7.67 us (6%)
  other arithmetic  6.35 us (5%)
  local copies, waits for them, and re-layouts  4.33 us (3%)
    ppermute x7, starting transfers between devices, ring_sum_scatter(): lax.ppermute(fwd, axis, fwd_perm) + pick(fwd_chunks, me + 2 * n - step - 2)  36.2 us
    ppermute x7, waiting for transfers between devices, ring_sum_scatter(): bwd = lax.ppermute(bwd, axis, bwd_perm) + pick(bwd_chunks, me + step + 2)  16.3 us
    all_to_all x1, starting transfers between devices, per_device(): lax.all_to_all(send, 'req', split_axis=0, concat_axis=0, tiled=True)  13.9 us
    ppermute x7, starting transfers between devices, ring_sum_scatter(): bwd = lax.ppermute(bwd, axis, bwd_perm) + pick(bwd_chunks, me + step + 2)  13.4 us
    all_to_all x1, waiting for transfers between devices, per_device(): lax.all_to_all(slot_attn.reshape(groups, capacity, q_width), 'req', split...  9.46 us
    all_to_all x1, starting transfers between devices, per_device(): lax.all_to_all(slot_attn.reshape(groups, capacity, q_width), 'req', split...  6.95 us
    all_to_all x1, waiting for transfers between devices, per_device(): lax.all_to_all(send, 'req', split_axis=0, concat_axis=0, tiled=True)  3.38 us
    dot_general x2, matrix products, term_maker(): return jnp.dot(rows_source, wo, preferred_element_type=jnp.float32)  2.91 us
  transfers between devices with their start and end apart: 17, of which 10 were waited for; matrix products, arithmetic and copies ran while one was open for 7% of the time, Pallas kernels for 0%

profile of v2, /device:TPU:28, one launch (start us, length us, event | category | flops | bytes accessed | tf_op | source)
XLA Modules:
  0.0 134.9 jit_solution(10148326410104173672)
XLA Ops:
  11.8 13.9 %all-to-all-start = ((bf16[64,4,640]{2,1,0:T(4,128)(2,1)}), bf16[64,4,640]{2,1,0:T(4,128)(2,1)S(1)}, u32[]{:S(2)}, u32[]{:S(2)}) async-start(bf16[64,4,640]{2,1,0:T(4,128)(2,1)} %reshape.271), calls=%async_computation | async-start | bytes 655360 | tf_op jit(solution)/shard_map/all_to_all | solution.py:137
  33.0 2.2 %convolution_convert_fusion = bf16[256,3072]{1,0:T(8,128)(2,1)} fusion(bf16[256,384]{0,1:T(8,128)(2,1)S(1)} %bitcast.182, bf16[384,3072]{1,0:T(8,128)(2,1)S(1)} %copy-done), kind=kOutput, calls=%fused_computation | convolution fusion | flops 604766208 | bytes 4128768 | tf_op jit(solution)/shard_map/dot_general | solution.py:87
  35.2 3.4 %all-to-all-done = bf16[64,4,640]{2,1,0:T(4,128)(2,1)S(1)} async-done(((bf16[64,4,640]{2,1,0:T(4,128)(2,1)}), bf16[64,4,640]{2,1,0:T(4,128)(2,1)S(1)}, u32[]{:S(2)}, u32[]{:S(2)}) %all-to-all-start) | async-done | bytes 327712 | tf_op jit(solution)/shard_map/all_to_all | solution.py:137
  42.6 6.9 %all-to-all-start.1 = ((bf16[64,4,384]{2,1,0:T(4,128)(2,1)}), bf16[64,4,384]{2,1,0:T(4,128)(2,1)S(1)}, u32[]{:S(2)}, u32[]{:S(2)}) async-start(bf16[64,4,384]{2,1,0:T(4,128)(2,1)} %reshape_reshape.3), calls=%async_computation.1 | async-start | bytes 393216 | tf_op jit(solution)/shard_map/all_to_all | solution.py:145
  50.3 9.5 %all-to-all-done.1 = bf16[64,4,384]{2,1,0:T(4,128)(2,1)S(1)} async-done(((bf16[64,4,384]{2,1,0:T(4,128)(2,1)}), bf16[64,4,384]{2,1,0:T(4,128)(2,1)S(1)}, u32[]{:S(2)}, u32[]{:S(2)}) %all-to-all-start.1) | async-done | bytes 196640 | tf_op jit(solution)/shard_map/all_to_all | solution.py:145
  60.6 4.7 %collective-permute-start = (f32[8,3072]{1,0:T(8,128)S(1)}, f32[8,3072]{1,0:T(8,128)S(1)}, u32[]{:S(2)}, u32[]{:S(2)}) collective-permute-start(f32[8,3072]{1,0:T(8,128)S(1)} %bitcast_convert_fusion.1), channel_id=1, source_target_pairs={{0,1},{1,2},{2,3},{3,4},{4,5},{5,6},{6,7},{7,0},{8,9},{9,10},{10,1... | collective-permute-start | bytes 294920 | tf_op jit(solution)/shard_map/ppermute | solution.py:107
  65.4 1.9 %collective-permute-start.7 = (f32[8,3072]{1,0:T(8,128)S(1)}, f32[8,3072]{1,0:T(8,128)S(1)}, u32[]{:S(2)}, u32[]{:S(2)}) collective-permute-start(f32[8,3072]{1,0:T(8,128)S(1)} %bitcast_convert_fusion), channel_id=1, source_target_pairs={{0,7},{1,0},{2,1},{3,2},{4,3},{5,4},{6,5},{7,6},{8,15},{9,8},{10,9... | collective-permute-start | bytes 294920 | tf_op jit(solution)/shard_map/ppermute | solution.py:108
  67.7 5.6 %collective-permute-start.1 = (f32[8,3072]{1,0:T(8,128)S(1)}, f32[8,3072]{1,0:T(8,128)S(1)}, u32[]{:S(2)}, u32[]{:S(2)}) collective-permute-start(f32[8,3072]{1,0:T(8,128)S(1)} %convert_add_fusion.13), channel_id=1, source_target_pairs={{0,1},{1,2},{2,3},{3,4},{4,5},{5,6},{6,7},{7,0},{8,9},{9,10},{10,1... | collective-permute-start | bytes 294920 | tf_op jit(solution)/shard_map/ppermute | solution.py:107
  73.3 2.0 %collective-permute-done.7 = f32[8,3072]{1,0:T(8,128)S(1)} collective-permute-done((f32[8,3072]{1,0:T(8,128)S(1)}, f32[8,3072]{1,0:T(8,128)S(1)}, u32[]{:S(2)}, u32[]{:S(2)}) %collective-permute-start.7) | collective-permute-done | bytes 98336 | tf_op jit(solution)/shard_map/ppermute | solution.py:108
  75.2 1.9 %collective-permute-start.8 = (f32[8,3072]{1,0:T(8,128)S(1)}, f32[8,3072]{1,0:T(8,128)S(1)}, u32[]{:S(2)}, u32[]{:S(2)}) collective-permute-start(f32[8,3072]{1,0:T(8,128)S(1)} %convert_add_fusion.6), channel_id=1, source_target_pairs={{0,7},{1,0},{2,1},{3,2},{4,3},{5,4},{6,5},{7,6},{8,15},{9,8},{10,9... | collective-permute-start | bytes 294920 | tf_op jit(solution)/shard_map/ppermute | solution.py:108
  77.2 5.4 %collective-permute-start.2 = (f32[8,3072]{1,0:T(8,128)S(1)}, f32[8,3072]{1,0:T(8,128)S(1)}, u32[]{:S(2)}, u32[]{:S(2)}) collective-permute-start(f32[8,3072]{1,0:T(8,128)S(1)} %convert_add_fusion.12), channel_id=1, source_target_pairs={{0,1},{1,2},{2,3},{3,4},{4,5},{5,6},{6,7},{7,0},{8,9},{9,10},{10,1... | collective-permute-start | bytes 294920 | tf_op jit(solution)/shard_map/ppermute | solution.py:107
  82.6 2.4 %collective-permute-done.8 = f32[8,3072]{1,0:T(8,128)S(1)} collective-permute-done((f32[8,3072]{1,0:T(8,128)S(1)}, f32[8,3072]{1,0:T(8,128)S(1)}, u32[]{:S(2)}, u32[]{:S(2)}) %collective-permute-start.8) | collective-permute-done | bytes 98336 | tf_op jit(solution)/shard_map/ppermute | solution.py:108
  84.9 1.9 %collective-permute-start.9 = (f32[8,3072]{1,0:T(8,128)S(1)}, f32[8,3072]{1,0:T(8,128)S(1)}, u32[]{:S(2)}, u32[]{:S(2)}) collective-permute-start(f32[8,3072]{1,0:T(8,128)S(1)} %convert_add_fusion.5), channel_id=1, source_target_pairs={{0,7},{1,0},{2,1},{3,2},{4,3},{5,4},{6,5},{7,6},{8,15},{9,8},{10,9... | collective-permute-start | bytes 294920 | tf_op jit(solution)/shard_map/ppermute | solution.py:108
  86.9 5.1 %collective-permute-start.3 = (f32[8,3072]{1,0:T(8,128)S(1)}, f32[8,3072]{1,0:T(8,128)S(1)}, u32[]{:S(2)}, u32[]{:S(2)}) collective-permute-start(f32[8,3072]{1,0:T(8,128)S(1)} %convert_add_fusion.11), channel_id=1, source_target_pairs={{0,1},{1,2},{2,3},{3,4},{4,5},{5,6},{6,7},{7,0},{8,9},{9,10},{10,1... | collective-permute-start | bytes 294920 | tf_op jit(solution)/shard_map/ppermute | solution.py:107
  92.1 3.3 %collective-permute-done.9 = f32[8,3072]{1,0:T(8,128)S(1)} collective-permute-done((f32[8,3072]{1,0:T(8,128)S(1)}, f32[8,3072]{1,0:T(8,128)S(1)}, u32[]{:S(2)}, u32[]{:S(2)}) %collective-permute-start.9) | collective-permute-done | bytes 98336 | tf_op jit(solution)/shard_map/ppermute | solution.py:108
  95.3 1.9 %collective-permute-start.10 = (f32[8,3072]{1,0:T(8,128)S(1)}, f32[8,3072]{1,0:T(8,128)S(1)}, u32[]{:S(2)}, u32[]{:S(2)}) collective-permute-start(f32[8,3072]{1,0:T(8,128)S(1)} %convert_add_fusion.4), channel_id=1, source_target_pairs={{0,7},{1,0},{2,1},{3,2},{4,3},{5,4},{6,5},{7,6},{8,15},{9,8},{10,9... | collective-permute-start | bytes 294920 | tf_op jit(solution)/shard_map/ppermute | solution.py:108
  97.3 5.1 %collective-permute-start.4 = (f32[8,3072]{1,0:T(8,128)S(1)}, f32[8,3072]{1,0:T(8,128)S(1)}, u32[]{:S(2)}, u32[]{:S(2)}) collective-permute-start(f32[8,3072]{1,0:T(8,128)S(1)} %convert_add_fusion.10), channel_id=1, source_target_pairs={{0,1},{1,2},{2,3},{3,4},{4,5},{5,6},{6,7},{7,0},{8,9},{9,10},{10,1... | collective-permute-start | bytes 294920 | tf_op jit(solution)/shard_map/ppermute | solution.py:107
  102.4 1.5 %collective-permute-done.10 = f32[8,3072]{1,0:T(8,128)S(1)} collective-permute-done((f32[8,3072]{1,0:T(8,128)S(1)}, f32[8,3072]{1,0:T(8,128)S(1)}, u32[]{:S(2)}, u32[]{:S(2)}) %collective-permute-start.10) | collective-permute-done | bytes 98336 | tf_op jit(solution)/shard_map/ppermute | solution.py:108
  104.0 1.9 %collective-permute-start.11 = (f32[8,3072]{1,0:T(8,128)S(1)}, f32[8,3072]{1,0:T(8,128)S(1)}, u32[]{:S(2)}, u32[]{:S(2)}) collective-permute-start(f32[8,3072]{1,0:T(8,128)S(1)} %convert_add_fusion.3), channel_id=1, source_target_pairs={{0,7},{1,0},{2,1},{3,2},{4,3},{5,4},{6,5},{7,6},{8,15},{9,8},{10,9... | collective-permute-start | bytes 294920 | tf_op jit(solution)/shard_map/ppermute | solution.py:108
  106.0 5.1 %collective-permute-start.5 = (f32[8,3072]{1,0:T(8,128)S(1)}, f32[8,3072]{1,0:T(8,128)S(1)}, u32[]{:S(2)}, u32[]{:S(2)}) collective-permute-start(f32[8,3072]{1,0:T(8,128)S(1)} %convert_add_fusion.9), channel_id=1, source_target_pairs={{0,1},{1,2},{2,3},{3,4},{4,5},{5,6},{6,7},{7,0},{8,9},{9,10},{10,1... | collective-permute-start | bytes 294920 | tf_op jit(solution)/shard_map/ppermute | solution.py:107
  111.9 1.9 %collective-permute-start.12 = (f32[8,3072]{1,0:T(8,128)S(1)}, f32[8,3072]{1,0:T(8,128)S(1)}, u32[]{:S(2)}, u32[]{:S(2)}) collective-permute-start(f32[8,3072]{1,0:T(8,128)S(1)} %convert_add_fusion.2), channel_id=1, source_target_pairs={{0,7},{1,0},{2,1},{3,2},{4,3},{5,4},{6,5},{7,6},{8,15},{9,8},{10,9... | collective-permute-start | bytes 294920 | tf_op jit(solution)/shard_map/ppermute | solution.py:108
  113.9 5.1 %collective-permute-start.6 = (f32[8,3072]{1,0:T(8,128)S(1)}, f32[8,3072]{1,0:T(8,128)S(1)}, u32[]{:S(2)}, u32[]{:S(2)}) collective-permute-start(f32[8,3072]{1,0:T(8,128)S(1)} %convert_add_fusion.8), channel_id=1, source_target_pairs={{0,1},{1,2},{2,3},{3,4},{4,5},{5,6},{6,7},{7,0},{8,9},{9,10},{10,1... | collective-permute-start | bytes 294920 | tf_op jit(solution)/shard_map/ppermute | solution.py:107
  119.7 1.9 %collective-permute-start.13 = (f32[8,3072]{1,0:T(8,128)S(1)}, f32[8,3072]{1,0:T(8,128)S(1)}, u32[]{:S(2)}, u32[]{:S(2)}) collective-permute-start(f32[8,3072]{1,0:T(8,128)S(1)} %convert_add_fusion.1), channel_id=1, source_target_pairs={{0,7},{1,0},{2,1},{3,2},{4,3},{5,4},{6,5},{7,6},{8,15},{9,8},{10,9... | collective-permute-start | bytes 294920 | tf_op jit(solution)/shard_map/ppermute | solution.py:108
  121.6 5.8 %collective-permute-done.13 = f32[8,3072]{1,0:T(8,128)S(1)} collective-permute-done((f32[8,3072]{1,0:T(8,128)S(1)}, f32[8,3072]{1,0:T(8,128)S(1)}, u32[]{:S(2)}, u32[]{:S(2)}) %collective-permute-start.13) | collective-permute-done | bytes 98336 | tf_op jit(solution)/shard_map/ppermute | solution.py:108
  (82 shorter events, 18.5 us)
Async XLA Ops:
  7.2 25.8 %copy-start = (bf16[384,3072]{1,0:T(8,128)(2,1)S(1)}, bf16[384,3072]{1,0:T(8,128)(2,1)}, u32[]{:S(2)}) copy-start(bf16[384,3072]{1,0:T(8,128)(2,1)} %param.17) | copy-start | bytes 7077892
  7.2 18.6 %copy-start.4 = (s32[1,3]{1,0:T(1,128)S(1)}, s32[1,3]{1,0:T(1,128)}, u32[]{:S(2)}) copy-start(s32[1,3]{1,0:T(1,128)} %param.15) | copy-start | bytes 40
  7.2 20.9 %copy-start.5 = (s32[256,2]{0,1:T(2,128)S(1)}, s32[256,2]{0,1:T(2,128)}, u32[]{:S(2)}) copy-start(s32[256,2]{0,1:T(2,128)} %param.12) | copy-start | bytes 6148
  7.2 20.9 %copy-start.3 = (bf16[256,256]{1,0:T(8,128)(2,1)S(1)}, bf16[256,256]{1,0:T(8,128)(2,1)}, u32[]{:S(2)}) copy-start(bf16[256,256]{1,0:T(8,128)(2,1)} %param.14) | copy-start | bytes 393220
  7.2 21.0 %copy-start.2 = (bf16[256,384]{1,0:T(8,128)(2,1)S(1)}, bf16[256,384]{1,0:T(8,128)(2,1)}, u32[]{:S(2)}) copy-start(bf16[256,384]{1,0:T(8,128)(2,1)} %param.13) | copy-start | bytes 589828
  11.8 26.8 %all-to-all-start = ((bf16[64,4,640]{2,1,0:T(4,128)(2,1)}), bf16[64,4,640]{2,1,0:T(4,128)(2,1)S(1)}, u32[]{:S(2)}, u32[]{:S(2)}) async-start(bf16[64,4,640]{2,1,0:T(4,128)(2,1)} %reshape.271), calls=%async_computation | async-start | bytes 655360 | tf_op jit(solution)/shard_map/all_to_all | solution.py:137
  39.0 1.6 %copy-start.1 = (pred[256,512]{0,1:T(8,128)(4,1)S(1)}, pred[256,512]{0,1:T(8,128)(4,1)}, u32[]{:S(2)}) copy-start(pred[256,512]{0,1:T(8,128)(4,1)} %fusion.16) | copy-start | bytes 393220
  42.6 17.2 %all-to-all-start.1 = ((bf16[64,4,384]{2,1,0:T(4,128)(2,1)}), bf16[64,4,384]{2,1,0:T(4,128)(2,1)S(1)}, u32[]{:S(2)}, u32[]{:S(2)}) async-start(bf16[64,4,384]{2,1,0:T(4,128)(2,1)} %reshape_reshape.3), calls=%async_computation.1 | async-start | bytes 393216 | tf_op jit(solution)/shard_map/all_to_all | solution.py:145
  49.5 78.5 %reduce-scatter.2.cloned.1.call-start = ((), (), s32[]{:S(2)}) async-start(), calls=%async_computation.3 | async-start | bytes 1769472 | tf_op jit(solution)/shard_map/reduce_scatter | solution.py:141
  60.6 7.0 %collective-permute-start = (f32[8,3072]{1,0:T(8,128)S(1)}, f32[8,3072]{1,0:T(8,128)S(1)}, u32[]{:S(2)}, u32[]{:S(2)}) collective-permute-start(f32[8,3072]{1,0:T(8,128)S(1)} %bitcast_convert_fusion.1), channel_id=1, source_target_pairs={{0,1},{1,2},{2,3},{3,4},{4,5},{5,6},{6,7},{7,0},{8,9},{9,10},{10,1... | collective-permute-start | bytes 294920 | tf_op jit(solution)/shard_map/ppermute | solution.py:107
  65.4 9.9 %collective-permute-start.7 = (f32[8,3072]{1,0:T(8,128)S(1)}, f32[8,3072]{1,0:T(8,128)S(1)}, u32[]{:S(2)}, u32[]{:S(2)}) collective-permute-start(f32[8,3072]{1,0:T(8,128)S(1)} %bitcast_convert_fusion), channel_id=1, source_target_pairs={{0,7},{1,0},{2,1},{3,2},{4,3},{5,4},{6,5},{7,6},{8,15},{9,8},{10,9... | collective-permute-start | bytes 294920 | tf_op jit(solution)/shard_map/ppermute | solution.py:108
  67.7 9.5 %collective-permute-start.1 = (f32[8,3072]{1,0:T(8,128)S(1)}, f32[8,3072]{1,0:T(8,128)S(1)}, u32[]{:S(2)}, u32[]{:S(2)}) collective-permute-start(f32[8,3072]{1,0:T(8,128)S(1)} %convert_add_fusion.13), channel_id=1, source_target_pairs={{0,1},{1,2},{2,3},{3,4},{4,5},{5,6},{6,7},{7,0},{8,9},{9,10},{10,1... | collective-permute-start | bytes 294920 | tf_op jit(solution)/shard_map/ppermute | solution.py:107
  75.2 9.7 %collective-permute-start.8 = (f32[8,3072]{1,0:T(8,128)S(1)}, f32[8,3072]{1,0:T(8,128)S(1)}, u32[]{:S(2)}, u32[]{:S(2)}) collective-permute-start(f32[8,3072]{1,0:T(8,128)S(1)} %convert_add_fusion.6), channel_id=1, source_target_pairs={{0,7},{1,0},{2,1},{3,2},{4,3},{5,4},{6,5},{7,6},{8,15},{9,8},{10,9... | collective-permute-start | bytes 294920 | tf_op jit(solution)/shard_map/ppermute | solution.py:108
  77.2 9.7 %collective-permute-start.2 = (f32[8,3072]{1,0:T(8,128)S(1)}, f32[8,3072]{1,0:T(8,128)S(1)}, u32[]{:S(2)}, u32[]{:S(2)}) collective-permute-start(f32[8,3072]{1,0:T(8,128)S(1)} %convert_add_fusion.12), channel_id=1, source_target_pairs={{0,1},{1,2},{2,3},{3,4},{4,5},{5,6},{6,7},{7,0},{8,9},{9,10},{10,1... | collective-permute-start | bytes 294920 | tf_op jit(solution)/shard_map/ppermute | solution.py:107
  84.9 10.4 %collective-permute-start.9 = (f32[8,3072]{1,0:T(8,128)S(1)}, f32[8,3072]{1,0:T(8,128)S(1)}, u32[]{:S(2)}, u32[]{:S(2)}) collective-permute-start(f32[8,3072]{1,0:T(8,128)S(1)} %convert_add_fusion.5), channel_id=1, source_target_pairs={{0,7},{1,0},{2,1},{3,2},{4,3},{5,4},{6,5},{7,6},{8,15},{9,8},{10,9... | collective-permute-start | bytes 294920 | tf_op jit(solution)/shard_map/ppermute | solution.py:108
  86.9 10.3 %collective-permute-start.3 = (f32[8,3072]{1,0:T(8,128)S(1)}, f32[8,3072]{1,0:T(8,128)S(1)}, u32[]{:S(2)}, u32[]{:S(2)}) collective-permute-start(f32[8,3072]{1,0:T(8,128)S(1)} %convert_add_fusion.11), channel_id=1, source_target_pairs={{0,1},{1,2},{2,3},{3,4},{4,5},{5,6},{6,7},{7,0},{8,9},{9,10},{10,1... | collective-permute-start | bytes 294920 | tf_op jit(solution)/shard_map/ppermute | solution.py:107
  95.3 8.6 %collective-permute-start.10 = (f32[8,3072]{1,0:T(8,128)S(1)}, f32[8,3072]{1,0:T(8,128)S(1)}, u32[]{:S(2)}, u32[]{:S(2)}) collective-permute-start(f32[8,3072]{1,0:T(8,128)S(1)} %convert_add_fusion.4), channel_id=1, source_target_pairs={{0,7},{1,0},{2,1},{3,2},{4,3},{5,4},{6,5},{7,6},{8,15},{9,8},{10,9... | collective-permute-start | bytes 294920 | tf_op jit(solution)/shard_map/ppermute | solution.py:108
  97.3 8.6 %collective-permute-start.4 = (f32[8,3072]{1,0:T(8,128)S(1)}, f32[8,3072]{1,0:T(8,128)S(1)}, u32[]{:S(2)}, u32[]{:S(2)}) collective-permute-start(f32[8,3072]{1,0:T(8,128)S(1)} %convert_add_fusion.10), channel_id=1, source_target_pairs={{0,1},{1,2},{2,3},{3,4},{4,5},{5,6},{6,7},{7,0},{8,9},{9,10},{10,1... | collective-permute-start | bytes 294920 | tf_op jit(solution)/shard_map/ppermute | solution.py:107
  104.0 7.9 %collective-permute-start.11 = (f32[8,3072]{1,0:T(8,128)S(1)}, f32[8,3072]{1,0:T(8,128)S(1)}, u32[]{:S(2)}, u32[]{:S(2)}) collective-permute-start(f32[8,3072]{1,0:T(8,128)S(1)} %convert_add_fusion.3), channel_id=1, source_target_pairs={{0,7},{1,0},{2,1},{3,2},{4,3},{5,4},{6,5},{7,6},{8,15},{9,8},{10,9... | collective-permute-start | bytes 294920 | tf_op jit(solution)/shard_map/ppermute | solution.py:108
  106.0 7.9 %collective-permute-start.5 = (f32[8,3072]{1,0:T(8,128)S(1)}, f32[8,3072]{1,0:T(8,128)S(1)}, u32[]{:S(2)}, u32[]{:S(2)}) collective-permute-start(f32[8,3072]{1,0:T(8,128)S(1)} %convert_add_fusion.9), channel_id=1, source_target_pairs={{0,1},{1,2},{2,3},{3,4},{4,5},{5,6},{6,7},{7,0},{8,9},{9,10},{10,1... | collective-permute-start | bytes 294920 | tf_op jit(solution)/shard_map/ppermute | solution.py:107
  111.9 7.7 %collective-permute-start.12 = (f32[8,3072]{1,0:T(8,128)S(1)}, f32[8,3072]{1,0:T(8,128)S(1)}, u32[]{:S(2)}, u32[]{:S(2)}) collective-permute-start(f32[8,3072]{1,0:T(8,128)S(1)} %convert_add_fusion.2), channel_id=1, source_target_pairs={{0,7},{1,0},{2,1},{3,2},{4,3},{5,4},{6,5},{7,6},{8,15},{9,8},{10,9... | collective-permute-start | bytes 294920 | tf_op jit(solution)/shard_map/ppermute | solution.py:108
  113.9 7.7 %collective-permute-start.6 = (f32[8,3072]{1,0:T(8,128)S(1)}, f32[8,3072]{1,0:T(8,128)S(1)}, u32[]{:S(2)}, u32[]{:S(2)}) collective-permute-start(f32[8,3072]{1,0:T(8,128)S(1)} %convert_add_fusion.8), channel_id=1, source_target_pairs={{0,1},{1,2},{2,3},{3,4},{4,5},{5,6},{6,7},{7,0},{8,9},{9,10},{10,1... | collective-permute-start | bytes 294920 | tf_op jit(solution)/shard_map/ppermute | solution.py:107
  119.7 7.7 %collective-permute-start.13 = (f32[8,3072]{1,0:T(8,128)S(1)}, f32[8,3072]{1,0:T(8,128)S(1)}, u32[]{:S(2)}, u32[]{:S(2)}) collective-permute-start(f32[8,3072]{1,0:T(8,128)S(1)} %convert_add_fusion.1), channel_id=1, source_target_pairs={{0,7},{1,0},{2,1},{3,2},{4,3},{5,4},{6,5},{7,6},{8,15},{9,8},{10,9... | collective-permute-start | bytes 294920 | tf_op jit(solution)/shard_map/ppermute | solution.py:108
Sparse Core Ops, SparseCore 0:
  53.8 45.7 reduce-scatter.1

commit v3 on v1

--- a/solution.py
+++ b/solution.py
@@ -123,16 +123,22 @@
     replies = lax.all_to_all(
         slot_attn.reshape(groups, capacity, q_width), "req", split_axis=0, concat_axis=0, tiled=True
     )
-    pre_out, replies = lax.optimization_barrier((pre_out, replies))
     dec_attn = lax.dot_general(
         dispatch,
         replies.reshape(slot_count, q_width),
         (((0,), (0,)), ((), ())),
         preferred_element_type=jnp.float32,
     ).astype(jnp.bfloat16)
-    dec_out = lax.psum_scatter(
-        term_maker(dec_attn, wo).astype(jnp.bfloat16), "tp", scatter_dimension=0, tiled=True
+    tp_count = lax.axis_size("tp")
+    dec_part = term_maker(dec_attn, wo).astype(jnp.bfloat16)
+    pieces = lax.all_to_all(
+        dec_part.reshape(tp_count, tok_rows // tp_count, dec_part.shape[1]),
+        "tp",
+        split_axis=0,
+        concat_axis=0,
+        tiled=True,
     )
+    dec_out = jnp.sum(pieces.astype(jnp.float32), axis=0).astype(jnp.bfloat16)
     return (dec_out, pre_out)
 
 

time: 129 us -> 103 us (0.80)
  waiting for transfers between devices: 64.8 us -> 3.01 us
  blocking collectives: 17 us -> 48.1 us
  other arithmetic: 5.57 us -> 7.85 us
    reduce_scatter x1 -> x0, waiting for transfers between devices: 41.3 us -> none  [per_device(): lax.psum_scatter(term_maker(dec_attn, wo).astype(jnp.bfloat16), 'tp', sca...]
    all_to_all x0 -> x1, blocking collectives: none -> 30.7 us  [per_device(): lax.all_to_all(dec_part.reshape(tp_count, tok_rows // tp_count, dec_part....]
    reduce_scatter x1, waiting for transfers between devices: 19.6 us -> 0.01 us  [per_device(): pre_out = lax.psum_scatter(pre_part, 'tp', scatter_dimension=0, tiled=True)]
    reduce_sum x1, other arithmetic: 0.31 us -> 1.83 us  [decode_block(): row_total = jnp.sum(pool_exp, axis=-1) + self_exp]
  transfers between devices with their start and end apart: 3 -> 2, of which waited for: 3 -> 1; matrix products, arithmetic and copies ran while one was open for 8% -> 15% of each run, Pallas kernels for 0% -> 0%
where the time goes in v3:
time: 103 us; the launch traced here: 102 us
  blocking collectives  48.1 us (47%)
  between operations  15.7 us (15%)
  starting transfers between devices  14.1 us (14%)
  matrix products  8.78 us (9%)
  other arithmetic  7.85 us (8%)
  local copies, waits for them, and re-layouts  5.04 us (5%)
  waiting for transfers between devices  3.01 us (3%)
    all_to_all x1, blocking collectives, per_device(): lax.all_to_all(dec_part.reshape(tp_count, tok_rows // tp_count, dec_part....  30.7 us
    all_to_all x1, blocking collectives, per_device(): lax.all_to_all(slot_attn.reshape(groups, capacity, q_width), 'req', split...  17.3 us
    all_to_all x1, starting transfers between devices, per_device(): lax.all_to_all(send, 'req', split_axis=0, concat_axis=0, tiled=True)  14 us
    dot_general x2, matrix products, term_maker(): return jnp.dot(rows_source, wo, preferred_element_type=jnp.float32)  3.79 us
    all_to_all x1, waiting for transfers between devices, per_device(): lax.all_to_all(send, 'req', split_axis=0, concat_axis=0, tiled=True)  3 us
    unnamed x19, local copies, waits for them, and re-layouts  2.09 us
  transfers between devices with their start and end apart: 2, of which 1 were waited for; matrix products, arithmetic and copies ran while one was open for 15% of the time, Pallas kernels for 0%

profile of v3, /device:TPU:6, one launch (start us, length us, event | category | flops | bytes accessed | tf_op | source)
XLA Modules:
  0.0 102.5 jit_solution(15518226015428374698)
XLA Ops:
  7.2 0.9 fusion.27
  8.3 0.8 select_reduce_fusion
  9.1 0.7 multiply_add_fusion
  9.8 1.2 %convolution_convert_fusion.2 = bf16[256,640]{1,0:T(8,128)(2,1)S(1)} fusion(bf16[128,256]{1,0:T(8,128)(2,1)} %param.10, bf16[128,384]{1,0:T(8,128)(2,1)} %param.9, s32[128]{0:T(128)S(1)} %multiply_add_fusion), kind=kOutput, calls=%fused_computation.15 | convolution fusion | flops 42467328 | bytes 492032 | tf_op jit(solution)/shard_map/dot_general | solution.py:111
  11.0 0.8 reshape.239
  11.8 14.0 %all-to-all-start = ((bf16[64,4,640]{2,1,0:T(4,128)(2,1)}), bf16[64,4,640]{2,1,0:T(4,128)(2,1)S(1)}, u32[]{:S(2)}, u32[]{:S(2)}) async-start(bf16[64,4,640]{2,1,0:T(4,128)(2,1)} %reshape.239), calls=%async_computation | async-start | bytes 655360 | tf_op jit(solution)/shard_map/all_to_all | solution.py:115
  25.9 0.7 fusion.36
  27.9 0.7 fusion.28
  28.9 1.1 %copy.35 = bf16[512,256]{0,1:T(8,128)(2,1)S(1)} copy(bf16[512,256]{1,0:T(8,128)(2,1)} %param.16) | data formatting | bytes 524288 | tf_op args[7]
  30.3 0.4 bitcast_reduce_fusion
  31.2 0.5 fusion.12
  31.7 0.8 fusion.16
  32.5 0.6 iota_compare_fusion.10
  33.5 2.2 %convolution_convert_fusion = bf16[256,3072]{1,0:T(8,128)(2,1)} fusion(bf16[256,384]{0,1:T(8,128)(2,1)S(1)} %bitcast.134, bf16[384,3072]{1,0:T(8,128)(2,1)S(1)} %copy-done), kind=kOutput, calls=%fused_computation | convolution fusion | flops 604766208 | bytes 4128768 | tf_op jit(solution)/shard_map/dot_general | solution.py:87
  35.7 3.0 %all-to-all-done = bf16[64,4,640]{2,1,0:T(4,128)(2,1)S(1)} async-done(((bf16[64,4,640]{2,1,0:T(4,128)(2,1)}), bf16[64,4,640]{2,1,0:T(4,128)(2,1)S(1)}, u32[]{:S(2)}, u32[]{:S(2)}) %all-to-all-start) | async-done | bytes 327712 | tf_op jit(solution)/shard_map/all_to_all | solution.py:115
  38.7 0.7 slice.53
  39.6 0.7 copy-done.2
  40.5 1.6 %fusion.38 = (f32[256,3]{0,1:T(4,128)S(1)}, f32[256,1,3,512]{0,3,2,1:T(8,128)}) fusion(bf16[256,3,128]{0,2,1:T(8,128)(2,1)S(1)} %bitcast.125, bf16[512,1,2,128]{0,3,2,1:T(8,128)(2,1)S(1)} %bitcast.129, pred[256,512]{0,1:T(8,128)(4,1)S(1)} %copy-done.3), kind=kOutput, calls=%fused_computation.74 | convolution fusion | flops 101842176 | bytes 2034688 | tf_op jit(solution)/shard_map/sghd,pgd->sghp/dot_general | solution.py:23
  42.2 1.8 %fusion.3 = f32[256,3]{0,1:T(4,128)S(1)} fusion(f32[256,1,3,512]{0,3,2,1:T(8,128)} %get-tuple-element.20, f32[256,3]{0,1:T(4,128)S(1)} %multiply_maximum_fusion, pred[256,512]{0,1:T(8,128)(4,1)S(1)} %copy-done.3), kind=kLoop, calls=%fused_computation.13 | loop fusion | flops 1178880 | bytes 1710080 | tf_op jit(solution)/shard_map/reduce_sum | solution.py:36
  44.1 0.7 fusion.10
  45.1 17.3 %all_to_all.15 = bf16[64,4,384]{2,1,0:T(4,128)(2,1)S(1)} all-to-all(bf16[64,4,384]{2,1,0:T(4,128)(2,1)S(1)} %reshape_reshape.3), channel_id=1, replica_groups=mesh['req'=64,'tp'=8] {'req'}, dimensions={0} | all-to-all | bytes 393216 | tf_op jit(solution)/shard_map/all_to_all | solution.py:123
  62.5 1.6 %convolution_convert_fusion.1 = bf16[128,3072]{1,0:T(8,128)(2,1)} fusion(bf16[384,3072]{1,0:T(8,128)(2,1)S(1)} %copy-done, bf16[256,384]{1,0:T(8,128)(2,1)S(1)} %reshape.245, s32[128]{0:T(128)S(1)} %multiply_add_fusion), kind=kOutput, calls=%fused_computation.1 | convolution fusion | flops 327630848 | bytes 3342848 | tf_op jit(solution)/shard_map/dot_general | solution.py:87
  64.1 30.7 %all_to_all.16 = bf16[8,16,3072]{2,1,0:T(8,128)(2,1)S(1)} all-to-all(bf16[8,16,3072]{2,1,0:T(8,128)(2,1)} %bitcast.122), channel_id=1, replica_groups=mesh['req'=64,'tp'=8] {'tp'}, dimensions={0} | all-to-all | bytes 1572864 | tf_op jit(solution)/shard_map/all_to_all | solution.py:134
  94.9 0.8 reduce_sum.52
  (41 shorter events, 2.6 us)
Async XLA Ops:
  7.2 26.3 %copy-start = (bf16[384,3072]{1,0:T(8,128)(2,1)S(1)}, bf16[384,3072]{1,0:T(8,128)(2,1)}, u32[]{:S(2)}) copy-start(bf16[384,3072]{1,0:T(8,128)(2,1)} %param.17) | copy-start | bytes 7077892
  7.2 18.7 %copy-start.6 = (s32[1,3]{1,0:T(1,128)S(1)}, s32[1,3]{1,0:T(1,128)}, u32[]{:S(2)}) copy-start(s32[1,3]{1,0:T(1,128)} %param.15) | copy-start | bytes 40
  7.2 21.4 %copy-start.7 = (s32[256,2]{0,1:T(2,128)S(1)}, s32[256,2]{0,1:T(2,128)}, u32[]{:S(2)}) copy-start(s32[256,2]{0,1:T(2,128)} %param.12) | copy-start | bytes 6148
  7.2 21.4 %copy-start.5 = (bf16[256,256]{1,0:T(8,128)(2,1)S(1)}, bf16[256,256]{1,0:T(8,128)(2,1)}, u32[]{:S(2)}) copy-start(bf16[256,256]{1,0:T(8,128)(2,1)} %param.14) | copy-start | bytes 393220
  7.2 21.5 %copy-start.4 = (bf16[256,384]{1,0:T(8,128)(2,1)S(1)}, bf16[256,384]{1,0:T(8,128)(2,1)}, u32[]{:S(2)}) copy-start(bf16[256,384]{1,0:T(8,128)(2,1)} %param.13) | copy-start | bytes 589828
  11.8 26.9 %all-to-all-start = ((bf16[64,4,640]{2,1,0:T(4,128)(2,1)}), bf16[64,4,640]{2,1,0:T(4,128)(2,1)S(1)}, u32[]{:S(2)}, u32[]{:S(2)}) async-start(bf16[64,4,640]{2,1,0:T(4,128)(2,1)} %reshape.239), calls=%async_computation | async-start | bytes 655360 | tf_op jit(solution)/shard_map/all_to_all | solution.py:115
  25.8 69.9 %reduce-scatter.2.cloned.1.call-start = ((), (), s32[]{:S(2)}) async-start(), calls=%async_computation.4 | async-start | bytes 1769472 | tf_op jit(solution)/shard_map/reduce_scatter | solution.py:119
  39.4 0.9 copy-start.2
  39.4 1.0 %copy-start.3 = (pred[256,512]{0,1:T(8,128)(4,1)S(1)}, pred[256,512]{0,1:T(8,128)(4,1)}, u32[]{:S(2)}) copy-start(pred[256,512]{0,1:T(8,128)(4,1)} %fusion.16) | copy-start | bytes 393220
  42.2 1.9 %copy-start.1 = (f32[256,1,3,512]{0,3,2,1:T(8,128)S(1)}, f32[256,1,3,512]{0,3,2,1:T(8,128)}, u32[]{:S(2)}) copy-start(f32[256,1,3,512]{0,3,2,1:T(8,128)} %get-tuple-element.20) | copy-start | bytes 4718596
Sparse Core Ops, SparseCore 0:
  39.6 45.6 reduce-scatter.1

commit v4 on v3

--- a/solution.py
+++ b/solution.py
@@ -102,9 +102,9 @@
     pre_attn = prefill_attend(pre_q, pre_kv, pre_meta[0], pool_keys, pool_vals, kv_heads)
     pre_part = term_maker(pre_attn, wo).astype(jnp.bfloat16)
 
-    group_iota = lax.iota(jnp.int32, groups)
-    hot_table = (dec_owner[:, None] == group_iota[None, :]).astype(jnp.int32)
-    ranking = jnp.sum((jnp.cumsum(hot_table, axis=0) - hot_table) * hot_table, axis=1)
+    tok_iota = lax.iota(jnp.int32, tok_rows)
+    earlier_same = (dec_owner[:, None] == dec_owner[None, :]) & (tok_iota[None, :] < tok_iota[:, None])
+    ranking = jnp.sum(earlier_same.astype(jnp.int32), axis=1)
     slot_ids = dec_owner * capacity + ranking
     dispatch = (slot_ids[None, :] == lax.iota(jnp.int32, slot_count)[:, None]).astype(jnp.bfloat16)
     send = (

time: 103 us -> 102 us (level)
  no operation moved by 1% of the time
where the time goes in v4:
time: 102 us
  blocking collectives  48.2 us (47%)
  between operations  15.7 us (15%)
  starting transfers between devices  14.1 us (14%)
  matrix products  8.77 us (9%)
  other arithmetic  6.95 us (7%)
  local copies, waits for them, and re-layouts  5.04 us (5%)
  waiting for transfers between devices  3.02 us (3%)
    all_to_all x1, blocking collectives, per_device(): lax.all_to_all(dec_part.reshape(tp_count, tok_rows // tp_count, dec_part....  30.8 us
    all_to_all x1, blocking collectives, per_device(): lax.all_to_all(slot_attn.reshape(groups, capacity, q_width), 'req', split...  17.3 us
    all_to_all x1, starting transfers between devices, per_device(): lax.all_to_all(send, 'req', split_axis=0, concat_axis=0, tiled=True)  14 us
    dot_general x2, matrix products, term_maker(): return jnp.dot(rows_source, wo, preferred_element_type=jnp.float32)  3.79 us
    all_to_all x1, waiting for transfers between devices, per_device(): lax.all_to_all(send, 'req', split_axis=0, concat_axis=0, tiled=True)  3.01 us
    unnamed x19, local copies, waits for them, and re-layouts  2.09 us
  transfers between devices with their start and end apart: 2, of which 1 were waited for; matrix products, arithmetic and copies ran while one was open for 15% of the time, Pallas kernels for 0%

profile of v4, /device:TPU:6, one launch (start us, length us, event | category | flops | bytes accessed | tf_op | source)
XLA Modules:
  0.0 101.7 jit_solution(1344021074509425432)
XLA Ops:
  7.2 1.0 convert_reduce_fusion
  8.2 0.7 multiply_add_fusion
  8.9 1.2 %convolution_convert_fusion.2 = bf16[256,640]{1,0:T(8,128)(2,1)S(1)} fusion(bf16[128,256]{1,0:T(8,128)(2,1)} %param.10, bf16[128,384]{1,0:T(8,128)(2,1)} %param.9, s32[128]{0:T(128)S(1)} %multiply_add_fusion), kind=kOutput, calls=%fused_computation.15 | convolution fusion | flops 42467328 | bytes 492032 | tf_op jit(solution)/shard_map/dot_general | solution.py:111
  10.1 0.8 reshape.240
  10.9 14.0 %all-to-all-start = ((bf16[64,4,640]{2,1,0:T(4,128)(2,1)}), bf16[64,4,640]{2,1,0:T(4,128)(2,1)S(1)}, u32[]{:S(2)}, u32[]{:S(2)}) async-start(bf16[64,4,640]{2,1,0:T(4,128)(2,1)} %reshape.240), calls=%async_computation | async-start | bytes 655360 | tf_op jit(solution)/shard_map/all_to_all | solution.py:115
  25.0 0.7 fusion.36
  27.0 0.7 fusion.28
  28.0 1.1 %copy.52 = bf16[512,256]{0,1:T(8,128)(2,1)S(1)} copy(bf16[512,256]{1,0:T(8,128)(2,1)} %param.16) | data formatting | bytes 524288 | tf_op args[7]
  29.4 0.4 bitcast_reduce_fusion
  30.3 0.5 fusion.12
  30.8 0.8 fusion.16
  31.6 0.6 iota_compare_fusion.10
  32.2 0.3 fusion.9
  32.6 2.2 %convolution_convert_fusion = bf16[256,3072]{1,0:T(8,128)(2,1)} fusion(bf16[256,384]{0,1:T(8,128)(2,1)S(1)} %bitcast.134, bf16[384,3072]{1,0:T(8,128)(2,1)S(1)} %copy-done), kind=kOutput, calls=%fused_computation | convolution fusion | flops 604766208 | bytes 4128768 | tf_op jit(solution)/shard_map/dot_general | solution.py:87
  34.7 3.0 %all-to-all-done = bf16[64,4,640]{2,1,0:T(4,128)(2,1)S(1)} async-done(((bf16[64,4,640]{2,1,0:T(4,128)(2,1)}), bf16[64,4,640]{2,1,0:T(4,128)(2,1)S(1)}, u32[]{:S(2)}, u32[]{:S(2)}) %all-to-all-start) | async-done | bytes 327712 | tf_op jit(solution)/shard_map/all_to_all | solution.py:115
  37.8 0.7 slice.53
  38.7 0.7 copy-done.2
  39.6 1.6 %fusion.38 = (f32[256,3]{0,1:T(4,128)S(1)}, f32[256,1,3,512]{0,3,2,1:T(8,128)}) fusion(bf16[256,3,128]{0,2,1:T(8,128)(2,1)S(1)} %bitcast.125, bf16[512,1,2,128]{0,3,2,1:T(8,128)(2,1)S(1)} %bitcast.129, pred[256,512]{0,1:T(8,128)(4,1)S(1)} %copy-done.3), kind=kOutput, calls=%fused_computation.74 | convolution fusion | flops 101842176 | bytes 2034688 | tf_op jit(solution)/shard_map/sghd,pgd->sghp/dot_general | solution.py:23
  41.3 1.8 %fusion.3 = f32[256,3]{0,1:T(4,128)S(1)} fusion(f32[256,1,3,512]{0,3,2,1:T(8,128)} %get-tuple-element.20, f32[256,3]{0,1:T(4,128)S(1)} %multiply_maximum_fusion, pred[256,512]{0,1:T(8,128)(4,1)S(1)} %copy-done.3), kind=kLoop, calls=%fused_computation.13 | loop fusion | flops 1178880 | bytes 1710080 | tf_op jit(solution)/shard_map/reduce_sum | solution.py:36
  43.2 0.7 fusion.10
  44.2 17.3 %all_to_all.15 = bf16[64,4,384]{2,1,0:T(4,128)(2,1)S(1)} all-to-all(bf16[64,4,384]{2,1,0:T(4,128)(2,1)S(1)} %reshape_reshape.3), channel_id=1, replica_groups=mesh['req'=64,'tp'=8] {'req'}, dimensions={0} | all-to-all | bytes 393216 | tf_op jit(solution)/shard_map/all_to_all | solution.py:123
  61.6 1.6 %convolution_convert_fusion.1 = bf16[128,3072]{1,0:T(8,128)(2,1)} fusion(bf16[384,3072]{1,0:T(8,128)(2,1)S(1)} %copy-done, bf16[256,384]{1,0:T(8,128)(2,1)S(1)} %reshape.246, s32[128]{0:T(128)S(1)} %multiply_add_fusion), kind=kOutput, calls=%fused_computation.1 | convolution fusion | flops 327630848 | bytes 3342848 | tf_op jit(solution)/shard_map/dot_general | solution.py:87
  63.2 30.8 %all_to_all.16 = bf16[8,16,3072]{2,1,0:T(8,128)(2,1)S(1)} all-to-all(bf16[8,16,3072]{2,1,0:T(8,128)(2,1)} %bitcast.122), channel_id=1, replica_groups=mesh['req'=64,'tp'=8] {'tp'}, dimensions={0} | all-to-all | bytes 1572864 | tf_op jit(solution)/shard_map/all_to_all | solution.py:134
  94.1 0.8 reduce_sum.52
  (39 shorter events, 2.1 us)
Async XLA Ops:
  7.2 25.4 %copy-start = (bf16[384,3072]{1,0:T(8,128)(2,1)S(1)}, bf16[384,3072]{1,0:T(8,128)(2,1)}, u32[]{:S(2)}) copy-start(bf16[384,3072]{1,0:T(8,128)(2,1)} %param.17) | copy-start | bytes 7077892
  7.2 17.8 %copy-start.6 = (s32[1,3]{1,0:T(1,128)S(1)}, s32[1,3]{1,0:T(1,128)}, u32[]{:S(2)}) copy-start(s32[1,3]{1,0:T(1,128)} %param.15) | copy-start | bytes 40
  7.2 20.5 %copy-start.7 = (s32[256,2]{0,1:T(2,128)S(1)}, s32[256,2]{0,1:T(2,128)}, u32[]{:S(2)}) copy-start(s32[256,2]{0,1:T(2,128)} %param.12) | copy-start | bytes 6148
  7.2 20.5 %copy-start.5 = (bf16[256,256]{1,0:T(8,128)(2,1)S(1)}, bf16[256,256]{1,0:T(8,128)(2,1)}, u32[]{:S(2)}) copy-start(bf16[256,256]{1,0:T(8,128)(2,1)} %param.14) | copy-start | bytes 393220
  7.2 20.6 %copy-start.4 = (bf16[256,384]{1,0:T(8,128)(2,1)S(1)}, bf16[256,384]{1,0:T(8,128)(2,1)}, u32[]{:S(2)}) copy-start(bf16[256,384]{1,0:T(8,128)(2,1)} %param.13) | copy-start | bytes 589828
  10.9 26.9 %all-to-all-start = ((bf16[64,4,640]{2,1,0:T(4,128)(2,1)}), bf16[64,4,640]{2,1,0:T(4,128)(2,1)S(1)}, u32[]{:S(2)}, u32[]{:S(2)}) async-start(bf16[64,4,640]{2,1,0:T(4,128)(2,1)} %reshape.240), calls=%async_computation | async-start | bytes 655360 | tf_op jit(solution)/shard_map/all_to_all | solution.py:115
  24.9 69.9 %reduce-scatter.2.cloned.1.call-start = ((), (), s32[]{:S(2)}) async-start(), calls=%async_computation.4 | async-start | bytes 1769472 | tf_op jit(solution)/shard_map/reduce_scatter | solution.py:119
  38.5 0.9 copy-start.2
  38.5 1.0 %copy-start.3 = (pred[256,512]{0,1:T(8,128)(4,1)S(1)}, pred[256,512]{0,1:T(8,128)(4,1)}, u32[]{:S(2)}) copy-start(pred[256,512]{0,1:T(8,128)(4,1)} %fusion.16) | copy-start | bytes 393220
  41.3 1.9 %copy-start.1 = (f32[256,1,3,512]{0,3,2,1:T(8,128)S(1)}, f32[256,1,3,512]{0,3,2,1:T(8,128)}, u32[]{:S(2)}) copy-start(f32[256,1,3,512]{0,3,2,1:T(8,128)} %get-tuple-element.20) | copy-start | bytes 4718596
Sparse Core Ops, SparseCore 0:
  38.7 45.7 reduce-scatter.1

commit v5 on v4

v5 whole, which is shorter than its diff:
```python
import math

import jax
import jax.numpy as jnp
from jax import lax
from jax.experimental import pallas as pl
from jax.experimental.pallas import tpu as pltpu
from jax.sharding import PartitionSpec as P

HD = 128
QPK = 3


MASKED_SCORE = -1e30


def decode_kernel(recv_ref, table_ref, pool_ref, out_ref):
    score_scale = 1.0 / math.sqrt(HD)
    slot_rows = recv_ref.shape[0]
    kv_heads = pool_ref.shape[1] // (2 * HD)
    q_width = kv_heads * QPK * HD
    table = table_ref[...]
    begins = table[:, 0:1]
    ends = begins + table[:, 1:2]
    places = lax.broadcasted_iota(jnp.int32, (slot_rows, pool_ref.shape[0]), 1)
    visible = (places >= begins) & (places < ends)
    for g in range(kv_heads):
        keys = pool_ref[:, g * 2 * HD : g * 2 * HD + HD]
        vals = pool_ref[:, g * 2 * HD + HD : (g + 1) * 2 * HD]
        own_key = recv_ref[:, q_width + g * 2 * HD : q_width + g * 2 * HD + HD].astype(jnp.float32)
        own_val = recv_ref[:, q_width + g * 2 * HD + HD : q_width + (g + 1) * 2 * HD].astype(jnp.float32)
        for h in range(QPK):
            col = (g * QPK + h) * HD
            q = recv_ref[:, col : col + HD]
            scores = lax.dot_general(
                q, keys, (((1,), (1,)), ((), ())), preferred_element_type=jnp.float32
            ) * score_scale
            scores = jnp.where(visible, scores, MASKED_SCORE)
            own = jnp.sum(q.astype(jnp.float32) * own_key, axis=1, keepdims=True) * score_scale
            peak = jnp.maximum(jnp.max(scores, axis=1, keepdims=True), own)
            weights = jnp.where(visible, jnp.exp(scores - peak), 0.0)
            own_exp = jnp.exp(own - peak)
            total = jnp.sum(weights, axis=1, keepdims=True) + own_exp
            weights = (weights / total).astype(jnp.bfloat16)
            own_weight = (own_exp / total).astype(jnp.bfloat16).astype(jnp.float32)
            mixed = jnp.dot(weights, vals, preferred_element_type=jnp.float32) + own_weight * own_val
            out_ref[:, col : col + HD] = mixed.astype(jnp.bfloat16)


def prefill_kernel(q_ref, kv_ref, meta_ref, pool_ref, out_ref):
    score_scale = 1.0 / math.sqrt(HD)
    span_rows = q_ref.shape[0]
    pool_len = pool_ref.shape[0]
    kv_heads = pool_ref.shape[1] // (2 * HD)
    meta = meta_ref[...]
    begin = meta[:, 0:1]
    end = begin + meta[:, 1:2]
    places = lax.broadcasted_iota(jnp.int32, (span_rows, pool_len), 1)
    visible = (places >= begin) & (places < end)
    row_iota = lax.broadcasted_iota(jnp.int32, (span_rows, span_rows), 0)
    col_iota = lax.broadcasted_iota(jnp.int32, (span_rows, span_rows), 1)
    causal = col_iota <= row_iota
    live = lax.broadcasted_iota(jnp.int32, (span_rows, 1), 0) < meta[:, 2:3]
    for g in range(kv_heads):
        keys = pool_ref[:, g * 2 * HD : g * 2 * HD + HD]
        vals = pool_ref[:, g * 2 * HD + HD : (g + 1) * 2 * HD]
        span_keys = kv_ref[:, g * 2 * HD : g * 2 * HD + HD]
        span_vals = kv_ref[:, g * 2 * HD + HD : (g + 1) * 2 * HD]
        for h in range(QPK):
            col = (g * QPK + h) * HD
            q = q_ref[:, col : col + HD]
            dims = (((1,), (1,)), ((), ()))
            pool_scores = lax.dot_general(q, keys, dims, preferred_element_type=jnp.float32) * score_scale
            pool_scores = jnp.where(visible, pool_scores, MASKED_SCORE)
            span_scores = lax.dot_general(q, span_keys, dims, preferred_element_type=jnp.float32) * score_scale
            span_scores = jnp.where(causal, span_scores, MASKED_SCORE)
            peak = jnp.maximum(
                jnp.max(pool_scores, axis=1, keepdims=True), jnp.max(span_scores, axis=1, keepdims=True)
            )
            pool_exp = jnp.where(visible, jnp.exp(pool_scores - peak), 0.0)
            span_exp = jnp.where(causal, jnp.exp(span_scores - peak), 0.0)
            total = jnp.sum(pool_exp, axis=1, keepdims=True) + jnp.sum(span_exp, axis=1, keepdims=True)
            pool_weight = (pool_exp / total).astype(jnp.bfloat16)
            span_weight = (span_exp / total).astype(jnp.bfloat16)
            mixed = jnp.dot(pool_weight, vals, preferred_element_type=jnp.float32) + jnp.dot(
                span_weight, span_vals, preferred_element_type=jnp.float32
            )
            out_ref[:, col : col + HD] = jnp.where(live, mixed, 0.0).astype(jnp.bfloat16)


def vmem_call(kernel, out_shape, operands, flops, transcendentals):
    bytes_accessed = sum(x.size * x.dtype.itemsize for x in operands) + out_shape.size * 2
    return pl.pallas_call(
        kernel,
        out_shape=out_shape,
        in_specs=[pl.BlockSpec(memory_space=pltpu.VMEM)] * len(operands),
        out_specs=pl.BlockSpec(memory_space=pltpu.VMEM),
        cost_estimate=pl.CostEstimate(
            flops=flops, transcendentals=transcendentals, bytes_accessed=bytes_accessed
        ),
    )(*operands)


def term_maker(rows_source, wo):
    return jnp.dot(rows_source, wo, preferred_element_type=jnp.float32)


def per_device(dec_q, dec_kv, dec_owner, dec_table, pre_q, pre_kv, pre_meta, pool, wo):
    groups = lax.axis_size("req")
    tok_rows = dec_q.shape[0]
    capacity = max(2, (2 * tok_rows + groups - 1) // groups)
    slot_count = groups * capacity
    q_width = dec_q.shape[1]
    kv_width = dec_kv.shape[1]

    span_rows = pre_q.shape[0]
    pre_attn = vmem_call(
        prefill_kernel,
        jax.ShapeDtypeStruct((span_rows, q_width), jnp.bfloat16),
        (pre_q, pre_kv, pre_meta, pool),
        4 * span_rows * (pool.shape[0] + span_rows) * q_width,
        span_rows * (pool.shape[0] + span_rows) * q_width // HD,
    )
    pre_part = term_maker(pre_attn, wo).astype(jnp.bfloat16)

    tok_iota = lax.iota(jnp.int32, tok_rows)
    earlier_same = (dec_owner[:, None] == dec_owner[None, :]) & (tok_iota[None, :] < tok_iota[:, None])
    ranking = jnp.sum(earlier_same.astype(jnp.int32), axis=1)
    slot_ids = dec_owner * capacity + ranking
    dispatch = (slot_ids[None, :] == lax.iota(jnp.int32, slot_count)[:, None]).astype(jnp.bfloat16)
    send = (
        jnp.dot(dispatch, jnp.concatenate([dec_q, dec_kv], axis=1), preferred_element_type=jnp.float32)
        .astype(jnp.bfloat16)
        .reshape(groups, capacity, q_width + kv_width)
    )
    recv = lax.all_to_all(send, "req", split_axis=0, concat_axis=0, tiled=True).reshape(
        slot_count, q_width + kv_width
    )
    pre_part, recv = lax.optimization_barrier((pre_part, recv))
    pre_out = lax.psum_scatter(pre_part, "tp", scatter_dimension=0, tiled=True)
    slot_attn = vmem_call(
        decode_kernel,
        jax.ShapeDtypeStruct((slot_count, q_width), jnp.bfloat16),
        (recv, dec_table, pool),
        4 * slot_count * pool.shape[0] * q_width,
        slot_count * pool.shape[0] * q_width // HD,
    )
    replies = lax.all_to_all(
        slot_attn.reshape(groups, capacity, q_width), "req", split_axis=0, concat_axis=0, tiled=True
    )
    dec_attn = lax.dot_general(
        dispatch,
        replies.reshape(slot_count, q_width),
        (((0,), (0,)), ((), ())),
        preferred_element_type=jnp.float32,
    ).astype(jnp.bfloat16)
    tp_count = lax.axis_size("tp")
    dec_part = term_maker(dec_attn, wo).astype(jnp.bfloat16)
    pieces = lax.all_to_all(
        dec_part.reshape(tp_count, tok_rows // tp_count, dec_part.shape[1]),
        "tp",
        split_axis=0,
        concat_axis=0,
        tiled=True,
    )
    dec_out = jnp.sum(pieces.astype(jnp.float32), axis=0).astype(jnp.bfloat16)
    return (dec_out, pre_out)


def solution(mesh):
    placed = (
        P("req", "tp"),
        P("req", "tp"),
        P("req"),
        P("req", None),
        P("req", "tp"),
        P("req", "tp"),
        P("req", None),
        P("req", "tp"),
        P("tp", None),
    )
    return jax.shard_map(
        per_device,
        mesh=mesh,
        in_specs=placed,
        out_specs=(P(("req", "tp"), None), P(("req", "tp"), None)),
        check_vma=False,
    )
```

time: 102 us -> 101 us (level)
  Pallas kernels: 0 us -> 6.97 us
  other arithmetic: 6.95 us -> 2.41 us
  waiting for transfers between devices: 3.02 us -> 6.19 us
  matrix products: 8.77 us -> 5.87 us
  between operations: 15.7 us -> 14.1 us
  local copies, waits for them, and re-layouts: 5.04 us -> 3.45 us
  blocking collectives: 48.2 us -> 47 us
    pallas_call x0 -> x2, Pallas kernels: none -> 6.97 us  [vmem_call(): pl.pallas_call(kernel, out_shape=out_shape, in_specs=[pl.BlockSpec(memory...]
    dot_general x6 -> x0, matrix products: 3.82 us -> none  [the longest x1 1.59 us: decode_block(): jnp.einsum('sghd,pgd->sghp', q_block, pool_keys, preferred_element_type=j...]
    all_to_all x1, waiting for transfers between devices: 3.01 us -> 6.17 us  [per_device(): lax.all_to_all(send, 'req', split_axis=0, concat_axis=0, tiled=True)]
    reduce_sum x3 -> x0, other arithmetic: 2.29 us -> none  [the longest x1 1.83 us: decode_block(): row_total = jnp.sum(pool_exp, axis=-1) + self_exp]
    slice x5 -> x0, local copies, waits for them, and re-layouts: 1.58 us -> none  [the longest x2 0.75 us: per_device(): kv_slots = recv[:, q_width:].reshape(slot_count, kv_heads, 2, HD)]
    and x2 -> x0, other arithmetic: 1.46 us -> none  [the longest x1 0.77 us: decode_block(): (places[None, :] >= begins) & (places[None, :] < begins + windows[:, 1:2])]
    unnamed x19 -> x5, local copies, waits for them, and re-layouts: 2.09 us -> 0.81 us
  transfers between devices with their start and end apart: 2 -> 2, of which waited for: 1 -> 1; matrix products, arithmetic and copies ran while one was open for 15% -> 7% of each run, Pallas kernels for 0% -> 7%
where the time goes in v5:
time: 101 us; the launch traced here: 100 us
  blocking collectives  47 us (47%)
  starting transfers between devices  14.1 us (14%)
  between operations  14.1 us (14%)
  Pallas kernels  6.97 us (7%)
  waiting for transfers between devices  6.19 us (6%)
  matrix products  5.87 us (6%)
  local copies, waits for them, and re-layouts  3.45 us (3%)
  other arithmetic  2.41 us (2%)
    all_to_all x1, blocking collectives, per_device(): lax.all_to_all(dec_part.reshape(tp_count, tok_rows // tp_count, dec_part....  30.5 us
    all_to_all x1, blocking collectives, per_device(): lax.all_to_all(slot_attn.reshape(groups, capacity, q_width), 'req', split...  16.5 us
    all_to_all x1, starting transfers between devices, per_device(): lax.all_to_all(send, 'req', split_axis=0, concat_axis=0, tiled=True)  14 us
    pallas_call x2, Pallas kernels, vmem_call(): pl.pallas_call(kernel, out_shape=out_shape, in_specs=[pl.BlockSpec(memory...  6.97 us
    all_to_all x1, waiting for transfers between devices, per_device(): lax.all_to_all(send, 'req', split_axis=0, concat_axis=0, tiled=True)  6.17 us
    dot_general x2, matrix products, term_maker(): return jnp.dot(rows_source, wo, preferred_element_type=jnp.float32)  4.71 us
  transfers between devices with their start and end apart: 2, of which 1 were waited for; matrix products, arithmetic and copies ran while one was open for 7% of the time, Pallas kernels for 7%

profile of v5, /device:TPU:6, one launch (start us, length us, event | category | flops | bytes accessed | tf_op | source)
XLA Modules:
  0.0 100.1 jit_solution(15931481508692855306)
XLA Ops:
  7.2 0.0 copy-start
  7.2 1.0 convert_reduce_fusion
  8.2 0.7 multiply_add_fusion
  8.8 1.2 %convolution_convert_fusion.2 = bf16[256,640]{1,0:T(8,128)(2,1)S(1)} fusion(bf16[128,256]{1,0:T(8,128)(2,1)} %param.10, bf16[128,384]{1,0:T(8,128)(2,1)} %param.9, s32[128]{0:T(128)S(1)} %multiply_add_fusion), kind=kOutput, calls=%fused_computation.2 | convolution fusion | flops 42467328 | bytes 492032 | tf_op jit(solution)/shard_map/dot_general | solution.py:132
  10.0 0.8 reshape.22
  10.8 14.0 %all-to-all-start = ((bf16[64,4,640]{2,1,0:T(4,128)(2,1)}), bf16[64,4,640]{2,1,0:T(4,128)(2,1)S(1)}, u32[]{:S(2)}, u32[]{:S(2)}) async-start(bf16[64,4,640]{2,1,0:T(4,128)(2,1)} %reshape.22), calls=%async_computation | async-start | bytes 655360 | tf_op jit(solution)/shard_map/all_to_all | solution.py:136
  24.8 0.0 reduce-scatter.2.cloned.1.call-start
  24.9 3.6 %shard_map.104 = bf16[256,384]{1,0:T(8,128)(2,1)} custom-call(bf16[256,384]{1,0:T(8,128)(2,1)} %q_ref.1, bf16[256,256]{1,0:T(8,128)(2,1)} %kv_ref.1, s32[1,3]{1,0:T(1,128)} %meta_ref.1, bf16[512,256]{1,0:T(8,128)(2,1)} %pool_ref.3), custom_call_target="tpu_custom_call" | custom-call | flops 301989888 | bytes 786444 | tf_op jit(solution)/shard_map/pallas_call | solution.py:93
  28.5 0.0 copy-done
  28.5 0.0 copy-start.1
  28.5 3.1 %convolution_convert_fusion = bf16[256,3072]{1,0:T(8,128)(2,1)} fusion(bf16[256,384]{1,0:T(8,128)(2,1)} %shard_map.104, bf16[384,3072]{1,0:T(8,128)(2,1)S(1)} %copy-done), kind=kOutput, calls=%fused_computation | convolution fusion | flops 604766208 | bytes 4128768 | tf_op jit(solution)/shard_map/dot_general | solution.py:105
  31.5 6.2 %all-to-all-done = bf16[64,4,640]{2,1,0:T(4,128)(2,1)S(1)} async-done(((bf16[64,4,640]{2,1,0:T(4,128)(2,1)}), bf16[64,4,640]{2,1,0:T(4,128)(2,1)S(1)}, u32[]{:S(2)}, u32[]{:S(2)}) %all-to-all-start) | async-done | bytes 327712 | tf_op jit(solution)/shard_map/all_to_all | solution.py:136
  37.7 0.8 reshape.23.recv_ref
  38.5 0.0 reduce-scatter.2.cloned.1.call-update
  38.5 0.0 copy-done.1
  38.5 0.8 copy.12.table_ref
  39.3 3.4 %shard_map.105 = bf16[256,384]{1,0:T(8,128)(2,1)} custom-call(bf16[256,640]{1,0:T(8,128)(2,1)} %reshape.23.recv_ref, s32[256,2]{1,0:T(8,128)} %copy.12.table_ref, bf16[512,256]{1,0:T(8,128)(2,1)} %pool_ref.3), custom_call_target="tpu_custom_call" | custom-call | flops 201326592 | bytes 788480 | tf_op jit(solution)/shard_map/pallas_call | solution.py:93
  42.8 1.0 reshape.24
  43.7 16.5 %all_to_all.15 = bf16[64,4,384]{2,1,0:T(4,128)(2,1)S(1)} all-to-all(bf16[64,4,384]{2,1,0:T(4,128)(2,1)S(1)} %reshape.24), channel_id=1, replica_groups=mesh['req'=64,'tp'=8] {'req'}, dimensions={0} | all-to-all | bytes 393216 | tf_op jit(solution)/shard_map/all_to_all | solution.py:148
  60.3 0.1 reshape.25
  60.3 1.6 %convolution_convert_fusion.1 = bf16[128,3072]{1,0:T(8,128)(2,1)} fusion(bf16[384,3072]{1,0:T(8,128)(2,1)S(1)} %copy-done, bf16[256,384]{1,0:T(8,128)(2,1)S(1)} %reshape.25, s32[128]{0:T(128)S(1)} %multiply_add_fusion), kind=kOutput, calls=%fused_computation.1 | convolution fusion | flops 327630848 | bytes 3342848 | tf_op jit(solution)/shard_map/dot_general | solution.py:105
  61.9 30.5 %all_to_all.16 = bf16[8,16,3072]{2,1,0:T(8,128)(2,1)S(1)} all-to-all(bf16[8,16,3072]{2,1,0:T(8,128)(2,1)} %bitcast.5), channel_id=1, replica_groups=mesh['req'=64,'tp'=8] {'tp'}, dimensions={0} | all-to-all | bytes 1572864 | tf_op jit(solution)/shard_map/all_to_all | solution.py:159
  92.5 0.8 reduce_sum.22
  93.2 0.0 reduce-scatter.2.cloned.1.call-done
Async XLA Ops:
  7.2 21.3 %copy-start = (bf16[384,3072]{1,0:T(8,128)(2,1)S(1)}, bf16[384,3072]{1,0:T(8,128)(2,1)}, u32[]{:S(2)}) copy-start(bf16[384,3072]{1,0:T(8,128)(2,1)} %param.17) | copy-start | bytes 7077892
  10.8 26.9 %all-to-all-start = ((bf16[64,4,640]{2,1,0:T(4,128)(2,1)}), bf16[64,4,640]{2,1,0:T(4,128)(2,1)S(1)}, u32[]{:S(2)}, u32[]{:S(2)}) async-start(bf16[64,4,640]{2,1,0:T(4,128)(2,1)} %reshape.22), calls=%async_computation | async-start | bytes 655360 | tf_op jit(solution)/shard_map/all_to_all | solution.py:136
  24.8 68.4 %reduce-scatter.2.cloned.1.call-start = ((), (), s32[]{:S(2)}) async-start(), calls=%async_computation.4 | async-start | bytes 1769472 | tf_op jit(solution)/shard_map/reduce_scatter | solution.py:140
  28.5 10.1 %copy-start.1 = (s32[256,2]{0,1:T(2,128)S(1)}, s32[256,2]{0,1:T(2,128)}, u32[]{:S(2)}) copy-start(s32[256,2]{0,1:T(2,128)} %param.12) | copy-start | bytes 6148
Sparse Core Ops, SparseCore 0:
  38.7 45.2 reduce-scatter.1

commit v6 on v5

--- a/solution.py
+++ b/solution.py
@@ -133,10 +133,10 @@
         .astype(jnp.bfloat16)
         .reshape(groups, capacity, q_width + kv_width)
     )
+    pre_part, send = lax.optimization_barrier((pre_part, send))
     recv = lax.all_to_all(send, "req", split_axis=0, concat_axis=0, tiled=True).reshape(
         slot_count, q_width + kv_width
     )
-    pre_part, recv = lax.optimization_barrier((pre_part, recv))
     pre_out = lax.psum_scatter(pre_part, "tp", scatter_dimension=0, tiled=True)
     slot_attn = vmem_call(
         decode_kernel,

time: 101 us -> 107 us (1.059)
  waiting for transfers between devices: 6.19 us -> 12.1 us
    all_to_all x1, waiting for transfers between devices: 6.17 us -> 12.1 us  [per_device(): lax.all_to_all(send, 'req', split_axis=0, concat_axis=0, tiled=True)]
  transfers between devices with their start and end apart: 2 -> 2, of which waited for: 1 -> 1; matrix products, arithmetic and copies ran while one was open for 7% -> 5% of each run, Pallas kernels for 7% -> 3%
where the time goes in v6:
time: 107 us; the launch traced here: 106 us
  blocking collectives  47 us (44%)
  starting transfers between devices  14.1 us (13%)
  between operations  14.1 us (13%)
  waiting for transfers between devices  12.1 us (11%)
  Pallas kernels  7 us (7%)
  matrix products  5.88 us (5%)
  local copies, waits for them, and re-layouts  3.45 us (3%)
  other arithmetic  2.41 us (2%)
    all_to_all x1, blocking collectives, per_device(): lax.all_to_all(dec_part.reshape(tp_count, tok_rows // tp_count, dec_part....  30.5 us
    all_to_all x1, blocking collectives, per_device(): lax.all_to_all(slot_attn.reshape(groups, capacity, q_width), 'req', split...  16.5 us
    all_to_all x1, starting transfers between devices, per_device(): lax.all_to_all(send, 'req', split_axis=0, concat_axis=0, tiled=True)  14 us
    all_to_all x1, waiting for transfers between devices, per_device(): lax.all_to_all(send, 'req', split_axis=0, concat_axis=0, tiled=True)  12.1 us
    pallas_call x2, Pallas kernels, vmem_call(): pl.pallas_call(kernel, out_shape=out_shape, in_specs=[pl.BlockSpec(memory...  7 us
    dot_general x2, matrix products, term_maker(): return jnp.dot(rows_source, wo, preferred_element_type=jnp.float32)  4.72 us
  transfers between devices with their start and end apart: 2, of which 1 were waited for; matrix products, arithmetic and copies ran while one was open for 5% of the time, Pallas kernels for 3%

profile of v6, /device:TPU:6, one launch (start us, length us, event | category | flops | bytes accessed | tf_op | source)
XLA Modules:
  0.0 106.0 jit_solution(13644930207880866286)
XLA Ops:
  7.2 0.0 copy-start
  7.2 0.0 reduce-scatter.2.cloned.1.call-start
  7.2 1.0 convert_reduce_fusion
  8.2 0.7 multiply_add_fusion
  8.9 1.2 %convolution_convert_fusion.2 = bf16[256,640]{1,0:T(8,128)(2,1)S(1)} fusion(bf16[128,256]{1,0:T(8,128)(2,1)} %param.10, bf16[128,384]{1,0:T(8,128)(2,1)} %param.9, s32[128]{0:T(128)S(1)} %multiply_add_fusion), kind=kOutput, calls=%fused_computation.2 | convolution fusion | flops 42467328 | bytes 492032 | tf_op jit(solution)/shard_map/dot_general | solution.py:132
  10.1 0.8 reshape.22
  10.9 3.6 %shard_map.104 = bf16[256,384]{1,0:T(8,128)(2,1)} custom-call(bf16[256,384]{1,0:T(8,128)(2,1)} %q_ref.1, bf16[256,256]{1,0:T(8,128)(2,1)} %kv_ref.1, s32[1,3]{1,0:T(1,128)} %meta_ref.1, bf16[512,256]{1,0:T(8,128)(2,1)} %pool_ref.3), custom_call_target="tpu_custom_call" | custom-call | flops 301989888 | bytes 786444 | tf_op jit(solution)/shard_map/pallas_call | solution.py:93
  14.4 0.0 copy-done
  14.4 0.0 copy-start.1
  14.4 3.1 %convolution_convert_fusion = bf16[256,3072]{1,0:T(8,128)(2,1)} fusion(bf16[256,384]{1,0:T(8,128)(2,1)} %shard_map.104, bf16[384,3072]{1,0:T(8,128)(2,1)S(1)} %copy-done), kind=kOutput, calls=%fused_computation | convolution fusion | flops 604766208 | bytes 4128768 | tf_op jit(solution)/shard_map/dot_general | solution.py:105
  17.5 0.0 reduce-scatter.2.cloned.1.call-update
  17.5 14.0 %all-to-all-start = ((bf16[64,4,640]{2,1,0:T(4,128)(2,1)}), bf16[64,4,640]{2,1,0:T(4,128)(2,1)S(1)}, u32[]{:S(2)}, u32[]{:S(2)}) async-start(bf16[64,4,640]{2,1,0:T(4,128)(2,1)} %reshape.22), calls=%async_computation | async-start | bytes 655360 | tf_op jit(solution)/shard_map/all_to_all | solution.py:137
  31.6 0.0 copy-done.1
  31.6 0.8 copy.12.table_ref
  32.4 12.1 %all-to-all-done = bf16[64,4,640]{2,1,0:T(4,128)(2,1)S(1)} async-done(((bf16[64,4,640]{2,1,0:T(4,128)(2,1)}), bf16[64,4,640]{2,1,0:T(4,128)(2,1)S(1)}, u32[]{:S(2)}, u32[]{:S(2)}) %all-to-all-start) | async-done | bytes 327712 | tf_op jit(solution)/shard_map/all_to_all | solution.py:137
  44.4 0.8 reshape.23.recv_ref
  45.2 3.4 %shard_map.105 = bf16[256,384]{1,0:T(8,128)(2,1)} custom-call(bf16[256,640]{1,0:T(8,128)(2,1)} %reshape.23.recv_ref, s32[256,2]{1,0:T(8,128)} %copy.12.table_ref, bf16[512,256]{1,0:T(8,128)(2,1)} %pool_ref.3), custom_call_target="tpu_custom_call" | custom-call | flops 201326592 | bytes 788480 | tf_op jit(solution)/shard_map/pallas_call | solution.py:93
  48.7 1.0 reshape.24
  49.7 16.5 %all_to_all.15 = bf16[64,4,384]{2,1,0:T(4,128)(2,1)S(1)} all-to-all(bf16[64,4,384]{2,1,0:T(4,128)(2,1)S(1)} %reshape.24), channel_id=1, replica_groups=mesh['req'=64,'tp'=8] {'req'}, dimensions={0} | all-to-all | bytes 393216 | tf_op jit(solution)/shard_map/all_to_all | solution.py:148
  66.2 0.1 reshape.25
  66.2 1.6 %convolution_convert_fusion.1 = bf16[128,3072]{1,0:T(8,128)(2,1)} fusion(bf16[384,3072]{1,0:T(8,128)(2,1)S(1)} %copy-done, bf16[256,384]{1,0:T(8,128)(2,1)S(1)} %reshape.25, s32[128]{0:T(128)S(1)} %multiply_add_fusion), kind=kOutput, calls=%fused_computation.1 | convolution fusion | flops 327630848 | bytes 3342848 | tf_op jit(solution)/shard_map/dot_general | solution.py:105
  67.9 30.5 %all_to_all.16 = bf16[8,16,3072]{2,1,0:T(8,128)(2,1)S(1)} all-to-all(bf16[8,16,3072]{2,1,0:T(8,128)(2,1)} %bitcast.5), channel_id=1, replica_groups=mesh['req'=64,'tp'=8] {'tp'}, dimensions={0} | all-to-all | bytes 1572864 | tf_op jit(solution)/shard_map/all_to_all | solution.py:159
  98.4 0.8 reduce_sum.22
  99.1 0.0 reduce-scatter.2.cloned.1.call-done
Async XLA Ops:
  7.2 7.3 %copy-start = (bf16[384,3072]{1,0:T(8,128)(2,1)S(1)}, bf16[384,3072]{1,0:T(8,128)(2,1)}, u32[]{:S(2)}) copy-start(bf16[384,3072]{1,0:T(8,128)(2,1)} %param.17) | copy-start | bytes 7077892
  7.2 91.9 %reduce-scatter.2.cloned.1.call-start = ((), (), s32[]{:S(2)}) async-start(), calls=%async_computation.4 | async-start | bytes 1769472 | tf_op jit(solution)/shard_map/reduce_scatter | solution.py:140
  14.4 17.1 %copy-start.1 = (s32[256,2]{0,1:T(2,128)S(1)}, s32[256,2]{0,1:T(2,128)}, u32[]{:S(2)}) copy-start(s32[256,2]{0,1:T(2,128)} %param.12) | copy-start | bytes 6148
  17.5 26.9 %all-to-all-start = ((bf16[64,4,640]{2,1,0:T(4,128)(2,1)}), bf16[64,4,640]{2,1,0:T(4,128)(2,1)S(1)}, u32[]{:S(2)}, u32[]{:S(2)}) async-start(bf16[64,4,640]{2,1,0:T(4,128)(2,1)} %reshape.22), calls=%async_computation | async-start | bytes 655360 | tf_op jit(solution)/shard_map/all_to_all | solution.py:137
Sparse Core Ops, SparseCore 0:
  17.7 47.5 reduce-scatter.1

commit v7 on v5

--- a/solution.py
+++ b/solution.py
@@ -20,8 +20,9 @@
     kv_heads = pool_ref.shape[1] // (2 * HD)
     q_width = kv_heads * QPK * HD
     table = table_ref[...]
-    begins = table[:, 0:1]
-    ends = begins + table[:, 1:2]
+    spread = jnp.broadcast_to(table[0:1, :], (HD, slot_rows))
+    begins = jnp.transpose(spread)[:, 0:1]
+    ends = begins + jnp.transpose(jnp.broadcast_to(table[1:2, :], (HD, slot_rows)))[:, 0:1]
     places = lax.broadcasted_iota(jnp.int32, (slot_rows, pool_ref.shape[0]), 1)
     visible = (places >= begins) & (places < ends)
     for g in range(kv_heads):
@@ -141,7 +142,7 @@
     slot_attn = vmem_call(
         decode_kernel,
         jax.ShapeDtypeStruct((slot_count, q_width), jnp.bfloat16),
-        (recv, dec_table, pool),
+        (recv, jnp.transpose(dec_table), pool),
         4 * slot_count * pool.shape[0] * q_width,
         slot_count * pool.shape[0] * q_width // HD,
     )

time: 101 us -> 101 us (level)
  blocking collectives: 47 us -> 48.2 us
    all_to_all x1, blocking collectives: 30.5 us -> 31.7 us  [per_device(): lax.all_to_all(dec_part.reshape(tp_count, tok_rows // tp_count, dec_part....]
  transfers between devices with their start and end apart: 2 -> 2, of which waited for: 1 -> 1; matrix products, arithmetic and copies ran while one was open for 7% -> 6% of each run, Pallas kernels for 7% -> 7%
where the time goes in v7:
time: 101 us; the launch traced here: 100 us
  blocking collectives  48.2 us (48%)
  starting transfers between devices  14.1 us (14%)
  between operations  14.1 us (14%)
  Pallas kernels  6.97 us (7%)
  waiting for transfers between devices  6.2 us (6%)
  matrix products  5.87 us (6%)
  local copies, waits for them, and re-layouts  2.65 us (3%)
  other arithmetic  2.41 us (2%)
    all_to_all x1, blocking collectives, per_device(): lax.all_to_all(dec_part.reshape(tp_count, tok_rows // tp_count, dec_part....  31.7 us
    all_to_all x1, blocking collectives, per_device(): lax.all_to_all(slot_attn.reshape(groups, capacity, q_width), 'req', split...  16.5 us
    all_to_all x1, starting transfers between devices, per_device(): lax.all_to_all(send, 'req', split_axis=0, concat_axis=0, tiled=True)  14 us
    pallas_call x2, Pallas kernels, vmem_call(): pl.pallas_call(kernel, out_shape=out_shape, in_specs=[pl.BlockSpec(memory...  6.97 us
    all_to_all x1, waiting for transfers between devices, per_device(): lax.all_to_all(send, 'req', split_axis=0, concat_axis=0, tiled=True)  6.18 us
    dot_general x2, matrix products, term_maker(): return jnp.dot(rows_source, wo, preferred_element_type=jnp.float32)  4.71 us
  transfers between devices with their start and end apart: 2, of which 1 were waited for; matrix products, arithmetic and copies ran while one was open for 6% of the time, Pallas kernels for 7%

profile of v7, /device:TPU:6, one launch (start us, length us, event | category | flops | bytes accessed | tf_op | source)
XLA Modules:
  0.0 100.4 jit_solution(4089480667064317418)
XLA Ops:
  7.2 0.0 copy-start
  7.2 1.0 convert_reduce_fusion
  8.2 0.7 multiply_add_fusion
  8.8 1.2 %convolution_convert_fusion.2 = bf16[256,640]{1,0:T(8,128)(2,1)S(1)} fusion(bf16[128,256]{1,0:T(8,128)(2,1)} %param.10, bf16[128,384]{1,0:T(8,128)(2,1)} %param.9, s32[128]{0:T(128)S(1)} %multiply_add_fusion), kind=kOutput, calls=%fused_computation.2 | convolution fusion | flops 42467328 | bytes 492032 | tf_op jit(solution)/shard_map/dot_general | solution.py:133
  10.0 0.8 reshape.22
  10.8 14.0 %all-to-all-start = ((bf16[64,4,640]{2,1,0:T(4,128)(2,1)}), bf16[64,4,640]{2,1,0:T(4,128)(2,1)S(1)}, u32[]{:S(2)}, u32[]{:S(2)}) async-start(bf16[64,4,640]{2,1,0:T(4,128)(2,1)} %reshape.22), calls=%async_computation | async-start | bytes 655360 | tf_op jit(solution)/shard_map/all_to_all | solution.py:137
  24.8 0.0 reduce-scatter.2.cloned.1.call-start
  24.9 3.6 %shard_map.104 = bf16[256,384]{1,0:T(8,128)(2,1)} custom-call(bf16[256,384]{1,0:T(8,128)(2,1)} %q_ref.1, bf16[256,256]{1,0:T(8,128)(2,1)} %kv_ref.1, s32[1,3]{1,0:T(1,128)} %meta_ref.1, bf16[512,256]{1,0:T(8,128)(2,1)} %pool_ref.3), custom_call_target="tpu_custom_call" | custom-call | flops 301989888 | bytes 786444 | tf_op jit(solution)/shard_map/pallas_call | solution.py:94
  28.5 0.0 copy-done
  28.5 3.1 %convolution_convert_fusion = bf16[256,3072]{1,0:T(8,128)(2,1)} fusion(bf16[256,384]{1,0:T(8,128)(2,1)} %shard_map.104, bf16[384,3072]{1,0:T(8,128)(2,1)S(1)} %copy-done), kind=kOutput, calls=%fused_computation | convolution fusion | flops 604766208 | bytes 4128768 | tf_op jit(solution)/shard_map/dot_general | solution.py:106
  31.5 6.2 %all-to-all-done = bf16[64,4,640]{2,1,0:T(4,128)(2,1)S(1)} async-done(((bf16[64,4,640]{2,1,0:T(4,128)(2,1)}), bf16[64,4,640]{2,1,0:T(4,128)(2,1)S(1)}, u32[]{:S(2)}, u32[]{:S(2)}) %all-to-all-start) | async-done | bytes 327712 | tf_op jit(solution)/shard_map/all_to_all | solution.py:137
  37.7 0.8 reshape.23.recv_ref
  38.5 0.0 reduce-scatter.2.cloned.1.call-update
  38.5 3.4 %shard_map.105 = bf16[256,384]{1,0:T(8,128)(2,1)} custom-call(bf16[256,640]{1,0:T(8,128)(2,1)} %reshape.23.recv_ref, s32[2,256]{1,0:T(2,128)} %bitcast.7, bf16[512,256]{1,0:T(8,128)(2,1)} %pool_ref.3), custom_call_target="tpu_custom_call" | custom-call | flops 201326592 | bytes 788480 | tf_op jit(solution)/shard_map/pallas_call | solution.py:94
  41.9 1.0 reshape.24
  42.9 16.5 %all_to_all.15 = bf16[64,4,384]{2,1,0:T(4,128)(2,1)S(1)} all-to-all(bf16[64,4,384]{2,1,0:T(4,128)(2,1)S(1)} %reshape.24), channel_id=1, replica_groups=mesh['req'=64,'tp'=8] {'req'}, dimensions={0} | all-to-all | bytes 393216 | tf_op jit(solution)/shard_map/all_to_all | solution.py:149
  59.4 0.1 reshape.25
  59.5 1.6 %convolution_convert_fusion.1 = bf16[128,3072]{1,0:T(8,128)(2,1)} fusion(bf16[384,3072]{1,0:T(8,128)(2,1)S(1)} %copy-done, bf16[256,384]{1,0:T(8,128)(2,1)S(1)} %reshape.25, s32[128]{0:T(128)S(1)} %multiply_add_fusion), kind=kOutput, calls=%fused_computation.1 | convolution fusion | flops 327630848 | bytes 3342848 | tf_op jit(solution)/shard_map/dot_general | solution.py:106
  61.1 31.7 %all_to_all.16 = bf16[8,16,3072]{2,1,0:T(8,128)(2,1)S(1)} all-to-all(bf16[8,16,3072]{2,1,0:T(8,128)(2,1)} %bitcast.6), channel_id=1, replica_groups=mesh['req'=64,'tp'=8] {'tp'}, dimensions={0} | all-to-all | bytes 1572864 | tf_op jit(solution)/shard_map/all_to_all | solution.py:160
  92.8 0.8 reduce_sum.22
  93.5 0.0 reduce-scatter.2.cloned.1.call-done
Async XLA Ops:
  7.2 21.3 %copy-start = (bf16[384,3072]{1,0:T(8,128)(2,1)S(1)}, bf16[384,3072]{1,0:T(8,128)(2,1)}, u32[]{:S(2)}) copy-start(bf16[384,3072]{1,0:T(8,128)(2,1)} %param.17) | copy-start | bytes 7077892
  10.8 26.9 %all-to-all-start = ((bf16[64,4,640]{2,1,0:T(4,128)(2,1)}), bf16[64,4,640]{2,1,0:T(4,128)(2,1)S(1)}, u32[]{:S(2)}, u32[]{:S(2)}) async-start(bf16[64,4,640]{2,1,0:T(4,128)(2,1)} %reshape.22), calls=%async_computation | async-start | bytes 655360 | tf_op jit(solution)/shard_map/all_to_all | solution.py:137
  24.8 68.7 %reduce-scatter.2.cloned.1.call-start = ((), (), s32[]{:S(2)}) async-start(), calls=%async_computation.4 | async-start | bytes 1769472 | tf_op jit(solution)/shard_map/reduce_scatter | solution.py:141
Sparse Core Ops, SparseCore 0:
  38.7 47.1 reduce-scatter.1

commit v8 on v7

--- a/solution.py
+++ b/solution.py
@@ -16,7 +16,9 @@
 
 def decode_kernel(recv_ref, table_ref, pool_ref, out_ref):
     score_scale = 1.0 / math.sqrt(HD)
-    slot_rows = recv_ref.shape[0]
+    slot_rows = recv_ref.shape[0] * recv_ref.shape[1]
+    recv = recv_ref[...].reshape(slot_rows, recv_ref.shape[2])
+    outs = []
     kv_heads = pool_ref.shape[1] // (2 * HD)
     q_width = kv_heads * QPK * HD
     table = table_ref[...]
@@ -28,11 +30,11 @@
     for g in range(kv_heads):
         keys = pool_ref[:, g * 2 * HD : g * 2 * HD + HD]
         vals = pool_ref[:, g * 2 * HD + HD : (g + 1) * 2 * HD]
-        own_key = recv_ref[:, q_width + g * 2 * HD : q_width + g * 2 * HD + HD].astype(jnp.float32)
-        own_val = recv_ref[:, q_width + g * 2 * HD + HD : q_width + (g + 1) * 2 * HD].astype(jnp.float32)
+        own_key = recv[:, q_width + g * 2 * HD : q_width + g * 2 * HD + HD].astype(jnp.float32)
+        own_val = recv[:, q_width + g * 2 * HD + HD : q_width + (g + 1) * 2 * HD].astype(jnp.float32)
         for h in range(QPK):
             col = (g * QPK + h) * HD
-            q = recv_ref[:, col : col + HD]
+            q = recv[:, col : col + HD]
             scores = lax.dot_general(
                 q, keys, (((1,), (1,)), ((), ())), preferred_element_type=jnp.float32
             ) * score_scale
@@ -45,7 +47,8 @@
             weights = (weights / total).astype(jnp.bfloat16)
             own_weight = (own_exp / total).astype(jnp.bfloat16).astype(jnp.float32)
             mixed = jnp.dot(weights, vals, preferred_element_type=jnp.float32) + own_weight * own_val
-            out_ref[:, col : col + HD] = mixed.astype(jnp.bfloat16)
+            outs.append(mixed.astype(jnp.bfloat16))
+    out_ref[...] = jnp.concatenate(outs, axis=1).reshape(out_ref.shape)
 
 
 def prefill_kernel(q_ref, kv_ref, meta_ref, pool_ref, out_ref):
@@ -134,21 +137,17 @@
         .astype(jnp.bfloat16)
         .reshape(groups, capacity, q_width + kv_width)
     )
-    recv = lax.all_to_all(send, "req", split_axis=0, concat_axis=0, tiled=True).reshape(
-        slot_count, q_width + kv_width
-    )
+    recv = lax.all_to_all(send, "req", split_axis=0, concat_axis=0, tiled=True)
     pre_part, recv = lax.optimization_barrier((pre_part, recv))
     pre_out = lax.psum_scatter(pre_part, "tp", scatter_dimension=0, tiled=True)
     slot_attn = vmem_call(
         decode_kernel,
-        jax.ShapeDtypeStruct((slot_count, q_width), jnp.bfloat16),
+        jax.ShapeDtypeStruct((groups, capacity, q_width), jnp.bfloat16),
         (recv, jnp.transpose(dec_table), pool),
         4 * slot_count * pool.shape[0] * q_width,
         slot_count * pool.shape[0] * q_width // HD,
     )
-    replies = lax.all_to_all(
-        slot_attn.reshape(groups, capacity, q_width), "req", split_axis=0, concat_axis=0, tiled=True
-    )
+    replies = lax.all_to_all(slot_attn, "req", split_axis=0, concat_axis=0, tiled=True)
     dec_attn = lax.dot_general(
         dispatch,
         replies.reshape(slot_count, q_width),

time: 101 us -> 100 us (0.990)
  local copies, waits for them, and re-layouts: 2.65 us -> 1.57 us
    reshape x2 -> x0, local copies, waits for them, and re-layouts: 1.78 us -> none  [the longest x1 0.98 us: per_device(): slot_attn.reshape(groups, capacity, q_width)]
where the time goes in v8:
time: 100 us; the launch traced here: 99.6 us
  blocking collectives  48.4 us (48%)
  starting transfers between devices  14.1 us (14%)
  between operations  14.1 us (14%)
  Pallas kernels  6.97 us (7%)
  waiting for transfers between devices  6.2 us (6%)
  matrix products  5.86 us (6%)
  other arithmetic  2.41 us (2%)
  local copies, waits for them, and re-layouts  1.57 us (2%)
    all_to_all x1, blocking collectives, per_device(): lax.all_to_all(dec_part.reshape(tp_count, tok_rows // tp_count, dec_part....  31.7 us
    all_to_all x1, blocking collectives, per_device(): lax.all_to_all(slot_attn, 'req', split_axis=0, concat_axis=0, tiled=True)  16.7 us
    all_to_all x1, starting transfers between devices, per_device(): recv = lax.all_to_all(send, 'req', split_axis=0, concat_axis=0, tiled=True)  14 us
    pallas_call x2, Pallas kernels, vmem_call(): pl.pallas_call(kernel, out_shape=out_shape, in_specs=[pl.BlockSpec(memory...  6.97 us
    all_to_all x1, waiting for transfers between devices, per_device(): recv = lax.all_to_all(send, 'req', split_axis=0, concat_axis=0, tiled=True)  6.18 us
    dot_general x2, matrix products, term_maker(): return jnp.dot(rows_source, wo, preferred_element_type=jnp.float32)  4.7 us
  transfers between devices with their start and end apart: 2, of which 1 were waited for; matrix products, arithmetic and copies ran while one was open for 6% of the time, Pallas kernels for 7%

profile of v8, /device:TPU:6, one launch (start us, length us, event | category | flops | bytes accessed | tf_op | source)
XLA Modules:
  0.0 99.6 jit_solution(9627921009133737205)
XLA Ops:
  7.2 0.0 copy-start
  7.2 1.0 convert_reduce_fusion
  8.2 0.7 multiply_add_fusion
  8.8 1.2 %convolution_convert_fusion.2 = bf16[256,640]{1,0:T(8,128)(2,1)S(1)} fusion(bf16[128,256]{1,0:T(8,128)(2,1)} %param.10, bf16[128,384]{1,0:T(8,128)(2,1)} %param.9, s32[128]{0:T(128)S(1)} %multiply_add_fusion), kind=kOutput, calls=%fused_computation.2 | convolution fusion | flops 42467328 | bytes 492032 | tf_op jit(solution)/shard_map/dot_general | solution.py:136
  10.0 0.8 reshape.16
  10.8 14.0 %all-to-all-start = ((bf16[64,4,640]{2,1,0:T(4,128)(2,1)}), bf16[64,4,640]{2,1,0:T(4,128)(2,1)S(1)}, u32[]{:S(2)}, u32[]{:S(2)}) async-start(bf16[64,4,640]{2,1,0:T(4,128)(2,1)} %reshape.16), calls=%async_computation | async-start | bytes 655360 | tf_op jit(solution)/shard_map/all_to_all | solution.py:140
  24.8 0.0 reduce-scatter.2.cloned.1.call-start
  24.9 3.6 %shard_map.104 = bf16[256,384]{1,0:T(8,128)(2,1)} custom-call(bf16[256,384]{1,0:T(8,128)(2,1)} %q_ref.1, bf16[256,256]{1,0:T(8,128)(2,1)} %kv_ref.1, s32[1,3]{1,0:T(1,128)} %meta_ref.1, bf16[512,256]{1,0:T(8,128)(2,1)} %pool_ref.3), custom_call_target="tpu_custom_call" | custom-call | flops 301989888 | bytes 786444 | tf_op jit(solution)/shard_map/pallas_call | solution.py:97
  28.5 0.0 copy-done
  28.5 3.1 %convolution_convert_fusion = bf16[256,3072]{1,0:T(8,128)(2,1)} fusion(bf16[256,384]{1,0:T(8,128)(2,1)} %shard_map.104, bf16[384,3072]{1,0:T(8,128)(2,1)S(1)} %copy-done), kind=kOutput, calls=%fused_computation | convolution fusion | flops 604766208 | bytes 4128768 | tf_op jit(solution)/shard_map/dot_general | solution.py:109
  31.5 6.2 %all-to-all-done.recv_ref = bf16[64,4,640]{2,1,0:T(4,128)(2,1)S(1)} async-done(((bf16[64,4,640]{2,1,0:T(4,128)(2,1)}), bf16[64,4,640]{2,1,0:T(4,128)(2,1)S(1)}, u32[]{:S(2)}, u32[]{:S(2)}) %all-to-all-start) | async-done | bytes 327712 | tf_op jit(solution)/shard_map/all_to_all | solution.py:140
  37.7 0.0 copy-start.1
  37.7 0.0 reduce-scatter.2.cloned.1.call-update
  37.7 0.7 copy-done.1
  38.4 3.4 %shard_map.105 = bf16[64,4,384]{2,1,0:T(4,128)(2,1)} custom-call(bf16[64,4,640]{2,1,0:T(4,128)(2,1)} %copy-done.1, s32[2,256]{1,0:T(2,128)} %bitcast.7, bf16[512,256]{1,0:T(8,128)(2,1)} %pool_ref.3), custom_call_target="tpu_custom_call" | custom-call | flops 201326592 | bytes 788480 | tf_op jit(solution)/shard_map/pallas_call | solution.py:97
  41.8 16.7 %all_to_all.15 = bf16[64,4,384]{2,1,0:T(4,128)(2,1)S(1)} all-to-all(bf16[64,4,384]{2,1,0:T(4,128)(2,1)} %shard_map.105), channel_id=1, replica_groups=mesh['req'=64,'tp'=8] {'req'}, dimensions={0} | all-to-all | bytes 393216 | tf_op jit(solution)/shard_map/all_to_all | solution.py:150
  58.6 0.1 reshape.17
  58.6 1.6 %convolution_convert_fusion.1 = bf16[128,3072]{1,0:T(8,128)(2,1)} fusion(bf16[384,3072]{1,0:T(8,128)(2,1)S(1)} %copy-done, bf16[256,384]{1,0:T(8,128)(2,1)S(1)} %reshape.17, s32[128]{0:T(128)S(1)} %multiply_add_fusion), kind=kOutput, calls=%fused_computation.1 | convolution fusion | flops 327630848 | bytes 3342848 | tf_op jit(solution)/shard_map/dot_general | solution.py:109
  60.3 31.7 %all_to_all.16 = bf16[8,16,3072]{2,1,0:T(8,128)(2,1)S(1)} all-to-all(bf16[8,16,3072]{2,1,0:T(8,128)(2,1)} %bitcast.6), channel_id=1, replica_groups=mesh['req'=64,'tp'=8] {'tp'}, dimensions={0} | all-to-all | bytes 1572864 | tf_op jit(solution)/shard_map/all_to_all | solution.py:159
  92.0 0.8 reduce_sum.22
  92.7 0.0 reduce-scatter.2.cloned.1.call-done
Async XLA Ops:
  7.2 21.3 %copy-start = (bf16[384,3072]{1,0:T(8,128)(2,1)S(1)}, bf16[384,3072]{1,0:T(8,128)(2,1)}, u32[]{:S(2)}) copy-start(bf16[384,3072]{1,0:T(8,128)(2,1)} %param.17) | copy-start | bytes 7077892
  10.8 26.9 %all-to-all-start = ((bf16[64,4,640]{2,1,0:T(4,128)(2,1)}), bf16[64,4,640]{2,1,0:T(4,128)(2,1)S(1)}, u32[]{:S(2)}, u32[]{:S(2)}) async-start(bf16[64,4,640]{2,1,0:T(4,128)(2,1)} %reshape.16), calls=%async_computation | async-start | bytes 655360 | tf_op jit(solution)/shard_map/all_to_all | solution.py:140
  24.8 67.9 %reduce-scatter.2.cloned.1.call-start = ((), (), s32[]{:S(2)}) async-start(), calls=%async_computation.4 | async-start | bytes 1769472 | tf_op jit(solution)/shard_map/reduce_scatter | solution.py:142
  37.7 0.7 copy-start.1
Sparse Core Ops, SparseCore 0:
  37.9 47.1 reduce-scatter.1

commit v9 on v8

--- a/solution.py
+++ b/solution.py
@@ -92,6 +92,26 @@
             out_ref[:, col : col + HD] = jnp.where(live, mixed, 0.0).astype(jnp.bfloat16)
 
 
+def route_kernel(owner_ref, q_ref, kv_ref, send_ref, dispatch_ref):
+    tok_rows = q_ref.shape[0]
+    slot_count = dispatch_ref.shape[0]
+    capacity = slot_count // send_ref.shape[0]
+    owner_row = owner_ref[...]
+    owner_col = jnp.transpose(jnp.broadcast_to(owner_row, (tok_rows, tok_rows)))
+    earlier = lax.broadcasted_iota(jnp.int32, (tok_rows, tok_rows), 0) < lax.broadcasted_iota(
+        jnp.int32, (tok_rows, tok_rows), 1
+    )
+    same = (owner_col == owner_row) & earlier
+    ranking = jnp.sum(same.astype(jnp.int32), axis=0, keepdims=True)
+    slot_ids = owner_row * capacity + ranking
+    slots = lax.broadcasted_iota(jnp.int32, (slot_count, tok_rows), 0)
+    dispatch = (slots == slot_ids).astype(jnp.bfloat16)
+    dispatch_ref[...] = dispatch
+    rows = jnp.concatenate([q_ref[...], kv_ref[...]], axis=1)
+    send = jnp.dot(dispatch, rows, preferred_element_type=jnp.float32).astype(jnp.bfloat16)
+    send_ref[...] = send.reshape(send_ref.shape)
+
+
 def vmem_call(kernel, out_shape, operands, flops, transcendentals):
     bytes_accessed = sum(x.size * x.dtype.itemsize for x in operands) + out_shape.size * 2
     return pl.pallas_call(
@@ -127,16 +147,20 @@
     )
     pre_part = term_maker(pre_attn, wo).astype(jnp.bfloat16)
 
-    tok_iota = lax.iota(jnp.int32, tok_rows)
-    earlier_same = (dec_owner[:, None] == dec_owner[None, :]) & (tok_iota[None, :] < tok_iota[:, None])
-    ranking = jnp.sum(earlier_same.astype(jnp.int32), axis=1)
-    slot_ids = dec_owner * capacity + ranking
-    dispatch = (slot_ids[None, :] == lax.iota(jnp.int32, slot_count)[:, None]).astype(jnp.bfloat16)
-    send = (
-        jnp.dot(dispatch, jnp.concatenate([dec_q, dec_kv], axis=1), preferred_element_type=jnp.float32)
-        .astype(jnp.bfloat16)
-        .reshape(groups, capacity, q_width + kv_width)
-    )
+    send, dispatch = pl.pallas_call(
+        route_kernel,
+        out_shape=(
+            jax.ShapeDtypeStruct((groups, capacity, q_width + kv_width), jnp.bfloat16),
+            jax.ShapeDtypeStruct((slot_count, tok_rows), jnp.bfloat16),
+        ),
+        in_specs=[pl.BlockSpec(memory_space=pltpu.VMEM)] * 3,
+        out_specs=(pl.BlockSpec(memory_space=pltpu.VMEM), pl.BlockSpec(memory_space=pltpu.VMEM)),
+        cost_estimate=pl.CostEstimate(
+            flops=2 * slot_count * tok_rows * (q_width + kv_width),
+            transcendentals=0,
+            bytes_accessed=2 * (tok_rows + slot_count) * (q_width + kv_width),
+        ),
+    )(dec_owner.reshape(1, tok_rows), dec_q, dec_kv)
     recv = lax.all_to_all(send, "req", split_axis=0, concat_axis=0, tiled=True)
     pre_part, recv = lax.optimization_barrier((pre_part, recv))
     pre_out = lax.psum_scatter(pre_part, "tp", scatter_dimension=0, tiled=True)

time: 100 us -> 99 us (0.990)
  Pallas kernels: 6.97 us -> 9.05 us
  other arithmetic: 2.41 us -> 0.75 us
  matrix products: 5.86 us -> 4.71 us
    pallas_call x0 -> x1, Pallas kernels: none -> 2.1 us  [per_device(): pl.pallas_call(route_kernel, out_shape=(jax.ShapeDtypeStruct((groups, cap...]
    dot_general x1 -> x0, matrix products: 1.16 us -> none  [per_device(): jnp.dot(dispatch, jnp.concatenate([dec_q, dec_kv], axis=1), preferred_ele...]
where the time goes in v9:
time: 99 us; the launch traced here: 98 us
  blocking collectives  48.4 us (49%)
  starting transfers between devices  14.1 us (14%)
  between operations  14.1 us (14%)
  Pallas kernels  9.05 us (9%)
  waiting for transfers between devices  6.18 us (6%)
  matrix products  4.71 us (5%)
    all_to_all x1, blocking collectives, per_device(): lax.all_to_all(dec_part.reshape(tp_count, tok_rows // tp_count, dec_part....  31.7 us
    all_to_all x1, blocking collectives, per_device(): lax.all_to_all(slot_attn, 'req', split_axis=0, concat_axis=0, tiled=True)  16.7 us
    all_to_all x1, starting transfers between devices, per_device(): recv = lax.all_to_all(send, 'req', split_axis=0, concat_axis=0, tiled=True)  14 us
    pallas_call x2, Pallas kernels, vmem_call(): pl.pallas_call(kernel, out_shape=out_shape, in_specs=[pl.BlockSpec(memory...  6.95 us
    all_to_all x1, waiting for transfers between devices, per_device(): recv = lax.all_to_all(send, 'req', split_axis=0, concat_axis=0, tiled=True)  6.17 us
    dot_general x2, matrix products, term_maker(): return jnp.dot(rows_source, wo, preferred_element_type=jnp.float32)  4.71 us
    pallas_call x1, Pallas kernels, per_device(): pl.pallas_call(route_kernel, out_shape=(jax.ShapeDtypeStruct((groups, cap...  2.1 us
  transfers between devices with their start and end apart: 2, of which 1 were waited for; matrix products, arithmetic and copies ran while one was open for 6% of the time, Pallas kernels for 7%

profile of v9, /device:TPU:6, one launch (start us, length us, event | category | flops | bytes accessed | tf_op | source)
XLA Modules:
  0.0 98.0 jit_solution(1692798564399687837)
XLA Ops:
  7.2 0.0 copy-start
  7.2 2.1 %shard_map.104 = (bf16[64,4,640]{2,1,0:T(4,128)(2,1)}, bf16[256,128]{1,0:T(8,128)(2,1)}) custom-call(s32[1,128]{1,0:T(1,128)} %bitcast.10, bf16[128,384]{1,0:T(8,128)(2,1)} %q_ref.2, bf16[128,256]{1,0:T(8,128)(2,1)} %kv_ref.2), custom_call_target="tpu_custom_call" | custom-call | flops 41943040 | bytes 491520 | tf_op jit(solution)/shard_map/pallas_call | solution.py:150
  9.3 14.0 %all-to-all-start = ((bf16[64,4,640]{2,1,0:T(4,128)(2,1)}), bf16[64,4,640]{2,1,0:T(4,128)(2,1)S(1)}, u32[]{:S(2)}, u32[]{:S(2)}) async-start(bf16[64,4,640]{2,1,0:T(4,128)(2,1)} %get-tuple-element.7), calls=%async_computation | async-start | bytes 655360 | tf_op jit(solution)/shard_map/all_to_all | solution.py:164
  23.3 0.0 reduce-scatter.2.cloned.1.call-start
  23.4 3.6 %shard_map.105 = bf16[256,384]{1,0:T(8,128)(2,1)} custom-call(bf16[256,384]{1,0:T(8,128)(2,1)} %q_ref.3, bf16[256,256]{1,0:T(8,128)(2,1)} %kv_ref.3, s32[1,3]{1,0:T(1,128)} %meta_ref.1, bf16[512,256]{1,0:T(8,128)(2,1)} %pool_ref.3), custom_call_target="tpu_custom_call" | custom-call | flops 301989888 | bytes 786444 | tf_op jit(solution)/shard_map/pallas_call | solution.py:117
  26.9 0.0 copy-done
  26.9 3.1 %convolution_convert_fusion = bf16[256,3072]{1,0:T(8,128)(2,1)} fusion(bf16[256,384]{1,0:T(8,128)(2,1)} %shard_map.105, bf16[384,3072]{1,0:T(8,128)(2,1)S(1)} %copy-done), kind=kOutput, calls=%fused_computation | convolution fusion | flops 604766208 | bytes 4128768 | tf_op jit(solution)/shard_map/dot_general | solution.py:129
  30.0 0.0 copy-start.2
  30.0 6.2 %all-to-all-done.recv_ref = bf16[64,4,640]{2,1,0:T(4,128)(2,1)S(1)} async-done(((bf16[64,4,640]{2,1,0:T(4,128)(2,1)}), bf16[64,4,640]{2,1,0:T(4,128)(2,1)S(1)}, u32[]{:S(2)}, u32[]{:S(2)}) %all-to-all-start) | async-done | bytes 327712 | tf_op jit(solution)/shard_map/all_to_all | solution.py:164
  36.2 0.0 copy-start.1
  36.2 0.0 reduce-scatter.2.cloned.1.call-update
  36.2 0.7 copy-done.1
  36.9 3.4 %shard_map.106 = bf16[64,4,384]{2,1,0:T(4,128)(2,1)} custom-call(bf16[64,4,640]{2,1,0:T(4,128)(2,1)} %copy-done.1, s32[2,256]{1,0:T(2,128)} %bitcast.9, bf16[512,256]{1,0:T(8,128)(2,1)} %pool_ref.3), custom_call_target="tpu_custom_call" | custom-call | flops 201326592 | bytes 788480 | tf_op jit(solution)/shard_map/pallas_call | solution.py:117
  40.3 16.7 %all_to_all.15 = bf16[64,4,384]{2,1,0:T(4,128)(2,1)S(1)} all-to-all(bf16[64,4,384]{2,1,0:T(4,128)(2,1)} %shard_map.106), channel_id=1, replica_groups=mesh['req'=64,'tp'=8] {'req'}, dimensions={0} | all-to-all | bytes 393216 | tf_op jit(solution)/shard_map/all_to_all | solution.py:174
  57.0 0.1 reshape.14
  57.1 0.0 copy-done.2
  57.1 1.6 %convolution_convert_fusion.1 = bf16[128,3072]{1,0:T(8,128)(2,1)} fusion(bf16[384,3072]{1,0:T(8,128)(2,1)S(1)} %copy-done, bf16[256,128]{1,0:T(8,128)(2,1)S(1)} %copy-done.2, bf16[256,384]{1,0:T(8,128)(2,1)S(1)} %reshape.14), kind=kOutput, calls=%fused_computation.1 | convolution fusion | flops 327598080 | bytes 3407872 | tf_op jit(solution)/shard_map/dot_general | solution.py:129
  58.7 31.7 %all_to_all.16 = bf16[8,16,3072]{2,1,0:T(8,128)(2,1)S(1)} all-to-all(bf16[8,16,3072]{2,1,0:T(8,128)(2,1)} %bitcast.8), channel_id=1, replica_groups=mesh['req'=64,'tp'=8] {'tp'}, dimensions={0} | all-to-all | bytes 1572864 | tf_op jit(solution)/shard_map/all_to_all | solution.py:183
  90.4 0.8 reduce_sum.12
  91.1 0.0 reduce-scatter.2.cloned.1.call-done
Async XLA Ops:
  7.2 19.8 %copy-start = (bf16[384,3072]{1,0:T(8,128)(2,1)S(1)}, bf16[384,3072]{1,0:T(8,128)(2,1)}, u32[]{:S(2)}) copy-start(bf16[384,3072]{1,0:T(8,128)(2,1)} %param.17) | copy-start | bytes 7077892
  9.3 26.9 %all-to-all-start = ((bf16[64,4,640]{2,1,0:T(4,128)(2,1)}), bf16[64,4,640]{2,1,0:T(4,128)(2,1)S(1)}, u32[]{:S(2)}, u32[]{:S(2)}) async-start(bf16[64,4,640]{2,1,0:T(4,128)(2,1)} %get-tuple-element.7), calls=%async_computation | async-start | bytes 655360 | tf_op jit(solution)/shard_map/all_to_all | solution.py:164
  23.3 67.8 %reduce-scatter.2.cloned.1.call-start = ((), (), s32[]{:S(2)}) async-start(), calls=%async_computation.4 | async-start | bytes 1769472 | tf_op jit(solution)/shard_map/reduce_scatter | solution.py:166
  30.0 27.1 %copy-start.2 = (bf16[256,128]{1,0:T(8,128)(2,1)S(1)}, bf16[256,128]{1,0:T(8,128)(2,1)}, u32[]{:S(2)}) copy-start(bf16[256,128]{1,0:T(8,128)(2,1)} %get-tuple-element.6) | copy-start | bytes 196612
  36.2 0.7 copy-start.1
Sparse Core Ops, SparseCore 0:
  36.3 47.1 reduce-scatter.1

commit v10 on v9

--- a/solution.py
+++ b/solution.py
@@ -41,11 +41,12 @@
             scores = jnp.where(visible, scores, MASKED_SCORE)
             own = jnp.sum(q.astype(jnp.float32) * own_key, axis=1, keepdims=True) * score_scale
             peak = jnp.maximum(jnp.max(scores, axis=1, keepdims=True), own)
-            weights = jnp.where(visible, jnp.exp(scores - peak), 0.0)
+            weights = jnp.exp(scores - peak)
             own_exp = jnp.exp(own - peak)
             total = jnp.sum(weights, axis=1, keepdims=True) + own_exp
-            weights = (weights / total).astype(jnp.bfloat16)
-            own_weight = (own_exp / total).astype(jnp.bfloat16).astype(jnp.float32)
+            inverse = 1.0 / total
+            weights = (weights * inverse).astype(jnp.bfloat16)
+            own_weight = (own_exp * inverse).astype(jnp.bfloat16).astype(jnp.float32)
             mixed = jnp.dot(weights, vals, preferred_element_type=jnp.float32) + own_weight * own_val
             outs.append(mixed.astype(jnp.bfloat16))
     out_ref[...] = jnp.concatenate(outs, axis=1).reshape(out_ref.shape)

time: 99 us -> 99.1 us (level)
  no operation moved by 1% of the time
where the time goes in v10:
time: 99.1 us; the launch traced here: 98 us
  blocking collectives  48.4 us (49%)
  starting transfers between devices  14.1 us (14%)
  between operations  14.1 us (14%)
  Pallas kernels  9.01 us (9%)
  waiting for transfers between devices  6.18 us (6%)
  matrix products  4.71 us (5%)
    all_to_all x1, blocking collectives, per_device(): lax.all_to_all(dec_part.reshape(tp_count, tok_rows // tp_count, dec_part....  31.7 us
    all_to_all x1, blocking collectives, per_device(): lax.all_to_all(slot_attn, 'req', split_axis=0, concat_axis=0, tiled=True)  16.7 us
    all_to_all x1, starting transfers between devices, per_device(): recv = lax.all_to_all(send, 'req', split_axis=0, concat_axis=0, tiled=True)  14 us
    pallas_call x2, Pallas kernels, vmem_call(): pl.pallas_call(kernel, out_shape=out_shape, in_specs=[pl.BlockSpec(memory...  6.91 us
    all_to_all x1, waiting for transfers between devices, per_device(): recv = lax.all_to_all(send, 'req', split_axis=0, concat_axis=0, tiled=True)  6.17 us
    dot_general x2, matrix products, term_maker(): return jnp.dot(rows_source, wo, preferred_element_type=jnp.float32)  4.71 us
    pallas_call x1, Pallas kernels, per_device(): pl.pallas_call(route_kernel, out_shape=(jax.ShapeDtypeStruct((groups, cap...  2.1 us
  transfers between devices with their start and end apart: 2, of which 1 were waited for; matrix products, arithmetic and copies ran while one was open for 6% of the time, Pallas kernels for 7%

profile of v10, /device:TPU:6, one launch (start us, length us, event | category | flops | bytes accessed | tf_op | source)
XLA Modules:
  0.0 98.0 jit_solution(4241680650026459847)
XLA Ops:
  7.2 0.0 copy-start
  7.2 2.1 %shard_map.104 = (bf16[64,4,640]{2,1,0:T(4,128)(2,1)}, bf16[256,128]{1,0:T(8,128)(2,1)}) custom-call(s32[1,128]{1,0:T(1,128)} %bitcast.10, bf16[128,384]{1,0:T(8,128)(2,1)} %q_ref.2, bf16[128,256]{1,0:T(8,128)(2,1)} %kv_ref.2), custom_call_target="tpu_custom_call" | custom-call | flops 41943040 | bytes 491520 | tf_op jit(solution)/shard_map/pallas_call | solution.py:151
  9.3 14.0 %all-to-all-start = ((bf16[64,4,640]{2,1,0:T(4,128)(2,1)}), bf16[64,4,640]{2,1,0:T(4,128)(2,1)S(1)}, u32[]{:S(2)}, u32[]{:S(2)}) async-start(bf16[64,4,640]{2,1,0:T(4,128)(2,1)} %get-tuple-element.7), calls=%async_computation | async-start | bytes 655360 | tf_op jit(solution)/shard_map/all_to_all | solution.py:165
  23.3 0.0 reduce-scatter.2.cloned.1.call-start
  23.4 3.6 %shard_map.105 = bf16[256,384]{1,0:T(8,128)(2,1)} custom-call(bf16[256,384]{1,0:T(8,128)(2,1)} %q_ref.3, bf16[256,256]{1,0:T(8,128)(2,1)} %kv_ref.3, s32[1,3]{1,0:T(1,128)} %meta_ref.1, bf16[512,256]{1,0:T(8,128)(2,1)} %pool_ref.3), custom_call_target="tpu_custom_call" | custom-call | flops 301989888 | bytes 786444 | tf_op jit(solution)/shard_map/pallas_call | solution.py:118
  26.9 0.0 copy-done
  26.9 3.1 %convolution_convert_fusion = bf16[256,3072]{1,0:T(8,128)(2,1)} fusion(bf16[256,384]{1,0:T(8,128)(2,1)} %shard_map.105, bf16[384,3072]{1,0:T(8,128)(2,1)S(1)} %copy-done), kind=kOutput, calls=%fused_computation | convolution fusion | flops 604766208 | bytes 4128768 | tf_op jit(solution)/shard_map/dot_general | solution.py:130
  30.0 0.0 copy-start.2
  30.0 6.2 %all-to-all-done.recv_ref = bf16[64,4,640]{2,1,0:T(4,128)(2,1)S(1)} async-done(((bf16[64,4,640]{2,1,0:T(4,128)(2,1)}), bf16[64,4,640]{2,1,0:T(4,128)(2,1)S(1)}, u32[]{:S(2)}, u32[]{:S(2)}) %all-to-all-start) | async-done | bytes 327712 | tf_op jit(solution)/shard_map/all_to_all | solution.py:165
  36.2 0.0 copy-start.1
  36.2 0.0 reduce-scatter.2.cloned.1.call-update
  36.2 0.7 copy-done.1
  36.9 3.3 %shard_map.106 = bf16[64,4,384]{2,1,0:T(4,128)(2,1)} custom-call(bf16[64,4,640]{2,1,0:T(4,128)(2,1)} %copy-done.1, s32[2,256]{1,0:T(2,128)} %bitcast.9, bf16[512,256]{1,0:T(8,128)(2,1)} %pool_ref.3), custom_call_target="tpu_custom_call" | custom-call | flops 201326592 | bytes 788480 | tf_op jit(solution)/shard_map/pallas_call | solution.py:118
  40.2 16.7 %all_to_all.15 = bf16[64,4,384]{2,1,0:T(4,128)(2,1)S(1)} all-to-all(bf16[64,4,384]{2,1,0:T(4,128)(2,1)} %shard_map.106), channel_id=1, replica_groups=mesh['req'=64,'tp'=8] {'req'}, dimensions={0} | all-to-all | bytes 393216 | tf_op jit(solution)/shard_map/all_to_all | solution.py:175
  57.0 0.1 reshape.14
  57.0 0.0 copy-done.2
  57.0 1.6 %convolution_convert_fusion.1 = bf16[128,3072]{1,0:T(8,128)(2,1)} fusion(bf16[384,3072]{1,0:T(8,128)(2,1)S(1)} %copy-done, bf16[256,128]{1,0:T(8,128)(2,1)S(1)} %copy-done.2, bf16[256,384]{1,0:T(8,128)(2,1)S(1)} %reshape.14), kind=kOutput, calls=%fused_computation.1 | convolution fusion | flops 327598080 | bytes 3407872 | tf_op jit(solution)/shard_map/dot_general | solution.py:130
  58.7 31.7 %all_to_all.16 = bf16[8,16,3072]{2,1,0:T(8,128)(2,1)S(1)} all-to-all(bf16[8,16,3072]{2,1,0:T(8,128)(2,1)} %bitcast.8), channel_id=1, replica_groups=mesh['req'=64,'tp'=8] {'tp'}, dimensions={0} | all-to-all | bytes 1572864 | tf_op jit(solution)/shard_map/all_to_all | solution.py:184
  90.4 0.8 reduce_sum.12
  91.1 0.0 reduce-scatter.2.cloned.1.call-done
Async XLA Ops:
  7.2 19.8 %copy-start = (bf16[384,3072]{1,0:T(8,128)(2,1)S(1)}, bf16[384,3072]{1,0:T(8,128)(2,1)}, u32[]{:S(2)}) copy-start(bf16[384,3072]{1,0:T(8,128)(2,1)} %param.17) | copy-start | bytes 7077892
  9.3 26.9 %all-to-all-start = ((bf16[64,4,640]{2,1,0:T(4,128)(2,1)}), bf16[64,4,640]{2,1,0:T(4,128)(2,1)S(1)}, u32[]{:S(2)}, u32[]{:S(2)}) async-start(bf16[64,4,640]{2,1,0:T(4,128)(2,1)} %get-tuple-element.7), calls=%async_computation | async-start | bytes 655360 | tf_op jit(solution)/shard_map/all_to_all | solution.py:165
  23.3 67.8 %reduce-scatter.2.cloned.1.call-start = ((), (), s32[]{:S(2)}) async-start(), calls=%async_computation.4 | async-start | bytes 1769472 | tf_op jit(solution)/shard_map/reduce_scatter | solution.py:167
  30.0 27.0 %copy-start.2 = (bf16[256,128]{1,0:T(8,128)(2,1)S(1)}, bf16[256,128]{1,0:T(8,128)(2,1)}, u32[]{:S(2)}) copy-start(bf16[256,128]{1,0:T(8,128)(2,1)} %get-tuple-element.6) | copy-start | bytes 196612
  36.2 0.7 copy-start.1
Sparse Core Ops, SparseCore 0:
  36.3 47.2 reduce-scatter.1

commit v11 on v9

--- a/solution.py
+++ b/solution.py
@@ -32,22 +32,27 @@
         vals = pool_ref[:, g * 2 * HD + HD : (g + 1) * 2 * HD]
         own_key = recv[:, q_width + g * 2 * HD : q_width + g * 2 * HD + HD].astype(jnp.float32)
         own_val = recv[:, q_width + g * 2 * HD + HD : q_width + (g + 1) * 2 * HD].astype(jnp.float32)
-        for h in range(QPK):
-            col = (g * QPK + h) * HD
-            q = recv[:, col : col + HD]
-            scores = lax.dot_general(
-                q, keys, (((1,), (1,)), ((), ())), preferred_element_type=jnp.float32
-            ) * score_scale
-            scores = jnp.where(visible, scores, MASKED_SCORE)
-            own = jnp.sum(q.astype(jnp.float32) * own_key, axis=1, keepdims=True) * score_scale
-            peak = jnp.maximum(jnp.max(scores, axis=1, keepdims=True), own)
-            weights = jnp.where(visible, jnp.exp(scores - peak), 0.0)
-            own_exp = jnp.exp(own - peak)
-            total = jnp.sum(weights, axis=1, keepdims=True) + own_exp
-            weights = (weights / total).astype(jnp.bfloat16)
-            own_weight = (own_exp / total).astype(jnp.bfloat16).astype(jnp.float32)
-            mixed = jnp.dot(weights, vals, preferred_element_type=jnp.float32) + own_weight * own_val
-            outs.append(mixed.astype(jnp.bfloat16))
+        first = g * QPK * HD
+        q = jnp.concatenate(
+            [recv[:, first + h * HD : first + (h + 1) * HD] for h in range(QPK)], axis=0
+        )
+        own_key = jnp.concatenate([own_key] * QPK, axis=0)
+        own_val = jnp.concatenate([own_val] * QPK, axis=0)
+        seen = jnp.concatenate([visible] * QPK, axis=0)
+        scores = lax.dot_general(
+            q, keys, (((1,), (1,)), ((), ())), preferred_element_type=jnp.float32
+        ) * score_scale
+        scores = jnp.where(seen, scores, MASKED_SCORE)
+        own = jnp.sum(q.astype(jnp.float32) * own_key, axis=1, keepdims=True) * score_scale
+        peak = jnp.maximum(jnp.max(scores, axis=1, keepdims=True), own)
+        weights = jnp.where(seen, jnp.exp(scores - peak), 0.0)
+        own_exp = jnp.exp(own - peak)
+        total = jnp.sum(weights, axis=1, keepdims=True) + own_exp
+        weights = (weights / total).astype(jnp.bfloat16)
+        own_weight = (own_exp / total).astype(jnp.bfloat16).astype(jnp.float32)
+        mixed = jnp.dot(weights, vals, preferred_element_type=jnp.float32) + own_weight * own_val
+        mixed = mixed.astype(jnp.bfloat16)
+        outs.extend(mixed[h * slot_rows : (h + 1) * slot_rows] for h in range(QPK))
     out_ref[...] = jnp.concatenate(outs, axis=1).reshape(out_ref.shape)
 
 

time: 99 us -> 99.3 us (level)
  no operation moved by 1% of the time
where the time goes in v11:
time: 99.3 us; the launch traced here: 98 us
  blocking collectives  48.6 us (49%)
  starting transfers between devices  14.1 us (14%)
  between operations  14.1 us (14%)
  Pallas kernels  8.9 us (9%)
  waiting for transfers between devices  6.18 us (6%)
  matrix products  4.72 us (5%)
    all_to_all x1, blocking collectives, per_device(): lax.all_to_all(dec_part.reshape(tp_count, tok_rows // tp_count, dec_part....  31.9 us
    all_to_all x1, blocking collectives, per_device(): lax.all_to_all(slot_attn, 'req', split_axis=0, concat_axis=0, tiled=True)  16.7 us
    all_to_all x1, starting transfers between devices, per_device(): recv = lax.all_to_all(send, 'req', split_axis=0, concat_axis=0, tiled=True)  14 us
    pallas_call x2, Pallas kernels, vmem_call(): pl.pallas_call(kernel, out_shape=out_shape, in_specs=[pl.BlockSpec(memory...  6.8 us
    all_to_all x1, waiting for transfers between devices, per_device(): recv = lax.all_to_all(send, 'req', split_axis=0, concat_axis=0, tiled=True)  6.17 us
    dot_general x2, matrix products, term_maker(): return jnp.dot(rows_source, wo, preferred_element_type=jnp.float32)  4.72 us
    pallas_call x1, Pallas kernels, per_device(): pl.pallas_call(route_kernel, out_shape=(jax.ShapeDtypeStruct((groups, cap...  2.1 us
  transfers between devices with their start and end apart: 2, of which 1 were waited for; matrix products, arithmetic and copies ran while one was open for 6% of the time, Pallas kernels for 7%

profile of v11, /device:TPU:6, one launch (start us, length us, event | category | flops | bytes accessed | tf_op | source)
XLA Modules:
  0.0 98.0 jit_solution(17529335677464398386)
XLA Ops:
  7.2 0.0 copy-start
  7.2 2.1 %shard_map.104 = (bf16[64,4,640]{2,1,0:T(4,128)(2,1)}, bf16[256,128]{1,0:T(8,128)(2,1)}) custom-call(s32[1,128]{1,0:T(1,128)} %bitcast.10, bf16[128,384]{1,0:T(8,128)(2,1)} %q_ref.2, bf16[128,256]{1,0:T(8,128)(2,1)} %kv_ref.2), custom_call_target="tpu_custom_call" | custom-call | flops 41943040 | bytes 491520 | tf_op jit(solution)/shard_map/pallas_call | solution.py:155
  9.3 14.0 %all-to-all-start = ((bf16[64,4,640]{2,1,0:T(4,128)(2,1)}), bf16[64,4,640]{2,1,0:T(4,128)(2,1)S(1)}, u32[]{:S(2)}, u32[]{:S(2)}) async-start(bf16[64,4,640]{2,1,0:T(4,128)(2,1)} %get-tuple-element.7), calls=%async_computation | async-start | bytes 655360 | tf_op jit(solution)/shard_map/all_to_all | solution.py:169
  23.3 0.0 reduce-scatter.2.cloned.1.call-start
  23.4 3.6 %shard_map.105 = bf16[256,384]{1,0:T(8,128)(2,1)} custom-call(bf16[256,384]{1,0:T(8,128)(2,1)} %q_ref.3, bf16[256,256]{1,0:T(8,128)(2,1)} %kv_ref.3, s32[1,3]{1,0:T(1,128)} %meta_ref.1, bf16[512,256]{1,0:T(8,128)(2,1)} %pool_ref.3), custom_call_target="tpu_custom_call" | custom-call | flops 301989888 | bytes 786444 | tf_op jit(solution)/shard_map/pallas_call | solution.py:122
  26.9 0.0 copy-done
  26.9 3.1 %convolution_convert_fusion = bf16[256,3072]{1,0:T(8,128)(2,1)} fusion(bf16[256,384]{1,0:T(8,128)(2,1)} %shard_map.105, bf16[384,3072]{1,0:T(8,128)(2,1)S(1)} %copy-done), kind=kOutput, calls=%fused_computation | convolution fusion | flops 604766208 | bytes 4128768 | tf_op jit(solution)/shard_map/dot_general | solution.py:134
  30.0 0.0 copy-start.2
  30.0 6.2 %all-to-all-done.recv_ref = bf16[64,4,640]{2,1,0:T(4,128)(2,1)S(1)} async-done(((bf16[64,4,640]{2,1,0:T(4,128)(2,1)}), bf16[64,4,640]{2,1,0:T(4,128)(2,1)S(1)}, u32[]{:S(2)}, u32[]{:S(2)}) %all-to-all-start) | async-done | bytes 327712 | tf_op jit(solution)/shard_map/all_to_all | solution.py:169
  36.2 0.0 copy-start.1
  36.2 0.0 reduce-scatter.2.cloned.1.call-update
  36.2 0.7 copy-done.1
  36.9 3.2 %shard_map.106 = bf16[64,4,384]{2,1,0:T(4,128)(2,1)} custom-call(bf16[64,4,640]{2,1,0:T(4,128)(2,1)} %copy-done.1, s32[2,256]{1,0:T(2,128)} %bitcast.9, bf16[512,256]{1,0:T(8,128)(2,1)} %pool_ref.3), custom_call_target="tpu_custom_call" | custom-call | flops 201326592 | bytes 788480 | tf_op jit(solution)/shard_map/pallas_call | solution.py:122
  40.1 16.7 %all_to_all.15 = bf16[64,4,384]{2,1,0:T(4,128)(2,1)S(1)} all-to-all(bf16[64,4,384]{2,1,0:T(4,128)(2,1)} %shard_map.106), channel_id=1, replica_groups=mesh['req'=64,'tp'=8] {'req'}, dimensions={0} | all-to-all | bytes 393216 | tf_op jit(solution)/shard_map/all_to_all | solution.py:179
  56.8 0.1 reshape.14
  56.9 0.0 copy-done.2
  56.9 1.6 %convolution_convert_fusion.1 = bf16[128,3072]{1,0:T(8,128)(2,1)} fusion(bf16[384,3072]{1,0:T(8,128)(2,1)S(1)} %copy-done, bf16[256,128]{1,0:T(8,128)(2,1)S(1)} %copy-done.2, bf16[256,384]{1,0:T(8,128)(2,1)S(1)} %reshape.14), kind=kOutput, calls=%fused_computation.1 | convolution fusion | flops 327598080 | bytes 3407872 | tf_op jit(solution)/shard_map/dot_general | solution.py:134
  58.5 31.9 %all_to_all.16 = bf16[8,16,3072]{2,1,0:T(8,128)(2,1)S(1)} all-to-all(bf16[8,16,3072]{2,1,0:T(8,128)(2,1)} %bitcast.8), channel_id=1, replica_groups=mesh['req'=64,'tp'=8] {'tp'}, dimensions={0} | all-to-all | bytes 1572864 | tf_op jit(solution)/shard_map/all_to_all | solution.py:188
  90.4 0.8 reduce_sum.12
  91.2 0.0 reduce-scatter.2.cloned.1.call-done
Async XLA Ops:
  7.2 19.8 %copy-start = (bf16[384,3072]{1,0:T(8,128)(2,1)S(1)}, bf16[384,3072]{1,0:T(8,128)(2,1)}, u32[]{:S(2)}) copy-start(bf16[384,3072]{1,0:T(8,128)(2,1)} %param.17) | copy-start | bytes 7077892
  9.3 26.9 %all-to-all-start = ((bf16[64,4,640]{2,1,0:T(4,128)(2,1)}), bf16[64,4,640]{2,1,0:T(4,128)(2,1)S(1)}, u32[]{:S(2)}, u32[]{:S(2)}) async-start(bf16[64,4,640]{2,1,0:T(4,128)(2,1)} %get-tuple-element.7), calls=%async_computation | async-start | bytes 655360 | tf_op jit(solution)/shard_map/all_to_all | solution.py:169
  23.3 67.9 %reduce-scatter.2.cloned.1.call-start = ((), (), s32[]{:S(2)}) async-start(), calls=%async_computation.4 | async-start | bytes 1769472 | tf_op jit(solution)/shard_map/reduce_scatter | solution.py:171
  30.0 26.9 %copy-start.2 = (bf16[256,128]{1,0:T(8,128)(2,1)S(1)}, bf16[256,128]{1,0:T(8,128)(2,1)}, u32[]{:S(2)}) copy-start(bf16[256,128]{1,0:T(8,128)(2,1)} %get-tuple-element.6) | copy-start | bytes 196612
  36.2 0.7 copy-start.1
Sparse Core Ops, SparseCore 0:
  36.3 47.1 reduce-scatter.1

commit v12 on v9

--- a/solution.py
+++ b/solution.py
@@ -14,7 +14,7 @@
 MASKED_SCORE = -1e30
 
 
-def decode_kernel(recv_ref, table_ref, pool_ref, out_ref):
+def decode_kernel(recv_ref, table_ref, pool_ref, keys_t_ref, out_ref):
     score_scale = 1.0 / math.sqrt(HD)
     slot_rows = recv_ref.shape[0] * recv_ref.shape[1]
     recv = recv_ref[...].reshape(slot_rows, recv_ref.shape[2])
@@ -28,16 +28,14 @@
     places = lax.broadcasted_iota(jnp.int32, (slot_rows, pool_ref.shape[0]), 1)
     visible = (places >= begins) & (places < ends)
     for g in range(kv_heads):
-        keys = pool_ref[:, g * 2 * HD : g * 2 * HD + HD]
+        keys_t = keys_t_ref[g * HD : (g + 1) * HD, :]
         vals = pool_ref[:, g * 2 * HD + HD : (g + 1) * 2 * HD]
         own_key = recv[:, q_width + g * 2 * HD : q_width + g * 2 * HD + HD].astype(jnp.float32)
         own_val = recv[:, q_width + g * 2 * HD + HD : q_width + (g + 1) * 2 * HD].astype(jnp.float32)
         for h in range(QPK):
             col = (g * QPK + h) * HD
             q = recv[:, col : col + HD]
-            scores = lax.dot_general(
-                q, keys, (((1,), (1,)), ((), ())), preferred_element_type=jnp.float32
-            ) * score_scale
+            scores = jnp.dot(q, keys_t, preferred_element_type=jnp.float32) * score_scale
             scores = jnp.where(visible, scores, MASKED_SCORE)
             own = jnp.sum(q.astype(jnp.float32) * own_key, axis=1, keepdims=True) * score_scale
             peak = jnp.maximum(jnp.max(scores, axis=1, keepdims=True), own)
@@ -51,7 +49,7 @@
     out_ref[...] = jnp.concatenate(outs, axis=1).reshape(out_ref.shape)
 
 
-def prefill_kernel(q_ref, kv_ref, meta_ref, pool_ref, out_ref):
+def prefill_kernel(q_ref, kv_ref, meta_ref, pool_ref, out_ref, keys_t_ref):
     score_scale = 1.0 / math.sqrt(HD)
     span_rows = q_ref.shape[0]
     pool_len = pool_ref.shape[0]
@@ -67,6 +65,7 @@
     live = lax.broadcasted_iota(jnp.int32, (span_rows, 1), 0) < meta[:, 2:3]
     for g in range(kv_heads):
         keys = pool_ref[:, g * 2 * HD : g * 2 * HD + HD]
+        keys_t_ref[g * HD : (g + 1) * HD, :] = jnp.transpose(keys)
         vals = pool_ref[:, g * 2 * HD + HD : (g + 1) * 2 * HD]
         span_keys = kv_ref[:, g * 2 * HD : g * 2 * HD + HD]
         span_vals = kv_ref[:, g * 2 * HD + HD : (g + 1) * 2 * HD]
@@ -138,13 +137,21 @@
     kv_width = dec_kv.shape[1]
 
     span_rows = pre_q.shape[0]
-    pre_attn = vmem_call(
+    kv_heads = pool.shape[1] // (2 * HD)
+    pre_attn, keys_t = pl.pallas_call(
         prefill_kernel,
-        jax.ShapeDtypeStruct((span_rows, q_width), jnp.bfloat16),
-        (pre_q, pre_kv, pre_meta, pool),
-        4 * span_rows * (pool.shape[0] + span_rows) * q_width,
-        span_rows * (pool.shape[0] + span_rows) * q_width // HD,
-    )
+        out_shape=(
+            jax.ShapeDtypeStruct((span_rows, q_width), jnp.bfloat16),
+            jax.ShapeDtypeStruct((kv_heads * HD, pool.shape[0]), jnp.bfloat16),
+        ),
+        in_specs=[pl.BlockSpec(memory_space=pltpu.VMEM)] * 4,
+        out_specs=(pl.BlockSpec(memory_space=pltpu.VMEM), pl.BlockSpec(memory_space=pltpu.VMEM)),
+        cost_estimate=pl.CostEstimate(
+            flops=4 * span_rows * (pool.shape[0] + span_rows) * q_width,
+            transcendentals=span_rows * (pool.shape[0] + span_rows) * q_width // HD,
+            bytes_accessed=2 * (pre_q.size + pre_kv.size + pool.size + span_rows * q_width),
+        ),
+    )(pre_q, pre_kv, pre_meta, pool)
     pre_part = term_maker(pre_attn, wo).astype(jnp.bfloat16)
 
     send, dispatch = pl.pallas_call(
@@ -167,7 +174,7 @@
     slot_attn = vmem_call(
         decode_kernel,
         jax.ShapeDtypeStruct((groups, capacity, q_width), jnp.bfloat16),
-        (recv, jnp.transpose(dec_table), pool),
+        (recv, jnp.transpose(dec_table), pool, keys_t),
         4 * slot_count * pool.shape[0] * q_width,
         slot_count * pool.shape[0] * q_width // HD,
     )

time: 99 us -> 98.9 us (level)
    pallas_call x0 -> x1, Pallas kernels: none -> 3.54 us  [per_device(): pl.pallas_call(prefill_kernel, out_shape=(jax.ShapeDtypeStruct((span_rows...]
    pallas_call x2 -> x1, Pallas kernels: 6.95 us -> 3.42 us  [vmem_call(): pl.pallas_call(kernel, out_shape=out_shape, in_specs=[pl.BlockSpec(memory...]
where the time goes in v12:
time: 98.9 us; the launch traced here: 98 us
  blocking collectives  48.4 us (49%)
  starting transfers between devices  14.1 us (14%)
  between operations  14.1 us (14%)
  Pallas kernels  9.06 us (9%)
  waiting for transfers between devices  6.21 us (6%)
  matrix products  4.71 us (5%)
    all_to_all x1, blocking collectives, per_device(): lax.all_to_all(dec_part.reshape(tp_count, tok_rows // tp_count, dec_part....  31.7 us
    all_to_all x1, blocking collectives, per_device(): lax.all_to_all(slot_attn, 'req', split_axis=0, concat_axis=0, tiled=True)  16.7 us
    all_to_all x1, starting transfers between devices, per_device(): recv = lax.all_to_all(send, 'req', split_axis=0, concat_axis=0, tiled=True)  14 us
    all_to_all x1, waiting for transfers between devices, per_device(): recv = lax.all_to_all(send, 'req', split_axis=0, concat_axis=0, tiled=True)  6.19 us
    dot_general x2, matrix products, term_maker(): return jnp.dot(rows_source, wo, preferred_element_type=jnp.float32)  4.71 us
    pallas_call x1, Pallas kernels, per_device(): pl.pallas_call(prefill_kernel, out_shape=(jax.ShapeDtypeStruct((span_rows...  3.54 us
    pallas_call x1, Pallas kernels, vmem_call(): pl.pallas_call(kernel, out_shape=out_shape, in_specs=[pl.BlockSpec(memory...  3.42 us
    pallas_call x1, Pallas kernels, per_device(): pl.pallas_call(route_kernel, out_shape=(jax.ShapeDtypeStruct((groups, cap...  2.1 us
  transfers between devices with their start and end apart: 2, of which 1 were waited for; matrix products, arithmetic and copies ran while one was open for 6% of the time, Pallas kernels for 7%

profile of v12, /device:TPU:6, one launch (start us, length us, event | category | flops | bytes accessed | tf_op | source)
XLA Modules:
  0.0 98.0 jit_solution(6658506347294928524)
XLA Ops:
  7.2 0.0 copy-start
  7.2 2.1 %shard_map.104 = (bf16[64,4,640]{2,1,0:T(4,128)(2,1)}, bf16[256,128]{1,0:T(8,128)(2,1)}) custom-call(s32[1,128]{1,0:T(1,128)} %bitcast.10, bf16[128,384]{1,0:T(8,128)(2,1)} %q_ref.2, bf16[128,256]{1,0:T(8,128)(2,1)} %kv_ref.2), custom_call_target="tpu_custom_call" | custom-call | flops 41943040 | bytes 491520 | tf_op jit(solution)/shard_map/pallas_call | solution.py:157
  9.3 14.0 %all-to-all-start = ((bf16[64,4,640]{2,1,0:T(4,128)(2,1)}), bf16[64,4,640]{2,1,0:T(4,128)(2,1)S(1)}, u32[]{:S(2)}, u32[]{:S(2)}) async-start(bf16[64,4,640]{2,1,0:T(4,128)(2,1)} %get-tuple-element.10), calls=%async_computation | async-start | bytes 655360 | tf_op jit(solution)/shard_map/all_to_all | solution.py:171
  23.3 0.0 reduce-scatter.2.cloned.1.call-start
  23.4 3.5 %shard_map.105 = (bf16[256,384]{1,0:T(8,128)(2,1)}, bf16[128,512]{1,0:T(8,128)(2,1)}) custom-call(bf16[256,384]{1,0:T(8,128)(2,1)} %q_ref.3, bf16[256,256]{1,0:T(8,128)(2,1)} %kv_ref.3, s32[1,3]{1,0:T(1,128)} %meta_ref.1, bf16[512,256]{1,0:T(8,128)(2,1)} %pool_ref.3), custom_call_target="tpu_custom_call" | custom-call | flops 301989888 | bytes 786432 | tf_op jit(solution)/shard_map/pallas_call | solution.py:141
  26.9 0.0 copy-done
  26.9 3.1 %convolution_convert_fusion = bf16[256,3072]{1,0:T(8,128)(2,1)} fusion(bf16[256,384]{1,0:T(8,128)(2,1)} %get-tuple-element.9, bf16[384,3072]{1,0:T(8,128)(2,1)S(1)} %copy-done), kind=kOutput, calls=%fused_computation | convolution fusion | flops 604766208 | bytes 4128768 | tf_op jit(solution)/shard_map/dot_general | solution.py:128
  30.0 0.0 copy-start.2
  30.0 6.2 %all-to-all-done.recv_ref = bf16[64,4,640]{2,1,0:T(4,128)(2,1)S(1)} async-done(((bf16[64,4,640]{2,1,0:T(4,128)(2,1)}), bf16[64,4,640]{2,1,0:T(4,128)(2,1)S(1)}, u32[]{:S(2)}, u32[]{:S(2)}) %all-to-all-start) | async-done | bytes 327712 | tf_op jit(solution)/shard_map/all_to_all | solution.py:171
  36.2 0.0 copy-start.1
  36.2 0.0 reduce-scatter.2.cloned.1.call-update
  36.2 0.7 copy-done.1
  36.9 3.4 %shard_map.106 = bf16[64,4,384]{2,1,0:T(4,128)(2,1)} custom-call(bf16[64,4,640]{2,1,0:T(4,128)(2,1)} %copy-done.1, s32[2,256]{1,0:T(2,128)} %bitcast.9, bf16[512,256]{1,0:T(8,128)(2,1)} %pool_ref.3, bf16[128,512]{1,0:T(8,128)(2,1)} %get-tuple-element.12.keys_t_ref), custom_call_target="tpu_custom_call" | custom-call | flops 201326592 | bytes 919552 | tf_op jit(solution)/shard_map/pallas_call | solution.py:116
  40.3 16.7 %all_to_all.15 = bf16[64,4,384]{2,1,0:T(4,128)(2,1)S(1)} all-to-all(bf16[64,4,384]{2,1,0:T(4,128)(2,1)} %shard_map.106), channel_id=1, replica_groups=mesh['req'=64,'tp'=8] {'req'}, dimensions={0} | all-to-all | bytes 393216 | tf_op jit(solution)/shard_map/all_to_all | solution.py:181
  57.0 0.1 reshape.14
  57.1 0.0 copy-done.2
  57.1 1.6 %convolution_convert_fusion.1 = bf16[128,3072]{1,0:T(8,128)(2,1)} fusion(bf16[384,3072]{1,0:T(8,128)(2,1)S(1)} %copy-done, bf16[256,128]{1,0:T(8,128)(2,1)S(1)} %copy-done.2, bf16[256,384]{1,0:T(8,128)(2,1)S(1)} %reshape.14), kind=kOutput, calls=%fused_computation.1 | convolution fusion | flops 327598080 | bytes 3407872 | tf_op jit(solution)/shard_map/dot_general | solution.py:128
  58.7 31.7 %all_to_all.16 = bf16[8,16,3072]{2,1,0:T(8,128)(2,1)S(1)} all-to-all(bf16[8,16,3072]{2,1,0:T(8,128)(2,1)} %bitcast.8), channel_id=1, replica_groups=mesh['req'=64,'tp'=8] {'tp'}, dimensions={0} | all-to-all | bytes 1572864 | tf_op jit(solution)/shard_map/all_to_all | solution.py:190
  90.4 0.8 reduce_sum.12
  91.2 0.0 reduce-scatter.2.cloned.1.call-done
Async XLA Ops:
  7.2 19.7 %copy-start = (bf16[384,3072]{1,0:T(8,128)(2,1)S(1)}, bf16[384,3072]{1,0:T(8,128)(2,1)}, u32[]{:S(2)}) copy-start(bf16[384,3072]{1,0:T(8,128)(2,1)} %param.17) | copy-start | bytes 7077892
  9.3 26.9 %all-to-all-start = ((bf16[64,4,640]{2,1,0:T(4,128)(2,1)}), bf16[64,4,640]{2,1,0:T(4,128)(2,1)S(1)}, u32[]{:S(2)}, u32[]{:S(2)}) async-start(bf16[64,4,640]{2,1,0:T(4,128)(2,1)} %get-tuple-element.10), calls=%async_computation | async-start | bytes 655360 | tf_op jit(solution)/shard_map/all_to_all | solution.py:171
  23.3 67.9 %reduce-scatter.2.cloned.1.call-start = ((), (), s32[]{:S(2)}) async-start(), calls=%async_computation.4 | async-start | bytes 1769472 | tf_op jit(solution)/shard_map/reduce_scatter | solution.py:173
  30.0 27.1 %copy-start.2 = (bf16[256,128]{1,0:T(8,128)(2,1)S(1)}, bf16[256,128]{1,0:T(8,128)(2,1)}, u32[]{:S(2)}) copy-start(bf16[256,128]{1,0:T(8,128)(2,1)} %get-tuple-element.8) | copy-start | bytes 196612
  36.2 0.7 copy-start.1
Sparse Core Ops, SparseCore 0:
  36.3 47.1 reduce-scatter.1

commit v13 on v9

--- a/solution.py
+++ b/solution.py
@@ -167,7 +167,7 @@
     slot_attn = vmem_call(
         decode_kernel,
         jax.ShapeDtypeStruct((groups, capacity, q_width), jnp.bfloat16),
-        (recv, jnp.transpose(dec_table), pool),
+        (pltpu.with_memory_space_constraint(recv, pltpu.VMEM), jnp.transpose(dec_table), pool),
         4 * slot_count * pool.shape[0] * q_width,
         slot_count * pool.shape[0] * q_width // HD,
     )

time: 99 us -> 99.4 us (level)
  no operation moved by 1% of the time
where the time goes in v13:
time: 99.4 us; the launch traced here: 98.1 us
  blocking collectives  49.3 us (50%)
  starting transfers between devices  14.1 us (14%)
  between operations  14.1 us (14%)
  Pallas kernels  8.99 us (9%)
  waiting for transfers between devices  6.18 us (6%)
  matrix products  4.71 us (5%)
    all_to_all x1, blocking collectives, per_device(): lax.all_to_all(dec_part.reshape(tp_count, tok_rows // tp_count, dec_part....  32.5 us
    all_to_all x1, blocking collectives, per_device(): lax.all_to_all(slot_attn, 'req', split_axis=0, concat_axis=0, tiled=True)  16.7 us
    all_to_all x1, starting transfers between devices, per_device(): recv = lax.all_to_all(send, 'req', split_axis=0, concat_axis=0, tiled=True)  14 us
    pallas_call x2, Pallas kernels, vmem_call(): pl.pallas_call(kernel, out_shape=out_shape, in_specs=[pl.BlockSpec(memory...  6.89 us
    all_to_all x1, waiting for transfers between devices, per_device(): recv = lax.all_to_all(send, 'req', split_axis=0, concat_axis=0, tiled=True)  6.16 us
    dot_general x2, matrix products, term_maker(): return jnp.dot(rows_source, wo, preferred_element_type=jnp.float32)  4.71 us
    pallas_call x1, Pallas kernels, per_device(): pl.pallas_call(route_kernel, out_shape=(jax.ShapeDtypeStruct((groups, cap...  2.1 us
  transfers between devices with their start and end apart: 2, of which 1 were waited for; matrix products, arithmetic and copies ran while one was open for 6% of the time, Pallas kernels for 7%

profile of v13, /device:TPU:6, one launch (start us, length us, event | category | flops | bytes accessed | tf_op | source)
XLA Modules:
  0.0 98.1 jit_solution(17598835399476875561)
XLA Ops:
  7.2 0.0 copy-start
  7.2 2.1 %shard_map.104 = (bf16[64,4,640]{2,1,0:T(4,128)(2,1)}, bf16[256,128]{1,0:T(8,128)(2,1)}) custom-call(s32[1,128]{1,0:T(1,128)} %bitcast.10, bf16[128,384]{1,0:T(8,128)(2,1)} %q_ref.2, bf16[128,256]{1,0:T(8,128)(2,1)} %kv_ref.2), custom_call_target="tpu_custom_call" | custom-call | flops 41943040 | bytes 491520 | tf_op jit(solution)/shard_map/pallas_call | solution.py:150
  9.3 14.0 %all-to-all-start = ((bf16[64,4,640]{2,1,0:T(4,128)(2,1)}), bf16[64,4,640]{2,1,0:T(4,128)(2,1)S(1)}, u32[]{:S(2)}, u32[]{:S(2)}) async-start(bf16[64,4,640]{2,1,0:T(4,128)(2,1)} %get-tuple-element.7), calls=%async_computation | async-start | bytes 655360 | tf_op jit(solution)/shard_map/all_to_all | solution.py:164
  23.3 0.0 reduce-scatter.2.cloned.1.call-start
  23.4 3.6 %shard_map.105 = bf16[256,384]{1,0:T(8,128)(2,1)} custom-call(bf16[256,384]{1,0:T(8,128)(2,1)} %q_ref.3, bf16[256,256]{1,0:T(8,128)(2,1)} %kv_ref.3, s32[1,3]{1,0:T(1,128)} %meta_ref.1, bf16[512,256]{1,0:T(8,128)(2,1)} %pool_ref.3), custom_call_target="tpu_custom_call" | custom-call | flops 301989888 | bytes 786444 | tf_op jit(solution)/shard_map/pallas_call | solution.py:117
  26.9 0.0 copy-done
  26.9 3.1 %convolution_convert_fusion = bf16[256,3072]{1,0:T(8,128)(2,1)} fusion(bf16[256,384]{1,0:T(8,128)(2,1)} %shard_map.105, bf16[384,3072]{1,0:T(8,128)(2,1)S(1)} %copy-done), kind=kOutput, calls=%fused_computation | convolution fusion | flops 604766208 | bytes 4128768 | tf_op jit(solution)/shard_map/dot_general | solution.py:129
  30.0 0.0 copy-start.1
  30.0 6.2 %all-to-all-done.recv_ref = bf16[64,4,640]{2,1,0:T(4,128)(2,1)S(1)} async-done(((bf16[64,4,640]{2,1,0:T(4,128)(2,1)}), bf16[64,4,640]{2,1,0:T(4,128)(2,1)S(1)}, u32[]{:S(2)}, u32[]{:S(2)}) %all-to-all-start) | async-done | bytes 327712 | tf_op jit(solution)/shard_map/all_to_all | solution.py:164
  36.2 0.0 reduce-scatter.2.cloned.1.call-update
  36.2 3.3 %shard_map.106 = bf16[64,4,384]{2,1,0:T(4,128)(2,1)} custom-call(bf16[64,4,640]{2,1,0:T(4,128)(2,1)S(1)} %all-to-all-done.recv_ref, s32[2,256]{1,0:T(2,128)} %bitcast.9, bf16[512,256]{1,0:T(8,128)(2,1)} %pool_ref.3), custom_call_target="tpu_custom_call" | custom-call | flops 201326592 | bytes 788480 | tf_op jit(solution)/shard_map/pallas_call | solution.py:117
  39.5 16.7 %all_to_all.15 = bf16[64,4,384]{2,1,0:T(4,128)(2,1)S(1)} all-to-all(bf16[64,4,384]{2,1,0:T(4,128)(2,1)} %shard_map.106), channel_id=1, replica_groups=mesh['req'=64,'tp'=8] {'req'}, dimensions={0} | all-to-all | bytes 393216 | tf_op jit(solution)/shard_map/all_to_all | solution.py:174
  56.2 0.1 reshape.14
  56.3 0.0 copy-done.1
  56.3 1.6 %convolution_convert_fusion.1 = bf16[128,3072]{1,0:T(8,128)(2,1)} fusion(bf16[384,3072]{1,0:T(8,128)(2,1)S(1)} %copy-done, bf16[256,128]{1,0:T(8,128)(2,1)S(1)} %copy-done.1, bf16[256,384]{1,0:T(8,128)(2,1)S(1)} %reshape.14), kind=kOutput, calls=%fused_computation.1 | convolution fusion | flops 327598080 | bytes 3407872 | tf_op jit(solution)/shard_map/dot_general | solution.py:129
  57.9 32.5 %all_to_all.16 = bf16[8,16,3072]{2,1,0:T(8,128)(2,1)S(1)} all-to-all(bf16[8,16,3072]{2,1,0:T(8,128)(2,1)} %bitcast.8), channel_id=1, replica_groups=mesh['req'=64,'tp'=8] {'tp'}, dimensions={0} | all-to-all | bytes 1572864 | tf_op jit(solution)/shard_map/all_to_all | solution.py:183
  90.5 0.8 reduce_sum.12
  91.2 0.0 reduce-scatter.2.cloned.1.call-done
Async XLA Ops:
  7.2 19.8 %copy-start = (bf16[384,3072]{1,0:T(8,128)(2,1)S(1)}, bf16[384,3072]{1,0:T(8,128)(2,1)}, u32[]{:S(2)}) copy-start(bf16[384,3072]{1,0:T(8,128)(2,1)} %param.17) | copy-start | bytes 7077892
  9.3 26.9 %all-to-all-start = ((bf16[64,4,640]{2,1,0:T(4,128)(2,1)}), bf16[64,4,640]{2,1,0:T(4,128)(2,1)S(1)}, u32[]{:S(2)}, u32[]{:S(2)}) async-start(bf16[64,4,640]{2,1,0:T(4,128)(2,1)} %get-tuple-element.7), calls=%async_computation | async-start | bytes 655360 | tf_op jit(solution)/shard_map/all_to_all | solution.py:164
  23.3 67.9 %reduce-scatter.2.cloned.1.call-start = ((), (), s32[]{:S(2)}) async-start(), calls=%async_computation.4 | async-start | bytes 1769472 | tf_op jit(solution)/shard_map/reduce_scatter | solution.py:166
  30.0 26.3 %copy-start.1 = (bf16[256,128]{1,0:T(8,128)(2,1)S(1)}, bf16[256,128]{1,0:T(8,128)(2,1)}, u32[]{:S(2)}) copy-start(bf16[256,128]{1,0:T(8,128)(2,1)} %get-tuple-element.6) | copy-start | bytes 196612
Sparse Core Ops, SparseCore 0:
  36.3 47.6 reduce-scatter.1

commit v14 on v9

--- a/solution.py
+++ b/solution.py
@@ -92,10 +92,10 @@
             out_ref[:, col : col + HD] = jnp.where(live, mixed, 0.0).astype(jnp.bfloat16)
 
 
-def route_kernel(owner_ref, q_ref, kv_ref, send_ref, dispatch_ref):
+def route_kernel(owner_ref, q_ref, kv_ref, send_ref):
     tok_rows = q_ref.shape[0]
-    slot_count = dispatch_ref.shape[0]
-    capacity = slot_count // send_ref.shape[0]
+    capacity = send_ref.shape[1]
+    slot_count = send_ref.shape[0] * capacity
     owner_row = owner_ref[...]
     owner_col = jnp.transpose(jnp.broadcast_to(owner_row, (tok_rows, tok_rows)))
     earlier = lax.broadcasted_iota(jnp.int32, (tok_rows, tok_rows), 0) < lax.broadcasted_iota(
@@ -106,7 +106,6 @@
     slot_ids = owner_row * capacity + ranking
     slots = lax.broadcasted_iota(jnp.int32, (slot_count, tok_rows), 0)
     dispatch = (slots == slot_ids).astype(jnp.bfloat16)
-    dispatch_ref[...] = dispatch
     rows = jnp.concatenate([q_ref[...], kv_ref[...]], axis=1)
     send = jnp.dot(dispatch, rows, preferred_element_type=jnp.float32).astype(jnp.bfloat16)
     send_ref[...] = send.reshape(send_ref.shape)
@@ -147,20 +146,21 @@
     )
     pre_part = term_maker(pre_attn, wo).astype(jnp.bfloat16)
 
-    send, dispatch = pl.pallas_call(
+    send = pl.pallas_call(
         route_kernel,
-        out_shape=(
-            jax.ShapeDtypeStruct((groups, capacity, q_width + kv_width), jnp.bfloat16),
-            jax.ShapeDtypeStruct((slot_count, tok_rows), jnp.bfloat16),
-        ),
+        out_shape=jax.ShapeDtypeStruct((groups, capacity, q_width + kv_width), jnp.bfloat16),
         in_specs=[pl.BlockSpec(memory_space=pltpu.VMEM)] * 3,
-        out_specs=(pl.BlockSpec(memory_space=pltpu.VMEM), pl.BlockSpec(memory_space=pltpu.VMEM)),
+        out_specs=pl.BlockSpec(memory_space=pltpu.VMEM),
         cost_estimate=pl.CostEstimate(
             flops=2 * slot_count * tok_rows * (q_width + kv_width),
             transcendentals=0,
             bytes_accessed=2 * (tok_rows + slot_count) * (q_width + kv_width),
         ),
     )(dec_owner.reshape(1, tok_rows), dec_q, dec_kv)
+    tok_iota = lax.iota(jnp.int32, tok_rows)
+    earlier_same = (dec_owner[:, None] == dec_owner[None, :]) & (tok_iota[None, :] < tok_iota[:, None])
+    slot_ids = dec_owner * capacity + jnp.sum(earlier_same.astype(jnp.int32), axis=1)
+    dispatch = (slot_ids[None, :] == lax.iota(jnp.int32, slot_count)[:, None]).astype(jnp.bfloat16)
     recv = lax.all_to_all(send, "req", split_axis=0, concat_axis=0, tiled=True)
     pre_part, recv = lax.optimization_barrier((pre_part, recv))
     pre_out = lax.psum_scatter(pre_part, "tp", scatter_dimension=0, tiled=True)

time: 99 us -> 99 us (level)
  blocking collectives: 48.4 us -> 31.7 us
  waiting for transfers between devices: 6.18 us -> 16.2 us
  starting transfers between devices: 14.1 us -> 20.6 us
    all_to_all x1 -> x0, blocking collectives: 16.7 us -> none  [per_device(): lax.all_to_all(slot_attn, 'req', split_axis=0, concat_axis=0, tiled=True)]
    all_to_all x0 -> x1, waiting for transfers between devices: none -> 10 us  [per_device(): lax.all_to_all(slot_attn, 'req', split_axis=0, concat_axis=0, tiled=True)]
    all_to_all x0 -> x1, starting transfers between devices: none -> 6.53 us  [per_device(): lax.all_to_all(slot_attn, 'req', split_axis=0, concat_axis=0, tiled=True)]
  transfers between devices with their start and end apart: 2 -> 3, of which waited for: 1 -> 2; matrix products, arithmetic and copies ran while one was open for 6% -> 6% of each run, Pallas kernels for 7% -> 7%
where the time goes in v14:
time: 99 us; the launch traced here: 98 us
  blocking collectives  31.7 us (32%)
  starting transfers between devices  20.6 us (21%)
  waiting for transfers between devices  16.2 us (16%)
  between operations  14.1 us (14%)
  Pallas kernels  9.06 us (9%)
  matrix products  4.71 us (5%)
    all_to_all x1, blocking collectives, per_device(): lax.all_to_all(dec_part.reshape(tp_count, tok_rows // tp_count, dec_part....  31.7 us
    all_to_all x1, starting transfers between devices, per_device(): recv = lax.all_to_all(send, 'req', split_axis=0, concat_axis=0, tiled=True)  14 us
    all_to_all x1, waiting for transfers between devices, per_device(): lax.all_to_all(slot_attn, 'req', split_axis=0, concat_axis=0, tiled=True)  10 us
    pallas_call x2, Pallas kernels, vmem_call(): pl.pallas_call(kernel, out_shape=out_shape, in_specs=[pl.BlockSpec(memory...  6.96 us
    all_to_all x1, starting transfers between devices, per_device(): lax.all_to_all(slot_attn, 'req', split_axis=0, concat_axis=0, tiled=True)  6.53 us
    all_to_all x1, waiting for transfers between devices, per_device(): recv = lax.all_to_all(send, 'req', split_axis=0, concat_axis=0, tiled=True)  6.17 us
    dot_general x2, matrix products, term_maker(): return jnp.dot(rows_source, wo, preferred_element_type=jnp.float32)  4.71 us
    pallas_call x1, Pallas kernels, per_device(): pl.pallas_call(route_kernel, out_shape=jax.ShapeDtypeStruct((groups, capa...  2.1 us
  transfers between devices with their start and end apart: 3, of which 2 were waited for; matrix products, arithmetic and copies ran while one was open for 6% of the time, Pallas kernels for 7%

profile of v14, /device:TPU:6, one launch (start us, length us, event | category | flops | bytes accessed | tf_op | source)
XLA Modules:
  0.0 98.0 jit_solution(11809172046584261917)
XLA Ops:
  7.2 0.0 copy-start
  7.2 2.1 %shard_map.105 = bf16[64,4,640]{2,1,0:T(4,128)(2,1)} custom-call(s32[1,128]{1,0:T(1,128)} %bitcast.9, bf16[128,384]{1,0:T(8,128)(2,1)} %q_ref.3, bf16[128,256]{1,0:T(8,128)(2,1)} %kv_ref.3), custom_call_target="tpu_custom_call" | custom-call | flops 41943040 | bytes 491520 | tf_op jit(solution)/shard_map/pallas_call | solution.py:149
  9.3 14.0 %all-to-all-start = ((bf16[64,4,640]{2,1,0:T(4,128)(2,1)}), bf16[64,4,640]{2,1,0:T(4,128)(2,1)S(1)}, u32[]{:S(2)}, u32[]{:S(2)}) async-start(bf16[64,4,640]{2,1,0:T(4,128)(2,1)} %shard_map.105), calls=%async_computation | async-start | bytes 655360 | tf_op jit(solution)/shard_map/all_to_all | solution.py:164
  23.3 0.0 reduce-scatter.2.cloned.1.call-start
  23.4 3.6 %shard_map.104 = bf16[256,384]{1,0:T(8,128)(2,1)} custom-call(bf16[256,384]{1,0:T(8,128)(2,1)} %q_ref.2, bf16[256,256]{1,0:T(8,128)(2,1)} %kv_ref.2, s32[1,3]{1,0:T(1,128)} %meta_ref.1, bf16[512,256]{1,0:T(8,128)(2,1)} %pool_ref.3), custom_call_target="tpu_custom_call" | custom-call | flops 301989888 | bytes 786444 | tf_op jit(solution)/shard_map/pallas_call | solution.py:116
  26.9 0.0 copy-done
  26.9 3.1 %convolution_convert_fusion = bf16[256,3072]{1,0:T(8,128)(2,1)} fusion(bf16[256,384]{1,0:T(8,128)(2,1)} %shard_map.104, bf16[384,3072]{1,0:T(8,128)(2,1)S(1)} %copy-done), kind=kOutput, calls=%fused_computation | convolution fusion | flops 604766208 | bytes 4128768 | tf_op jit(solution)/shard_map/dot_general | solution.py:128
  30.0 0.0 copy-start.2
  30.0 6.2 %all-to-all-done.recv_ref = bf16[64,4,640]{2,1,0:T(4,128)(2,1)S(1)} async-done(((bf16[64,4,640]{2,1,0:T(4,128)(2,1)}), bf16[64,4,640]{2,1,0:T(4,128)(2,1)S(1)}, u32[]{:S(2)}, u32[]{:S(2)}) %all-to-all-start) | async-done | bytes 327712 | tf_op jit(solution)/shard_map/all_to_all | solution.py:164
  36.2 0.0 copy-start.1
  36.2 0.0 reduce-scatter.2.cloned.1.call-update
  36.2 0.7 copy-done.1
  36.9 3.4 %shard_map.106 = bf16[64,4,384]{2,1,0:T(4,128)(2,1)} custom-call(bf16[64,4,640]{2,1,0:T(4,128)(2,1)} %copy-done.1, s32[2,256]{1,0:T(2,128)} %bitcast.8, bf16[512,256]{1,0:T(8,128)(2,1)} %pool_ref.3), custom_call_target="tpu_custom_call" | custom-call | flops 201326592 | bytes 788480 | tf_op jit(solution)/shard_map/pallas_call | solution.py:116
  40.3 6.5 %all-to-all-start.1 = ((bf16[64,4,384]{2,1,0:T(4,128)(2,1)}), bf16[64,4,384]{2,1,0:T(4,128)(2,1)S(1)}, u32[]{:S(2)}, u32[]{:S(2)}) async-start(bf16[64,4,384]{2,1,0:T(4,128)(2,1)} %shard_map.106), calls=%async_computation.1 | async-start | bytes 393216 | tf_op jit(solution)/shard_map/all_to_all | solution.py:174
  46.8 0.0 copy-done.2
  46.8 0.2 convert_reduce_fusion
  47.0 10.0 %all-to-all-done.1 = bf16[64,4,384]{2,1,0:T(4,128)(2,1)S(1)} async-done(((bf16[64,4,384]{2,1,0:T(4,128)(2,1)}), bf16[64,4,384]{2,1,0:T(4,128)(2,1)S(1)}, u32[]{:S(2)}, u32[]{:S(2)}) %all-to-all-start.1) | async-done | bytes 196640 | tf_op jit(solution)/shard_map/all_to_all | solution.py:174
  57.0 0.1 reshape.14
  57.1 1.6 %convolution_convert_fusion.1 = bf16[128,3072]{1,0:T(8,128)(2,1)} fusion(bf16[384,3072]{1,0:T(8,128)(2,1)S(1)} %copy-done, bf16[256,384]{1,0:T(8,128)(2,1)S(1)} %reshape.14, s32[128]{0:T(128)S(1)} %multiply_add_fusion), kind=kOutput, calls=%fused_computation.1 | convolution fusion | flops 327630848 | bytes 3342848 | tf_op jit(solution)/shard_map/dot_general | solution.py:128
  58.7 31.7 %all_to_all.15 = bf16[8,16,3072]{2,1,0:T(8,128)(2,1)S(1)} all-to-all(bf16[8,16,3072]{2,1,0:T(8,128)(2,1)} %bitcast.7), channel_id=1, replica_groups=mesh['req'=64,'tp'=8] {'tp'}, dimensions={0} | all-to-all | bytes 1572864 | tf_op jit(solution)/shard_map/all_to_all | solution.py:183
  90.4 0.8 reduce_sum.22
  91.2 0.0 reduce-scatter.2.cloned.1.call-done
  (1 shorter events, 0.0 us)
Async XLA Ops:
  7.2 19.8 %copy-start = (bf16[384,3072]{1,0:T(8,128)(2,1)S(1)}, bf16[384,3072]{1,0:T(8,128)(2,1)}, u32[]{:S(2)}) copy-start(bf16[384,3072]{1,0:T(8,128)(2,1)} %param.17) | copy-start | bytes 7077892
  9.3 26.9 %all-to-all-start = ((bf16[64,4,640]{2,1,0:T(4,128)(2,1)}), bf16[64,4,640]{2,1,0:T(4,128)(2,1)S(1)}, u32[]{:S(2)}, u32[]{:S(2)}) async-start(bf16[64,4,640]{2,1,0:T(4,128)(2,1)} %shard_map.105), calls=%async_computation | async-start | bytes 655360 | tf_op jit(solution)/shard_map/all_to_all | solution.py:164
  23.3 67.9 %reduce-scatter.2.cloned.1.call-start = ((), (), s32[]{:S(2)}) async-start(), calls=%async_computation.4 | async-start | bytes 1769472 | tf_op jit(solution)/shard_map/reduce_scatter | solution.py:166
  30.0 16.8 %copy-start.2 = (s32[128]{0:T(128)S(1)}, s32[128]{0:T(128)}, u32[]{:S(2)}) copy-start(s32[128]{0:T(128)} %param.11) | copy-start | bytes 1540
  36.2 0.7 copy-start.1
  40.3 16.7 %all-to-all-start.1 = ((bf16[64,4,384]{2,1,0:T(4,128)(2,1)}), bf16[64,4,384]{2,1,0:T(4,128)(2,1)S(1)}, u32[]{:S(2)}, u32[]{:S(2)}) async-start(bf16[64,4,384]{2,1,0:T(4,128)(2,1)} %shard_map.106), calls=%async_computation.1 | async-start | bytes 393216 | tf_op jit(solution)/shard_map/all_to_all | solution.py:174
Sparse Core Ops, SparseCore 0:
  36.3 47.1 reduce-scatter.1

commit v15 on v9

--- a/solution.py
+++ b/solution.py
@@ -163,7 +163,7 @@
     )(dec_owner.reshape(1, tok_rows), dec_q, dec_kv)
     recv = lax.all_to_all(send, "req", split_axis=0, concat_axis=0, tiled=True)
     pre_part, recv = lax.optimization_barrier((pre_part, recv))
-    pre_out = lax.psum_scatter(pre_part, "tp", scatter_dimension=0, tiled=True)
+    pre_out = lax.psum_scatter(pre_part, ("tpa", "tpb"), scatter_dimension=0, tiled=True)
     slot_attn = vmem_call(
         decode_kernel,
         jax.ShapeDtypeStruct((groups, capacity, q_width), jnp.bfloat16),
@@ -178,35 +178,42 @@
         (((0,), (0,)), ((), ())),
         preferred_element_type=jnp.float32,
     ).astype(jnp.bfloat16)
-    tp_count = lax.axis_size("tp")
+    tp_count = lax.axis_size(("tpa", "tpb"))
     dec_part = term_maker(dec_attn, wo).astype(jnp.bfloat16)
-    pieces = lax.all_to_all(
-        dec_part.reshape(tp_count, tok_rows // tp_count, dec_part.shape[1]),
-        "tp",
-        split_axis=0,
-        concat_axis=0,
-        tiled=True,
-    )
+    outer = lax.axis_size("tpa")
+    inner = lax.axis_size("tpb")
+    chunks = dec_part.reshape(outer, inner, tok_rows // tp_count, dec_part.shape[1])
+    me_inner = lax.axis_index("tpb")
+    kept = lax.dynamic_index_in_dim(chunks, me_inner, 1, keepdims=False)
+    given = lax.dynamic_index_in_dim(chunks, (me_inner + 1) % inner, 1, keepdims=False)
+    got = lax.ppermute(given, "tpb", [(i, (i + 1) % inner) for i in range(inner)])
+    pair = (kept.astype(jnp.float32) + got.astype(jnp.float32)).astype(jnp.bfloat16)
+    pieces = lax.all_to_all(pair, "tpa", split_axis=0, concat_axis=0, tiled=True)
     dec_out = jnp.sum(pieces.astype(jnp.float32), axis=0).astype(jnp.bfloat16)
     return (dec_out, pre_out)
 
 
 def solution(mesh):
+    n_tp = mesh.shape["tp"]
+    split = jax.sharding.Mesh(
+        mesh.devices.reshape(mesh.shape["req"], n_tp // 2, 2), ("req", "tpa", "tpb")
+    )
+    tp = ("tpa", "tpb")
     placed = (
-        P("req", "tp"),
-        P("req", "tp"),
+        P("req", tp),
+        P("req", tp),
         P("req"),
         P("req", None),
-        P("req", "tp"),
-        P("req", "tp"),
+        P("req", tp),
+        P("req", tp),
         P("req", None),
-        P("req", "tp"),
-        P("tp", None),
+        P("req", tp),
+        P(tp, None),
     )
     return jax.shard_map(
         per_device,
-        mesh=mesh,
+        mesh=split,
         in_specs=placed,
-        out_specs=(P(("req", "tp"), None), P(("req", "tp"), None)),
+        out_specs=(P(("req",) + tp, None), P(("req",) + tp, None)),
         check_vma=False,
     )

time: 99 us -> 105 us (1.061)
  blocking collectives: 48.4 us -> 19.4 us
  waiting for transfers between devices: 6.18 us -> 31.9 us
  starting transfers between devices: 14.1 us -> 24.1 us
    all_to_all x2 -> x1, blocking collectives: 48.4 us -> 19.4 us  [per_device(): lax.all_to_all(pair, 'tpa', split_axis=0, concat_axis=0, tiled=True)]
    ppermute x0 -> x1, waiting for transfers between devices: none -> 15.5 us  [per_device(): lax.ppermute(given, 'tpb', [(i, (i + 1) % inner) for i in range(inner)])]
    all_to_all x0 -> x1, waiting for transfers between devices: none -> 10.2 us  [per_device(): lax.all_to_all(slot_attn, 'req', split_axis=0, concat_axis=0, tiled=True)]
    all_to_all x0 -> x1, starting transfers between devices: none -> 6.53 us  [per_device(): lax.all_to_all(slot_attn, 'req', split_axis=0, concat_axis=0, tiled=True)]
    ppermute x0 -> x1, starting transfers between devices: none -> 3.47 us  [per_device(): lax.ppermute(given, 'tpb', [(i, (i + 1) % inner) for i in range(inner)])]
  transfers between devices with their start and end apart: 2 -> 4, of which waited for: 1 -> 3; matrix products, arithmetic and copies ran while one was open for 6% -> 5% of each run, Pallas kernels for 7% -> 7%
where the time goes in v15:
time: 105 us
  waiting for transfers between devices  31.9 us (30%)
  starting transfers between devices  24.1 us (23%)
  blocking collectives  19.4 us (18%)
  between operations  14.1 us (13%)
  Pallas kernels  9.09 us (9%)
  matrix products  3.79 us (4%)
  local copies, waits for them, and re-layouts  1.57 us (1%)
    all_to_all x1, blocking collectives, per_device(): lax.all_to_all(pair, 'tpa', split_axis=0, concat_axis=0, tiled=True)  19.4 us
    ppermute x1, waiting for transfers between devices, per_device(): lax.ppermute(given, 'tpb', [(i, (i + 1) % inner) for i in range(inner)])  15.5 us
    all_to_all x1, starting transfers between devices, per_device(): recv = lax.all_to_all(send, 'req', split_axis=0, concat_axis=0, tiled=True)  14 us
    all_to_all x1, waiting for transfers between devices, per_device(): lax.all_to_all(slot_attn, 'req', split_axis=0, concat_axis=0, tiled=True)  10.2 us
    pallas_call x2, Pallas kernels, vmem_call(): pl.pallas_call(kernel, out_shape=out_shape, in_specs=[pl.BlockSpec(memory...  6.97 us
    all_to_all x1, starting transfers between devices, per_device(): lax.all_to_all(slot_attn, 'req', split_axis=0, concat_axis=0, tiled=True)  6.53 us
    all_to_all x1, waiting for transfers between devices, per_device(): recv = lax.all_to_all(send, 'req', split_axis=0, concat_axis=0, tiled=True)  6.18 us
    dot_general x2, matrix products, term_maker(): return jnp.dot(rows_source, wo, preferred_element_type=jnp.float32)  3.79 us
  transfers between devices with their start and end apart: 4, of which 3 were waited for; matrix products, arithmetic and copies ran while one was open for 5% of the time, Pallas kernels for 7%

profile of v15, /device:TPU:6, one launch (start us, length us, event | category | flops | bytes accessed | tf_op | source)
XLA Modules:
  0.0 104.7 jit_solution(17140409308434858284)
XLA Ops:
  7.2 0.0 copy-start
  7.2 2.1 %shard_map.104 = (bf16[64,4,640]{2,1,0:T(4,128)(2,1)}, bf16[256,128]{1,0:T(8,128)(2,1)}) custom-call(s32[1,128]{1,0:T(1,128)} %bitcast.16, bf16[128,384]{1,0:T(8,128)(2,1)} %q_ref.2, bf16[128,256]{1,0:T(8,128)(2,1)} %kv_ref.2), custom_call_target="tpu_custom_call" | custom-call | flops 41943040 | bytes 491520 | tf_op jit(solution)/shard_map/pallas_call | solution.py:150
  9.3 14.0 %all-to-all-start = ((bf16[64,4,640]{2,1,0:T(4,128)(2,1)}), bf16[64,4,640]{2,1,0:T(4,128)(2,1)S(1)}, u32[]{:S(2)}, u32[]{:S(2)}) async-start(bf16[64,4,640]{2,1,0:T(4,128)(2,1)} %get-tuple-element.7), calls=%async_computation | async-start | bytes 655360 | tf_op jit(solution)/shard_map/all_to_all | solution.py:164
  23.3 0.0 reduce-scatter.2.cloned.1.call-start
  23.4 3.6 %shard_map.105 = bf16[256,384]{1,0:T(8,128)(2,1)} custom-call(bf16[256,384]{1,0:T(8,128)(2,1)} %q_ref.3, bf16[256,256]{1,0:T(8,128)(2,1)} %kv_ref.3, s32[1,3]{1,0:T(1,128)} %meta_ref.1, bf16[512,256]{1,0:T(8,128)(2,1)} %pool_ref.3), custom_call_target="tpu_custom_call" | custom-call | flops 301989888 | bytes 786444 | tf_op jit(solution)/shard_map/pallas_call | solution.py:117
  26.9 0.0 copy-done
  26.9 3.1 %convolution_convert_fusion = bf16[256,3072]{1,0:T(8,128)(2,1)} fusion(bf16[256,384]{1,0:T(8,128)(2,1)} %shard_map.105, bf16[384,3072]{1,0:T(8,128)(2,1)S(1)} %copy-done), kind=kOutput, calls=%fused_computation | convolution fusion | flops 604766208 | bytes 4128768 | tf_op jit(solution)/shard_map/dot_general | solution.py:129
  30.0 0.0 copy-start.2
  30.0 6.2 %all-to-all-done.recv_ref = bf16[64,4,640]{2,1,0:T(4,128)(2,1)S(1)} async-done(((bf16[64,4,640]{2,1,0:T(4,128)(2,1)}), bf16[64,4,640]{2,1,0:T(4,128)(2,1)S(1)}, u32[]{:S(2)}, u32[]{:S(2)}) %all-to-all-start) | async-done | bytes 327712 | tf_op jit(solution)/shard_map/all_to_all | solution.py:164
  36.2 0.0 copy-start.1
  36.2 0.0 reduce-scatter.2.cloned.1.call-update
  36.2 0.7 copy-done.1
  36.9 3.4 %shard_map.106 = bf16[64,4,384]{2,1,0:T(4,128)(2,1)} custom-call(bf16[64,4,640]{2,1,0:T(4,128)(2,1)} %copy-done.1, s32[2,256]{1,0:T(2,128)} %bitcast.15, bf16[512,256]{1,0:T(8,128)(2,1)} %pool_ref.3), custom_call_target="tpu_custom_call" | custom-call | flops 201326592 | bytes 788480 | tf_op jit(solution)/shard_map/pallas_call | solution.py:117
  40.3 6.5 %all-to-all-start.1 = ((bf16[64,4,384]{2,1,0:T(4,128)(2,1)}), bf16[64,4,384]{2,1,0:T(4,128)(2,1)S(1)}, u32[]{:S(2)}, u32[]{:S(2)}) async-start(bf16[64,4,384]{2,1,0:T(4,128)(2,1)} %shard_map.106), calls=%async_computation.1 | async-start | bytes 393216 | tf_op jit(solution)/shard_map/all_to_all | solution.py:174
  46.9 10.2 %all-to-all-done.1 = bf16[64,4,384]{2,1,0:T(4,128)(2,1)S(1)} async-done(((bf16[64,4,384]{2,1,0:T(4,128)(2,1)}), bf16[64,4,384]{2,1,0:T(4,128)(2,1)S(1)}, u32[]{:S(2)}, u32[]{:S(2)}) %all-to-all-start.1) | async-done | bytes 196640 | tf_op jit(solution)/shard_map/all_to_all | solution.py:174
  57.1 0.1 reshape.16
  57.1 0.0 copy-done.2
  57.1 0.7 convolution_convert_fusion.1
  57.9 0.8 dynamic-slice_bitcast_fusion
  58.7 3.5 %collective-permute-start = (bf16[4,16,3072]{2,1,0:T(8,128)(2,1)}, bf16[4,16,3072]{2,1,0:T(8,128)(2,1)S(1)}, u32[]{:S(2)}, u32[]{:S(2)}) collective-permute-start(bf16[4,16,3072]{2,1,0:T(8,128)(2,1)} %dynamic-slice_bitcast_fusion), channel_id=1, source_target_pairs={{0,1},{1,0},{2,3},{3,2},{4,5},{5,4},{6,7},{7,6},{8,9},{9,8},{10,11... | collective-permute-start | bytes 1179656 | tf_op jit(solution)/shard_map/ppermute | solution.py:189
  62.1 15.5 %collective-permute-done = bf16[4,16,3072]{2,1,0:T(8,128)(2,1)S(1)} collective-permute-done((bf16[4,16,3072]{2,1,0:T(8,128)(2,1)}, bf16[4,16,3072]{2,1,0:T(8,128)(2,1)S(1)}, u32[]{:S(2)}, u32[]{:S(2)}) %collective-permute-start) | collective-permute-done | bytes 393248 | tf_op jit(solution)/shard_map/ppermute | solution.py:189
  77.6 0.1 fusion
  77.7 19.4 %all_to_all.15 = bf16[4,16,3072]{2,1,0:T(8,128)(2,1)S(1)} all-to-all(bf16[4,16,3072]{2,1,0:T(8,128)(2,1)S(1)} %fusion), channel_id=1, replica_groups=mesh['req'=64,'tpa'=4,'tpb'=2] {'tpa'}, dimensions={0} | all-to-all | bytes 786432 | tf_op jit(solution)/shard_map/all_to_all | solution.py:191
  97.1 0.7 reduce_sum.12
  (1 shorter events, 0.0 us)
Async XLA Ops:
  7.2 19.8 %copy-start = (bf16[384,3072]{1,0:T(8,128)(2,1)S(1)}, bf16[384,3072]{1,0:T(8,128)(2,1)}, u32[]{:S(2)}) copy-start(bf16[384,3072]{1,0:T(8,128)(2,1)} %param.17) | copy-start | bytes 7077892
  9.3 26.9 %all-to-all-start = ((bf16[64,4,640]{2,1,0:T(4,128)(2,1)}), bf16[64,4,640]{2,1,0:T(4,128)(2,1)S(1)}, u32[]{:S(2)}, u32[]{:S(2)}) async-start(bf16[64,4,640]{2,1,0:T(4,128)(2,1)} %get-tuple-element.7), calls=%async_computation | async-start | bytes 655360 | tf_op jit(solution)/shard_map/all_to_all | solution.py:164
  23.3 74.5 %reduce-scatter.2.cloned.1.call-start = ((), (), s32[]{:S(2)}) async-start(), calls=%async_computation.4 | async-start | bytes 1769472 | tf_op jit(solution)/shard_map/reduce_scatter | solution.py:166
  30.0 27.1 %copy-start.2 = (bf16[256,128]{1,0:T(8,128)(2,1)S(1)}, bf16[256,128]{1,0:T(8,128)(2,1)}, u32[]{:S(2)}) copy-start(bf16[256,128]{1,0:T(8,128)(2,1)} %get-tuple-element.6) | copy-start | bytes 196612
  36.2 0.7 copy-start.1
  40.3 16.7 %all-to-all-start.1 = ((bf16[64,4,384]{2,1,0:T(4,128)(2,1)}), bf16[64,4,384]{2,1,0:T(4,128)(2,1)S(1)}, u32[]{:S(2)}, u32[]{:S(2)}) async-start(bf16[64,4,384]{2,1,0:T(4,128)(2,1)} %shard_map.106), calls=%async_computation.1 | async-start | bytes 393216 | tf_op jit(solution)/shard_map/all_to_all | solution.py:174
  58.7 19.0 %collective-permute-start = (bf16[4,16,3072]{2,1,0:T(8,128)(2,1)}, bf16[4,16,3072]{2,1,0:T(8,128)(2,1)S(1)}, u32[]{:S(2)}, u32[]{:S(2)}) collective-permute-start(bf16[4,16,3072]{2,1,0:T(8,128)(2,1)} %dynamic-slice_bitcast_fusion), channel_id=1, source_target_pairs={{0,1},{1,0},{2,3},{3,2},{4,5},{5,4},{6,7},{7,6},{8,9},{9,8},{10,11... | collective-permute-start | bytes 1179656 | tf_op jit(solution)/shard_map/ppermute | solution.py:189
Sparse Core Ops, SparseCore 0:
  36.3 42.0 reduce-scatter.1

commit v16 on v14

--- a/solution.py
+++ b/solution.py
@@ -167,7 +167,7 @@
     slot_attn = vmem_call(
         decode_kernel,
         jax.ShapeDtypeStruct((groups, capacity, q_width), jnp.bfloat16),
-        (recv, jnp.transpose(dec_table), pool),
+        (pltpu.with_memory_space_constraint(recv, pltpu.VMEM), jnp.transpose(dec_table), pool),
         4 * slot_count * pool.shape[0] * q_width,
         slot_count * pool.shape[0] * q_width // HD,
     )

time: 99 us -> 99.4 us (level)
  no operation moved by 1% of the time
where the time goes in v16:
time: 99.4 us; the launch traced here: 98.1 us
  blocking collectives  32.5 us (33%)
  starting transfers between devices  20.6 us (21%)
  waiting for transfers between devices  16.2 us (16%)
  between operations  14.1 us (14%)
  Pallas kernels  8.98 us (9%)
  matrix products  4.71 us (5%)
    all_to_all x1, blocking collectives, per_device(): lax.all_to_all(dec_part.reshape(tp_count, tok_rows // tp_count, dec_part....  32.5 us
    all_to_all x1, starting transfers between devices, per_device(): recv = lax.all_to_all(send, 'req', split_axis=0, concat_axis=0, tiled=True)  14 us
    all_to_all x1, waiting for transfers between devices, per_device(): lax.all_to_all(slot_attn, 'req', split_axis=0, concat_axis=0, tiled=True)  10 us
    pallas_call x2, Pallas kernels, vmem_call(): pl.pallas_call(kernel, out_shape=out_shape, in_specs=[pl.BlockSpec(memory...  6.88 us
    all_to_all x1, starting transfers between devices, per_device(): lax.all_to_all(slot_attn, 'req', split_axis=0, concat_axis=0, tiled=True)  6.53 us
    all_to_all x1, waiting for transfers between devices, per_device(): recv = lax.all_to_all(send, 'req', split_axis=0, concat_axis=0, tiled=True)  6.18 us
    dot_general x2, matrix products, term_maker(): return jnp.dot(rows_source, wo, preferred_element_type=jnp.float32)  4.71 us
    pallas_call x1, Pallas kernels, per_device(): pl.pallas_call(route_kernel, out_shape=jax.ShapeDtypeStruct((groups, capa...  2.11 us
  transfers between devices with their start and end apart: 3, of which 2 were waited for; matrix products, arithmetic and copies ran while one was open for 6% of the time, Pallas kernels for 7%

profile of v16, /device:TPU:6, one launch (start us, length us, event | category | flops | bytes accessed | tf_op | source)
XLA Modules:
  0.0 98.1 jit_solution(17998230889935679268)
XLA Ops:
  7.2 0.0 copy-start
  7.2 2.1 %shard_map.105 = bf16[64,4,640]{2,1,0:T(4,128)(2,1)} custom-call(s32[1,128]{1,0:T(1,128)} %bitcast.9, bf16[128,384]{1,0:T(8,128)(2,1)} %q_ref.3, bf16[128,256]{1,0:T(8,128)(2,1)} %kv_ref.3), custom_call_target="tpu_custom_call" | custom-call | flops 41943040 | bytes 491520 | tf_op jit(solution)/shard_map/pallas_call | solution.py:149
  9.3 14.0 %all-to-all-start = ((bf16[64,4,640]{2,1,0:T(4,128)(2,1)}), bf16[64,4,640]{2,1,0:T(4,128)(2,1)S(1)}, u32[]{:S(2)}, u32[]{:S(2)}) async-start(bf16[64,4,640]{2,1,0:T(4,128)(2,1)} %shard_map.105), calls=%async_computation | async-start | bytes 655360 | tf_op jit(solution)/shard_map/all_to_all | solution.py:164
  23.3 0.0 reduce-scatter.2.cloned.1.call-start
  23.4 3.6 %shard_map.104 = bf16[256,384]{1,0:T(8,128)(2,1)} custom-call(bf16[256,384]{1,0:T(8,128)(2,1)} %q_ref.2, bf16[256,256]{1,0:T(8,128)(2,1)} %kv_ref.2, s32[1,3]{1,0:T(1,128)} %meta_ref.1, bf16[512,256]{1,0:T(8,128)(2,1)} %pool_ref.3), custom_call_target="tpu_custom_call" | custom-call | flops 301989888 | bytes 786444 | tf_op jit(solution)/shard_map/pallas_call | solution.py:116
  26.9 0.0 copy-done
  26.9 3.1 %convolution_convert_fusion = bf16[256,3072]{1,0:T(8,128)(2,1)} fusion(bf16[256,384]{1,0:T(8,128)(2,1)} %shard_map.104, bf16[384,3072]{1,0:T(8,128)(2,1)S(1)} %copy-done), kind=kOutput, calls=%fused_computation | convolution fusion | flops 604766208 | bytes 4128768 | tf_op jit(solution)/shard_map/dot_general | solution.py:128
  30.0 0.0 copy-start.1
  30.0 6.2 %all-to-all-done.recv_ref = bf16[64,4,640]{2,1,0:T(4,128)(2,1)S(1)} async-done(((bf16[64,4,640]{2,1,0:T(4,128)(2,1)}), bf16[64,4,640]{2,1,0:T(4,128)(2,1)S(1)}, u32[]{:S(2)}, u32[]{:S(2)}) %all-to-all-start) | async-done | bytes 327712 | tf_op jit(solution)/shard_map/all_to_all | solution.py:164
  36.2 0.0 reduce-scatter.2.cloned.1.call-update
  36.2 3.3 %shard_map.106 = bf16[64,4,384]{2,1,0:T(4,128)(2,1)} custom-call(bf16[64,4,640]{2,1,0:T(4,128)(2,1)S(1)} %all-to-all-done.recv_ref, s32[2,256]{1,0:T(2,128)} %bitcast.8, bf16[512,256]{1,0:T(8,128)(2,1)} %pool_ref.3), custom_call_target="tpu_custom_call" | custom-call | flops 201326592 | bytes 788480 | tf_op jit(solution)/shard_map/pallas_call | solution.py:116
  39.5 6.5 %all-to-all-start.1 = ((bf16[64,4,384]{2,1,0:T(4,128)(2,1)}), bf16[64,4,384]{2,1,0:T(4,128)(2,1)S(1)}, u32[]{:S(2)}, u32[]{:S(2)}) async-start(bf16[64,4,384]{2,1,0:T(4,128)(2,1)} %shard_map.106), calls=%async_computation.1 | async-start | bytes 393216 | tf_op jit(solution)/shard_map/all_to_all | solution.py:174
  46.1 0.0 copy-done.1
  46.1 0.2 convert_reduce_fusion
  46.2 10.0 %all-to-all-done.1 = bf16[64,4,384]{2,1,0:T(4,128)(2,1)S(1)} async-done(((bf16[64,4,384]{2,1,0:T(4,128)(2,1)}), bf16[64,4,384]{2,1,0:T(4,128)(2,1)S(1)}, u32[]{:S(2)}, u32[]{:S(2)}) %all-to-all-start.1) | async-done | bytes 196640 | tf_op jit(solution)/shard_map/all_to_all | solution.py:174
  56.3 0.1 reshape.14
  56.3 1.6 %convolution_convert_fusion.1 = bf16[128,3072]{1,0:T(8,128)(2,1)} fusion(bf16[384,3072]{1,0:T(8,128)(2,1)S(1)} %copy-done, bf16[256,384]{1,0:T(8,128)(2,1)S(1)} %reshape.14, s32[128]{0:T(128)S(1)} %multiply_add_fusion), kind=kOutput, calls=%fused_computation.1 | convolution fusion | flops 327630848 | bytes 3342848 | tf_op jit(solution)/shard_map/dot_general | solution.py:128
  58.0 32.5 %all_to_all.15 = bf16[8,16,3072]{2,1,0:T(8,128)(2,1)S(1)} all-to-all(bf16[8,16,3072]{2,1,0:T(8,128)(2,1)} %bitcast.7), channel_id=1, replica_groups=mesh['req'=64,'tp'=8] {'tp'}, dimensions={0} | all-to-all | bytes 1572864 | tf_op jit(solution)/shard_map/all_to_all | solution.py:183
  90.5 0.8 reduce_sum.22
  91.2 0.0 reduce-scatter.2.cloned.1.call-done
  (1 shorter events, 0.0 us)
Async XLA Ops:
  7.2 19.8 %copy-start = (bf16[384,3072]{1,0:T(8,128)(2,1)S(1)}, bf16[384,3072]{1,0:T(8,128)(2,1)}, u32[]{:S(2)}) copy-start(bf16[384,3072]{1,0:T(8,128)(2,1)} %param.17) | copy-start | bytes 7077892
  9.3 26.9 %all-to-all-start = ((bf16[64,4,640]{2,1,0:T(4,128)(2,1)}), bf16[64,4,640]{2,1,0:T(4,128)(2,1)S(1)}, u32[]{:S(2)}, u32[]{:S(2)}) async-start(bf16[64,4,640]{2,1,0:T(4,128)(2,1)} %shard_map.105), calls=%async_computation | async-start | bytes 655360 | tf_op jit(solution)/shard_map/all_to_all | solution.py:164
  23.3 67.9 %reduce-scatter.2.cloned.1.call-start = ((), (), s32[]{:S(2)}) async-start(), calls=%async_computation.4 | async-start | bytes 1769472 | tf_op jit(solution)/shard_map/reduce_scatter | solution.py:166
  30.0 16.1 %copy-start.1 = (s32[128]{0:T(128)S(1)}, s32[128]{0:T(128)}, u32[]{:S(2)}) copy-start(s32[128]{0:T(128)} %param.11) | copy-start | bytes 1540
  39.5 16.7 %all-to-all-start.1 = ((bf16[64,4,384]{2,1,0:T(4,128)(2,1)}), bf16[64,4,384]{2,1,0:T(4,128)(2,1)S(1)}, u32[]{:S(2)}, u32[]{:S(2)}) async-start(bf16[64,4,384]{2,1,0:T(4,128)(2,1)} %shard_map.106), calls=%async_computation.1 | async-start | bytes 393216 | tf_op jit(solution)/shard_map/all_to_all | solution.py:174
Sparse Core Ops, SparseCore 0:
  36.3 47.4 reduce-scatter.1
